TPU v7x, 512 devices: a whole 4x4x16 slice. The times are simulated.
512 devices in a mesh: expert: 32 (over y, z_hi, x), dp: 16 (over z_lo, core).
Axes of the slice: x: 4, y: 4, z: 16 (z_hi: 2, z_lo: 8; z = z_hi * 8 + z_lo), core: 2. Of those that a mesh axis runs over, the one named last changes fastest.
Arguments:
- tokens: bfloat16 [4096, 3584], P('expert'), may hold values from -6 to 6
- expert_ids: int32 [4096, 8], P('expert'), may hold values from 0 to 31, all different within a row; in each aligned block of 128 rows (0 to 127, 128 to 255, ...) at most 48 rows name the same one
- route_weights: float32 [4096, 8], P('expert'), may hold values from 0.05 to 0.45
- gate_up_panels: bfloat16 [32, 16, 1792, 256], P('expert', 'dp'), may hold values from -0.09375 to 0.09375
- down_panels: bfloat16 [32, 1024, 3584], P('expert', None, 'dp'), may hold values from -0.1875 to 0.1875
- partner: int32 [32], replicated, may hold values from 0 to 31, as said below
Outputs:
- moe_out: bfloat16 [4096, 3584], P('expert', 'dp')
- new_gate_up: bfloat16 [32, 16, 1792, 256], P('expert', 'dp')
- new_down: bfloat16 [32, 1024, 3584], P('expert', None, 'dp')
Inputs may be any that keep to these rules, and one draw needn't show every extreme that they name: `expert_ids`: in the 128 rows of one index of the expert axis, each row names 8 different experts and no expert is named by more than 48 rows. partner[i] is i, i XOR 1 or i XOR 2, the same of these for the four indices of each aligned group of four; partner[partner[i]] = i; some group takes XOR 1 and some group XOR 2.
All inputs are finite; a program needn't handle non-finite values.
Results may differ from a plain program's by a relative error of at most 0.0057.
Values may be sent and summed in bfloat16 or wider, within the bound.
No kernel may reach another device: no remote copies, remote signals or barrier semaphores. Data moves between devices by JAX's collectives and lax.ppermute only.
A program may use at most 64 MiB of HBM per device.

v0:
```python
import jax
import jax.numpy as jnp
from jax import lax
from jax.sharding import PartitionSpec as P


def from_partner(block, axis, bit):
    count = lax.axis_size(axis)
    route = []
    for low in range(count):
        high = low | 1 << bit
        if high != low and high < count:
            route += [(low, high), (high, low)]
    return lax.ppermute(block, axis, route)


def swap_panels(gate_up, down, partner):
    here = lax.axis_index("expert")
    partner_id = partner[here]
    result_gate_up, result_down = (gate_up, down)
    for bit_number in range(2):
        moved_gate_up, moved_down = from_partner((gate_up, down), "expert", bit_number)
        taken = partner_id == jnp.bitwise_xor(here, 1 << bit_number)
        result_gate_up = jnp.where(taken, moved_gate_up, result_gate_up)
        result_down = jnp.where(taken, moved_down, result_down)
    return (result_gate_up, result_down)


def run_layer(tokens, expert_ids, route_weights, gate_up, down, owner_table):
    devices = lax.axis_size("expert")
    token_rows, model_width = tokens.shape
    top_count = expert_ids.shape[1]
    expert_count = owner_table.shape[0]
    capacity = min(token_rows, 3 * token_rows * top_count // (2 * expert_count))
    half_width = model_width // 2
    side = lax.rem(lax.axis_index("dp"), 2)
    own_half = lax.dynamic_slice_in_dim(tokens, side * half_width, half_width, 1)
    labels = jnp.arange(expert_count, dtype=jnp.int32)
    onehot = (expert_ids[:, :, None] == labels[None, None, :]).astype(jnp.int32)
    picked = jnp.sum(onehot, axis=1)
    slot_rank = jnp.cumsum(picked, axis=0) - picked
    slots = jnp.sum(onehot * slot_rank[:, None, :], axis=2)
    target = jnp.sum(onehot * owner_table[None, None, :], axis=2)
    place = (target * capacity + slots).reshape(-1)
    row_ids = jnp.repeat(jnp.arange(token_rows, dtype=jnp.int32), top_count)
    source = jnp.full((devices * capacity,), token_rows, jnp.int32).at[place].set(row_ids)
    padded = jnp.concatenate([own_half, jnp.zeros((1, half_width), own_half.dtype)], axis=0)
    outgoing = padded[source].reshape(devices, capacity, half_width)
    arrived = lax.all_to_all(outgoing, "expert", split_axis=0, concat_axis=0, tiled=True)
    flat = arrived.reshape(devices * capacity, half_width)
    partial_value = jnp.dot(flat, gate_up, preferred_element_type=jnp.float32)
    half_rows = flat.shape[0] // 2
    mine = lax.dynamic_slice_in_dim(partial_value, side * half_rows, half_rows, 0)
    other = lax.dynamic_slice_in_dim(partial_value, (1 - side) * half_rows, half_rows, 0)
    summed = mine + from_partner(other, "dp", 0)
    block_units = gate_up.shape[1] // 2
    hidden = (jax.nn.silu(summed[:, :block_units]) * summed[:, block_units:]).astype(jnp.bfloat16)
    gathered = lax.all_gather(hidden, "dp", axis=1, tiled=True)
    pair_count = lax.axis_size("dp") // 2
    out_columns = down.shape[1]
    outputs = jnp.einsum(
        "rqhk,qkc->hrc",
        gathered.reshape(half_rows, pair_count, 2, block_units),
        down.reshape(pair_count, block_units, out_columns),
        preferred_element_type=jnp.float32,
    )
    expert_out = outputs.reshape(devices, capacity, out_columns).astype(jnp.bfloat16)
    returned = lax.all_to_all(expert_out, "expert", split_axis=0, concat_axis=0, tiled=True)
    chosen = returned.reshape(devices * capacity, out_columns)[place].reshape(
        token_rows, top_count, out_columns
    )
    mixed = jnp.sum(chosen.astype(jnp.float32) * route_weights[:, :, None], axis=1)
    return mixed.astype(jnp.bfloat16)


def per_device(tokens, expert_ids, route_weights, gate_up_panels, down_panels, partner):
    new_gate_up, new_down = swap_panels(gate_up_panels, down_panels, partner)
    moe_out = run_layer(tokens, expert_ids, route_weights, new_gate_up[0, 0], new_down[0], partner)
    return (moe_out, new_gate_up, new_down)


def solution(mesh):
    return jax.shard_map(
        per_device,
        mesh=mesh,
        in_specs=(
            P("expert", None),
            P("expert", None),
            P("expert", None),
            P("expert", "dp", None, None),
            P("expert", None, "dp"),
            P(),
        ),
        out_specs=(P("expert", "dp"), P("expert", "dp", None, None), P("expert", None, "dp")),
        check_vma=False,
    )
```

profile of v0, /device:TPU:1, one launch (start us, length us, event | category | flops | bytes accessed | tf_op | source)
XLA Modules:
  0.0 459.6 jit_solution(5787766010149977916)
XLA Ops:
  9.5 4.3 scatter_custom_fusion
  13.9 6.7 %gather_fusion = bf16[1536,1792]{1,0:T(8,128)(2,1)} fusion(bf16[129,1792]{1,0:T(8,128)(2,1)S(1)} %concatenate.3, s32[2048]{0:T(1024)S(1)} %pad_clamp_fusion), kind=kCustom, calls=%fused_computation | custom fusion | bytes 11016192 | tf_op jit(solution)/shard_map/gather | solution.py:48
  20.7 21.4 %all-to-all-start = ((bf16[32,48,1792]{2,1,0:T(8,128)(2,1)}), bf16[32,48,1792]{2,1,0:T(8,128)(2,1)}, u32[]{:S(2)}, u32[]{:S(2)}) async-start(bf16[32,48,1792]{2,1,0:T(8,128)(2,1)} %bitcast.31), calls=%async_computation | async-start | bytes 11010048 | tf_op jit(solution)/shard_map/all_to_all | solution.py:49
  42.1 4.6 collective-permute-start.2
  46.7 2.2 collective-permute-start.3
  50.8 80.2 %collective-permute-done.2 = bf16[1,1,1792,256]{3,2,1,0:T(8,128)(2,1)S(1)} collective-permute-done((bf16[1,1,1792,256]{3,2,1,0:T(8,128)(2,1)S(1)}, bf16[1,1,1792,256]{3,2,1,0:T(8,128)(2,1)S(1)}, u32[]{:S(2)}, u32[]{:S(2)}) %collective-permute-start.2) | collective-permute-done | bytes 917536 | tf_op jit(solution)/shard_map/ppermute | solution.py:14
  131.9 24.1 %collective-permute-done.3 = bf16[1,1,1792,256]{3,2,1,0:T(8,128)(2,1)} collective-permute-done((bf16[1,1,1792,256]{3,2,1,0:T(8,128)(2,1)S(1)}, bf16[1,1,1792,256]{3,2,1,0:T(8,128)(2,1)}, u32[]{:S(2)}, u32[]{:S(2)}) %collective-permute-start.3) | collective-permute-done | bytes 917536 | tf_op jit(solution)/shard_map/ppermute | solution.py:14
  156.0 1.3 select_select_fusion
  157.3 4.5 fusion.12
  161.8 0.9 constant_dynamic-slice_fusion
  162.8 4.1 collective-permute-start.4
  166.9 2.1 collective-permute-done.4
  169.9 40.5 %collective-permute-start = (bf16[1,1024,224]{1,2,0:T(8,128)(2,1)}, bf16[1,1024,224]{1,2,0:T(8,128)(2,1)S(1)}, u32[]{:S(2)}, u32[]{:S(2)}) collective-permute-start(bf16[1,1024,224]{1,2,0:T(8,128)(2,1)} %param.10), channel_id=1, source_target_pairs={{0,32},{32,0},{16,48},{48,16},{64,96},{96,64},{80,112},{112,80},{1... | collective-permute-start | bytes 1376264 | tf_op jit(solution)/shard_map/ppermute | solution.py:14
  210.4 1.9 collective-permute-start.1
  212.3 8.8 %collective-permute-done = bf16[1,1024,224]{1,2,0:T(8,128)(2,1)S(1)} collective-permute-done((bf16[1,1024,224]{1,2,0:T(8,128)(2,1)}, bf16[1,1024,224]{1,2,0:T(8,128)(2,1)S(1)}, u32[]{:S(2)}, u32[]{:S(2)}) %collective-permute-start) | collective-permute-done | bytes 458784 | tf_op jit(solution)/shard_map/ppermute | solution.py:14
  221.1 8.9 %collective-permute-done.1 = bf16[1,1024,224]{1,2,0:T(8,128)(2,1)S(1)} collective-permute-done((bf16[1,1024,224]{1,2,0:T(8,128)(2,1)}, bf16[1,1024,224]{1,2,0:T(8,128)(2,1)S(1)}, u32[]{:S(2)}, u32[]{:S(2)}) %collective-permute-start.1) | collective-permute-done | bytes 458784 | tf_op jit(solution)/shard_map/ppermute | solution.py:14
  230.0 1.1 select_select_fusion.1
  231.2 157.7 %all-gather.2.cloned.1.call-done = bf16[768,2048]{1,0:T(8,128)(2,1)} async-done(((bf16[768,128]{1,0:T(8,128)(2,1)}), bf16[768,2048]{1,0:T(8,128)(2,1)}) %all-gather.2.cloned.1.call-update) | async-done | bytes 3145744 | tf_op jit(solution)/shard_map/all_gather | solution.py:58
  388.9 6.0 %reshape.76 = bf16[768,8,2,128]{3,2,1,0:T(2,128)(2,1)} reshape(bf16[768,2048]{1,0:T(8,128)(2,1)} %all-gather.2.cloned.1.call-done) | data formatting | bytes 6291456 | tf_op jit(solution)/shard_map/reshape | solution.py:63
  395.0 3.1 fusion.8
  398.1 1.2 copy.30
  399.3 10.9 %all-to-all-start.1 = ((bf16[32,48,224]{2,1,0:T(8,128)(2,1)}), bf16[32,48,224]{2,1,0:T(8,128)(2,1)S(1)}, u32[]{:S(2)}, u32[]{:S(2)}) async-start(bf16[32,48,224]{2,1,0:T(8,128)(2,1)} %bitcast.9), calls=%async_computation.1 | async-start | bytes 1572864 | tf_op jit(solution)/shard_map/all_to_all | solution.py:68
  410.3 37.3 %all-to-all-done.1 = bf16[32,48,224]{2,1,0:T(8,128)(2,1)S(1)} async-done(((bf16[32,48,224]{2,1,0:T(8,128)(2,1)}), bf16[32,48,224]{2,1,0:T(8,128)(2,1)S(1)}, u32[]{:S(2)}, u32[]{:S(2)}) %all-to-all-start.1) | async-done | bytes 688160 | tf_op jit(solution)/shard_map/all_to_all | solution.py:68
  447.6 3.9 gather_fusion.1
  (41 shorter events, 6.2 us)
Async XLA Ops:
  7.2 6.7 %copy-start = (bf16[128,3584]{1,0:T(8,128)(2,1)S(1)}, bf16[128,3584]{1,0:T(8,128)(2,1)}, u32[]{:S(2)}) copy-start(bf16[128,3584]{1,0:T(8,128)(2,1)} %param.6) | copy-start | bytes 2752516
  20.7 21.4 %copy-start.2 = (bf16[1,1,1792,256]{3,2,1,0:T(8,128)(2,1)S(1)}, bf16[1,1,1792,256]{3,2,1,0:T(8,128)(2,1)}, u32[]{:S(2)}) copy-start(bf16[1,1,1792,256]{3,2,1,0:T(8,128)(2,1)} %param.9) | copy-start | bytes 2752516
  20.7 28.2 %copy-start.6 = (s32[32]{0:T(128)S(1)}, s32[32]{0:T(128)}, u32[]{:S(2)}) copy-start(s32[32]{0:T(128)} %param.11) | copy-start | bytes 388
  20.7 136.7 %all-to-all-start = ((bf16[32,48,1792]{2,1,0:T(8,128)(2,1)}), bf16[32,48,1792]{2,1,0:T(8,128)(2,1)}, u32[]{:S(2)}, u32[]{:S(2)}) async-start(bf16[32,48,1792]{2,1,0:T(8,128)(2,1)} %bitcast.31), calls=%async_computation | async-start | bytes 11010048 | tf_op jit(solution)/shard_map/all_to_all | solution.py:49
  42.0 346.9 %all-gather.2.cloned.1.call-start = ((), (), s32[]{:S(2)}) async-start(), calls=%async_computation.2 | async-start | bytes 3342336 | tf_op jit(solution)/shard_map/all_gather | solution.py:58
  42.1 88.9 %collective-permute-start.2 = (bf16[1,1,1792,256]{3,2,1,0:T(8,128)(2,1)S(1)}, bf16[1,1,1792,256]{3,2,1,0:T(8,128)(2,1)S(1)}, u32[]{:S(2)}, u32[]{:S(2)}) collective-permute-start(bf16[1,1,1792,256]{3,2,1,0:T(8,128)(2,1)S(1)} %copy-done.2), channel_id=1, source_target_pairs={{0,32},{32,0},{16,48},{48,16},{64,96},{96,64},{80,112},{112,80},{1... | collective-permute-start | bytes 2752520 | tf_op jit(solution)/shard_map/ppermute | solution.py:14
  46.7 109.3 %collective-permute-start.3 = (bf16[1,1,1792,256]{3,2,1,0:T(8,128)(2,1)S(1)}, bf16[1,1,1792,256]{3,2,1,0:T(8,128)(2,1)}, u32[]{:S(2)}, u32[]{:S(2)}) collective-permute-start(bf16[1,1,1792,256]{3,2,1,0:T(8,128)(2,1)S(1)} %copy-done.2), channel_id=1, source_target_pairs={{0,16},{16,0},{32,48},{48,32},{64,80},{80,64},{96,112},{112,96},{1... | collective-permute-start | bytes 2752520 | tf_op jit(solution)/shard_map/ppermute | solution.py:14
  131.0 0.9 copy-start.4
  157.3 4.5 copy-start.3
  162.8 6.2 %collective-permute-start.4 = (f32[768,256]{1,0:T(8,128)}, f32[768,256]{1,0:T(8,128)S(1)}, u32[]{:S(2)}, u32[]{:S(2)}) collective-permute-start(f32[768,256]{1,0:T(8,128)} %constant_dynamic-slice_fusion), channel_id=1, source_target_pairs={{0,1},{1,0},{2,3},{3,2},{4,5},{5,4},{6,7},{7,6},{8,9},{9,8},{10,11... | collective-permute-start | bytes 2359304 | tf_op jit(solution)/shard_map/ppermute | solution.py:14
  169.9 51.2 %collective-permute-start = (bf16[1,1024,224]{1,2,0:T(8,128)(2,1)}, bf16[1,1024,224]{1,2,0:T(8,128)(2,1)S(1)}, u32[]{:S(2)}, u32[]{:S(2)}) collective-permute-start(bf16[1,1024,224]{1,2,0:T(8,128)(2,1)} %param.10), channel_id=1, source_target_pairs={{0,32},{32,0},{16,48},{48,16},{64,96},{96,64},{80,112},{112,80},{1... | collective-permute-start | bytes 1376264 | tf_op jit(solution)/shard_map/ppermute | solution.py:14
  210.4 19.6 %collective-permute-start.1 = (bf16[1,1024,224]{1,2,0:T(8,128)(2,1)}, bf16[1,1024,224]{1,2,0:T(8,128)(2,1)S(1)}, u32[]{:S(2)}, u32[]{:S(2)}) collective-permute-start(bf16[1,1024,224]{1,2,0:T(8,128)(2,1)} %param.10), channel_id=1, source_target_pairs={{0,16},{16,0},{32,48},{48,32},{64,80},{80,64},{96,112},{112,96},{1... | collective-permute-start | bytes 1376264 | tf_op jit(solution)/shard_map/ppermute | solution.py:14
  231.1 163.8 %copy-start.1 = (bf16[1,1024,224]{1,2,0:T(8,128)(2,1)}, bf16[1,1024,224]{1,2,0:T(8,128)(2,1)S(1)}, u32[]{:S(2)}) copy-start(bf16[1,1024,224]{1,2,0:T(8,128)(2,1)S(1)} %select_select_fusion.1) | copy-start | bytes 1376260
  395.0 15.2 %copy-start.5 = (f32[128,8]{0,1:T(8,128)S(1)}, f32[128,8]{0,1:T(8,128)}, u32[]{:S(2)}) copy-start(f32[128,8]{0,1:T(8,128)} %param.8) | copy-start | bytes 12292
  399.3 48.3 %all-to-all-start.1 = ((bf16[32,48,224]{2,1,0:T(8,128)(2,1)}), bf16[32,48,224]{2,1,0:T(8,128)(2,1)S(1)}, u32[]{:S(2)}, u32[]{:S(2)}) async-start(bf16[32,48,224]{2,1,0:T(8,128)(2,1)} %bitcast.9), calls=%async_computation.1 | async-start | bytes 1572864 | tf_op jit(solution)/shard_map/all_to_all | solution.py:68
Sparse Core Ops, SparseCore 0:
  170.0 218.8 all-gather.1
where the time goes:
time: 460 us
  waiting for transfers between devices  319 us (69%)
  starting transfers between devices  85.6 us (19%)
  local copies, waits for them, and re-layouts  26.1 us (6%)
  between operations  15.6 us (3%)
  matrix products  7.63 us (2%)
  other arithmetic  5.51 us (1%)
    all_gather x1, waiting for transfers between devices, run_layer(): gathered = lax.all_gather(hidden, 'dp', axis=1, tiled=True)  158 us
    ppermute x5, waiting for transfers between devices, from_partner(): return lax.ppermute(block, axis, route)  124 us
    ppermute x5, starting transfers between devices, from_partner(): return lax.ppermute(block, axis, route)  53.3 us
    all_to_all x1, waiting for transfers between devices, run_layer(): lax.all_to_all(expert_out, 'expert', split_axis=0, concat_axis=0, tiled=T...  37.3 us
    all_to_all x1, starting transfers between devices, run_layer(): lax.all_to_all(outgoing, 'expert', split_axis=0, concat_axis=0, tiled=True)  21.4 us
    all_to_all x1, starting transfers between devices, run_layer(): lax.all_to_all(expert_out, 'expert', split_axis=0, concat_axis=0, tiled=T...  10.9 us
  transfers between devices with their start and end apart: 8, of which 7 were waited for; matrix products, arithmetic and copies ran while one was open for 1% of the time, Pallas kernels for 0%

commit v1 on v0

v1 whole, which is shorter than its diff:
```python
import jax
import jax.numpy as jnp
from jax import lax
from jax.sharding import PartitionSpec as P


def shift_route(axis, step):
    count = lax.axis_size(axis)
    return [(low, (low & ~3) | ((low + step) & 3)) for low in range(count)]


def swap_panels(gate_up, down, partner):
    here = lax.axis_index("expert")
    kind = jnp.bitwise_xor(partner[here], here)
    even = (here & 1) == 0
    gate_rows = gate_up.shape[2] // 2
    down_rows = down.shape[1] // 2
    first = (gate_up[:, :, :gate_rows], down[:, :down_rows])
    second = (gate_up[:, :, gate_rows:], down[:, down_rows:])
    ahead, behind = shift_route("expert", 1), shift_route("expert", 3)
    from_behind = lax.ppermute(first, "expert", ahead)
    from_ahead = lax.ppermute(second, "expert", behind)
    is_two = kind == 2

    def pick(flag, left, right):
        return tuple(jnp.where(flag, l, r) for l, r in zip(left, right))

    send_ahead = pick(is_two, from_behind, second)
    send_behind = pick(is_two, from_ahead, first)
    got_behind = lax.ppermute(send_ahead, "expert", ahead)
    got_ahead = lax.ppermute(send_behind, "expert", behind)
    one_even = (kind == 1) & even
    one_odd = (kind == 1) & ~even
    new_first = pick(is_two, got_behind, pick(one_even, got_ahead, pick(one_odd, from_behind, first)))
    new_second = pick(is_two, got_ahead, pick(one_even, from_ahead, pick(one_odd, got_behind, second)))
    new_gate_up = jnp.concatenate([new_first[0], new_second[0]], axis=2)
    new_down = jnp.concatenate([new_first[1], new_second[1]], axis=1)
    return (new_gate_up, new_down)


def run_layer(tokens, expert_ids, route_weights, gate_up, down):
    devices = lax.axis_size("expert")
    token_rows, model_width = tokens.shape
    top_count = expert_ids.shape[1]
    expert_count = devices
    capacity = min(token_rows, 3 * token_rows * top_count // (2 * expert_count))
    half_width = model_width // 2
    side = lax.rem(lax.axis_index("dp"), 2)
    own_half = lax.dynamic_slice_in_dim(tokens, side * half_width, half_width, 1)
    labels = jnp.arange(expert_count, dtype=jnp.int32)
    onehot = (expert_ids[:, :, None] == labels[None, None, :]).astype(jnp.int32)
    picked = jnp.sum(onehot, axis=1)
    slot_rank = jnp.cumsum(picked, axis=0) - picked
    slots = jnp.sum(onehot * slot_rank[:, None, :], axis=2)
    place = (expert_ids * capacity + slots).reshape(-1)
    row_ids = jnp.repeat(jnp.arange(token_rows, dtype=jnp.int32), top_count)
    source = jnp.full((devices * capacity,), token_rows, jnp.int32).at[place].set(row_ids)
    padded = jnp.concatenate([own_half, jnp.zeros((1, half_width), own_half.dtype)], axis=0)
    outgoing = padded[source].reshape(devices, capacity, half_width)
    arrived = lax.all_to_all(outgoing, "expert", split_axis=0, concat_axis=0, tiled=True)
    flat = arrived.reshape(devices * capacity, half_width)
    partial_value = jnp.dot(flat, gate_up, preferred_element_type=jnp.float32)
    half_rows = flat.shape[0] // 2
    mine = lax.dynamic_slice_in_dim(partial_value, side * half_rows, half_rows, 0)
    other = lax.dynamic_slice_in_dim(partial_value, (1 - side) * half_rows, half_rows, 0)
    route = [(low, low ^ 1) for low in range(lax.axis_size("dp"))]
    summed = mine + lax.ppermute(other, "dp", route)
    block_units = gate_up.shape[1] // 2
    hidden = (jax.nn.silu(summed[:, :block_units]) * summed[:, block_units:]).astype(jnp.bfloat16)
    gathered = lax.all_gather(hidden, "dp", axis=0, tiled=False)
    pair_count = lax.axis_size("dp") // 2
    out_columns = down.shape[1]
    outputs = jnp.einsum(
        "qhrk,qkc->hrc",
        gathered.reshape(pair_count, 2, half_rows, block_units),
        down.reshape(pair_count, block_units, out_columns),
        preferred_element_type=jnp.float32,
    )
    expert_out = outputs.reshape(devices, capacity, out_columns).astype(jnp.bfloat16)
    returned = lax.all_to_all(expert_out, "expert", split_axis=0, concat_axis=0, tiled=True)
    chosen = returned.reshape(devices * capacity, out_columns)[place].reshape(
        token_rows, top_count, out_columns
    )
    mixed = jnp.sum(chosen.astype(jnp.float32) * route_weights[:, :, None], axis=1)
    return mixed.astype(jnp.bfloat16)


def per_device(tokens, expert_ids, route_weights, gate_up_panels, down_panels, partner):
    moe_out = run_layer(tokens, expert_ids, route_weights, gate_up_panels[0, 0], down_panels[0])
    new_gate_up, new_down = swap_panels(gate_up_panels, down_panels, partner)
    return (moe_out, new_gate_up, new_down)


def solution(mesh):
    return jax.shard_map(
        per_device,
        mesh=mesh,
        in_specs=(
            P("expert", None),
            P("expert", None),
            P("expert", None),
            P("expert", "dp", None, None),
            P("expert", None, "dp"),
            P(),
        ),
        out_specs=(P("expert", "dp"), P("expert", "dp", None, None), P("expert", None, "dp")),
        check_vma=False,
    )
```

time: 460 us -> 495 us (1.076); the launches traced: 460 us -> 487 us
  waiting for transfers between devices: 319 us -> 369 us
  starting transfers between devices: 85.6 us -> 60 us
  other arithmetic: 5.51 us -> 12.3 us
    all_to_all x1, waiting for transfers between devices: 0.01 us -> 108 us  [run_layer(): lax.all_to_all(outgoing, 'expert', split_axis=0, concat_axis=0, tiled=True)]
    ppermute x5 -> x9, waiting for transfers between devices: 124 us -> 18.7 us  [the longest x2 8.83 us: swap_panels(): from_behind = lax.ppermute(first, 'expert', ahead)]
    all_gather x1, waiting for transfers between devices: 158 us -> 242 us  [run_layer(): gathered = lax.all_gather(hidden, 'dp', axis=0, tiled=False)]
    all_to_all x1, waiting for transfers between devices: 37.3 us -> 0.01 us  [run_layer(): lax.all_to_all(expert_out, 'expert', split_axis=0, concat_axis=0, tiled=T...]
    ppermute x5 -> x9, starting transfers between devices: 53.3 us -> 28.2 us  [the longest x2 7.36 us: swap_panels(): got_behind = lax.ppermute(send_ahead, 'expert', ahead)]
  transfers between devices with their start and end apart: 8 -> 12, of which waited for: 7 -> 6; matrix products, arithmetic and copies ran while one was open for 1% -> 2% of each run, Pallas kernels for 0% -> 0%
where the time goes in v1:
time: 495 us; the launch traced here: 487 us
  waiting for transfers between devices  369 us (75%)
  starting transfers between devices  60 us (12%)
  local copies, waits for them, and re-layouts  25.2 us (5%)
  between operations  15 us (3%)
  other arithmetic  12.3 us (2%)
  matrix products  6.14 us (1%)
    all_gather x1, waiting for transfers between devices, run_layer(): gathered = lax.all_gather(hidden, 'dp', axis=0, tiled=False)  242 us
    all_to_all x1, waiting for transfers between devices, run_layer(): lax.all_to_all(outgoing, 'expert', split_axis=0, concat_axis=0, tiled=True)  108 us
    all_to_all x1, starting transfers between devices, run_layer(): lax.all_to_all(outgoing, 'expert', split_axis=0, concat_axis=0, tiled=True)  21.4 us
    all_to_all x1, starting transfers between devices, run_layer(): lax.all_to_all(expert_out, 'expert', split_axis=0, concat_axis=0, tiled=T...  10.4 us
  transfers between devices with their start and end apart: 12, of which 6 were waited for; matrix products, arithmetic and copies ran while one was open for 2% of the time, Pallas kernels for 0%

profile of v1, /device:TPU:1, one launch (start us, length us, event | category | flops | bytes accessed | tf_op | source)
XLA Modules:
  0.0 487.4 jit_solution(1345288775151102010)
XLA Ops:
  10.1 4.3 scatter_custom_fusion
  14.5 6.7 %gather_fusion = bf16[1536,1792]{1,0:T(8,128)(2,1)} fusion(bf16[129,1792]{1,0:T(8,128)(2,1)S(1)} %concatenate.9, s32[2048]{0:T(1024)S(1)} %pad_clamp_fusion), kind=kCustom, calls=%fused_computation | custom fusion | bytes 11016192 | tf_op jit(solution)/shard_map/gather | solution.py:59
  21.3 21.4 %all-to-all-start = ((bf16[32,48,1792]{2,1,0:T(8,128)(2,1)}), bf16[32,48,1792]{2,1,0:T(8,128)(2,1)}, u32[]{:S(2)}, u32[]{:S(2)}) async-start(bf16[32,48,1792]{2,1,0:T(8,128)(2,1)} %bitcast.28), calls=%async_computation | async-start | bytes 11010048 | tf_op jit(solution)/shard_map/all_to_all | solution.py:60
  42.7 108.3 %all-to-all-done = bf16[32,48,1792]{2,1,0:T(8,128)(2,1)} async-done(((bf16[32,48,1792]{2,1,0:T(8,128)(2,1)}), bf16[32,48,1792]{2,1,0:T(8,128)(2,1)}, u32[]{:S(2)}, u32[]{:S(2)}) %all-to-all-start) | async-done | bytes 5505056 | tf_op jit(solution)/shard_map/all_to_all | solution.py:60
  151.0 4.2 fusion.5
  157.3 3.5 collective-permute-start
  160.8 2.1 collective-permute-done
  165.1 241.7 %all-gather.3.cloned.1.call-done = bf16[12288,128]{1,0:T(8,128)(2,1)} async-done(((bf16[768,128]{1,0:T(8,128)(2,1)}), bf16[12288,128]{1,0:T(8,128)(2,1)}) %all-gather.3.cloned.1.call-update) | async-done | bytes 3145744 | tf_op jit(solution)/shard_map/all_gather | solution.py:70
  406.8 3.9 copy.29
  410.7 1.9 bitcast_convert_fusion
  412.6 10.4 %all-to-all-start.1 = ((bf16[32,48,224]{2,1,0:T(8,128)(2,1)}), bf16[32,48,224]{2,1,0:T(8,128)(2,1)S(1)}, u32[]{:S(2)}, u32[]{:S(2)}) async-start(bf16[32,48,224]{2,1,0:T(8,128)(2,1)} %bitcast_convert_fusion), calls=%async_computation.1 | async-start | bytes 1572864 | tf_op jit(solution)/shard_map/all_to_all | solution.py:80
  423.7 3.1 collective-permute-start.5
  427.6 3.1 collective-permute-start.1
  432.7 3.4 collective-permute-start.7
  436.1 8.8 %collective-permute-done.1 = bf16[1,1,896,256]{3,2,1,0:T(8,128)(2,1)S(1)} collective-permute-done((bf16[1,1,896,256]{3,2,1,0:T(8,128)(2,1)}, bf16[1,1,896,256]{3,2,1,0:T(8,128)(2,1)S(1)}, u32[]{:S(2)}, u32[]{:S(2)}) %collective-permute-start.1) | collective-permute-done | bytes 458784 | tf_op jit(solution)/shard_map/ppermute | solution.py:21
  445.9 1.9 collective-permute-start.3
  447.8 3.8 collective-permute-start.6
  451.6 3.5 collective-permute-start.2
  456.0 2.9 collective-permute-start.8
  459.8 2.9 collective-permute-start.4
  463.5 2.2 collective-permute-done.8
  467.6 5.6 %collective-permute-done.4 = bf16[1,1,896,256]{3,2,1,0:T(8,128)(2,1)} collective-permute-done((bf16[1,1,896,256]{3,2,1,0:T(8,128)(2,1)}, bf16[1,1,896,256]{3,2,1,0:T(8,128)(2,1)}, u32[]{:S(2)}, u32[]{:S(2)}) %collective-permute-start.4) | collective-permute-done | bytes 458784 | tf_op jit(solution)/shard_map/ppermute | solution.py:31
  473.2 1.3 select_select_fusion.1
  475.5 3.9 gather_fusion.1
  (60 shorter events, 17.4 us)
Async XLA Ops:
  7.2 7.3 %copy-start = (bf16[128,3584]{1,0:T(8,128)(2,1)S(1)}, bf16[128,3584]{1,0:T(8,128)(2,1)}, u32[]{:S(2)}) copy-start(bf16[128,3584]{1,0:T(8,128)(2,1)} %param.6) | copy-start | bytes 2752516
  21.3 129.7 %copy-start.1 = (bf16[1,1,1792,256]{3,2,1,0:T(8,128)(2,1)S(1)}, bf16[1,1,1792,256]{3,2,1,0:T(8,128)(2,1)}, u32[]{:S(2)}) copy-start(bf16[1,1,1792,256]{3,2,1,0:T(8,128)(2,1)} %param.9) | copy-start | bytes 2752516
  21.3 129.7 %all-to-all-start = ((bf16[32,48,1792]{2,1,0:T(8,128)(2,1)}), bf16[32,48,1792]{2,1,0:T(8,128)(2,1)}, u32[]{:S(2)}, u32[]{:S(2)}) async-start(bf16[32,48,1792]{2,1,0:T(8,128)(2,1)} %bitcast.28), calls=%async_computation | async-start | bytes 11010048 | tf_op jit(solution)/shard_map/all_to_all | solution.py:60
  42.6 364.2 %all-gather.3.cloned.1.call-start = ((), (), s32[]{:S(2)}) async-start(), calls=%async_computation.2 | async-start | bytes 3342336 | tf_op jit(solution)/shard_map/all_gather | solution.py:70
  155.2 1.2 copy-start.4
  156.4 8.6 %copy-start.2 = (bf16[1,1024,224]{1,2,0:T(8,128)(2,1)S(1)}, bf16[1,1024,224]{1,2,0:T(8,128)(2,1)}, u32[]{:S(2)}) copy-start(bf16[1,1024,224]{1,2,0:T(8,128)(2,1)} %param.10) | copy-start | bytes 1376260
  157.3 5.6 %collective-permute-start = (f32[768,256]{1,0:T(8,128)}, f32[768,256]{1,0:T(8,128)S(1)}, u32[]{:S(2)}, u32[]{:S(2)}) collective-permute-start(f32[768,256]{1,0:T(8,128)} %constant_dynamic-slice_fusion), channel_id=1, source_target_pairs={{0,1},{1,0},{2,3},{3,2},{4,5},{5,4},{6,7},{7,6},{8,9},{9,8},{10,11... | collective-permute-start | bytes 2359304 | tf_op jit(solution)/shard_map/ppermute | solution.py:67
  410.7 20.0 %copy-start.8 = (s32[32]{0:T(128)S(1)}, s32[32]{0:T(128)}, u32[]{:S(2)}) copy-start(s32[32]{0:T(128)} %param.11) | copy-start | bytes 388
  412.6 62.9 %all-to-all-start.1 = ((bf16[32,48,224]{2,1,0:T(8,128)(2,1)}), bf16[32,48,224]{2,1,0:T(8,128)(2,1)S(1)}, u32[]{:S(2)}, u32[]{:S(2)}) async-start(bf16[32,48,224]{2,1,0:T(8,128)(2,1)} %bitcast_convert_fusion), calls=%async_computation.1 | async-start | bytes 1572864 | tf_op jit(solution)/shard_map/all_to_all | solution.py:80
  423.0 39.7 %copy-start.7 = (f32[128,8]{0,1:T(8,128)S(1)}, f32[128,8]{0,1:T(8,128)}, u32[]{:S(2)}) copy-start(f32[128,8]{0,1:T(8,128)} %param.8) | copy-start | bytes 12292
  423.7 8.3 %collective-permute-start.5 = (bf16[1,512,224]{1,2,0:T(8,128)(2,1)}, bf16[1,512,224]{1,2,0:T(8,128)(2,1)}, u32[]{:S(2)}, u32[]{:S(2)}) collective-permute-start(bf16[1,512,224]{1,2,0:T(8,128)(2,1)} %slice.22), channel_id=1, source_target_pairs={{0,16},{16,32},{32,48},{48,0},{64,80},{80,96},{96,112},{112,64},{1... | collective-permute-start | bytes 688136 | tf_op jit(solution)/shard_map/ppermute | solution.py:21
  427.6 17.3 %collective-permute-start.1 = (bf16[1,1,896,256]{3,2,1,0:T(8,128)(2,1)}, bf16[1,1,896,256]{3,2,1,0:T(8,128)(2,1)S(1)}, u32[]{:S(2)}, u32[]{:S(2)}) collective-permute-start(bf16[1,1,896,256]{3,2,1,0:T(8,128)(2,1)} %slice.20), channel_id=1, source_target_pairs={{0,16},{16,32},{32,48},{48,0},{64,80},{80,96},{96,112},{112,64},{1... | collective-permute-start | bytes 1376264 | tf_op jit(solution)/shard_map/ppermute | solution.py:21
  432.7 22.5 %collective-permute-start.7 = (bf16[1,512,224]{1,2,0:T(8,128)(2,1)S(1)}, bf16[1,512,224]{1,2,0:T(8,128)(2,1)S(1)}, u32[]{:S(2)}, u32[]{:S(2)}) collective-permute-start(bf16[1,512,224]{1,2,0:T(8,128)(2,1)S(1)} %get-tuple-element.16), channel_id=1, source_target_pairs={{0,48},{16,0},{32,16},{48,32},{64,112},{80,64},{96,80},{112,96},{1... | collective-permute-start | bytes 688136 | tf_op jit(solution)/shard_map/ppermute | solution.py:22
  445.0 0.9 copy-start.3
  445.9 13.0 %collective-permute-start.3 = (bf16[1,1,896,256]{3,2,1,0:T(8,128)(2,1)S(1)}, bf16[1,1,896,256]{3,2,1,0:T(8,128)(2,1)S(1)}, u32[]{:S(2)}, u32[]{:S(2)}) collective-permute-start(bf16[1,1,896,256]{3,2,1,0:T(8,128)(2,1)S(1)} %get-tuple-element.14), channel_id=1, source_target_pairs={{0,48},{16,0},{32,16},{48,32},{64,112},{80,64},{96,80},{112,96},{1... | collective-permute-start | bytes 1376264 | tf_op jit(solution)/shard_map/ppermute | solution.py:22
  447.8 15.6 %collective-permute-start.6 = (bf16[1,512,224]{1,2,0:T(8,128)(2,1)}, bf16[1,512,224]{1,2,0:T(8,128)(2,1)}, u32[]{:S(2)}, u32[]{:S(2)}) collective-permute-start(bf16[1,512,224]{1,2,0:T(8,128)(2,1)} %get-tuple-element.15), channel_id=1, source_target_pairs={{0,16},{16,32},{32,48},{48,0},{64,80},{80,96},{96,112},{112,64},{1... | collective-permute-start | bytes 688136 | tf_op jit(solution)/shard_map/ppermute | solution.py:30
  451.6 16.0 %collective-permute-start.2 = (bf16[1,1,896,256]{3,2,1,0:T(8,128)(2,1)}, bf16[1,1,896,256]{3,2,1,0:T(8,128)(2,1)}, u32[]{:S(2)}, u32[]{:S(2)}) collective-permute-start(bf16[1,1,896,256]{3,2,1,0:T(8,128)(2,1)} %get-tuple-element.13), channel_id=1, source_target_pairs={{0,16},{16,32},{32,48},{48,0},{64,80},{80,96},{96,112},{112,64},{1... | collective-permute-start | bytes 1376264 | tf_op jit(solution)/shard_map/ppermute | solution.py:30
  455.2 3.7 copy-start.5
  456.0 9.7 %collective-permute-start.8 = (bf16[1,512,224]{1,2,0:T(8,128)(2,1)}, bf16[1,512,224]{1,2,0:T(8,128)(2,1)}, u32[]{:S(2)}, u32[]{:S(2)}) collective-permute-start(bf16[1,512,224]{1,2,0:T(8,128)(2,1)} %broadcast_select_fusion.2), channel_id=1, source_target_pairs={{0,48},{16,0},{32,16},{48,32},{64,112},{80,64},{96,80},{112,96},{1... | collective-permute-start | bytes 688136 | tf_op jit(solution)/shard_map/ppermute | solution.py:31
  459.8 13.4 %collective-permute-start.4 = (bf16[1,1,896,256]{3,2,1,0:T(8,128)(2,1)}, bf16[1,1,896,256]{3,2,1,0:T(8,128)(2,1)}, u32[]{:S(2)}, u32[]{:S(2)}) collective-permute-start(bf16[1,1,896,256]{3,2,1,0:T(8,128)(2,1)} %broadcast_select_fusion), channel_id=1, source_target_pairs={{0,48},{16,0},{32,16},{48,32},{64,112},{80,64},{96,80},{112,96},{1... | collective-permute-start | bytes 1376264 | tf_op jit(solution)/shard_map/ppermute | solution.py:31
  474.5 4.9 %copy-start.6 = (f32[128,8]{1,0:T(8,128)S(1)}, f32[128,8]{1,0:T(8,128)}, u32[]{:S(2)}) copy-start(f32[128,8]{1,0:T(8,128)} %copy.32) | copy-start | bytes 12292
Sparse Core Ops, SparseCore 0:
  165.1 241.6 all-gather.2

commit v2 on v1

v2 whole, which is shorter than its diff:
```python
import jax
import jax.numpy as jnp
from jax import lax
from jax.sharding import Mesh
from jax.sharding import PartitionSpec as P

EXPERT = ("y", "zhi", "x")
DP = ("zlo", "core")
FLIP = [(0, 1), (1, 0)]


def swap_panels(gate_up, down, partner):
    here = lax.axis_index(EXPERT)
    kind = jnp.bitwise_xor(partner[here], here)
    even = (lax.axis_index("x") & 1) == 0
    gate_rows = gate_up.shape[2] // 2
    down_rows = down.shape[1] // 2
    first = (gate_up[:, :, :gate_rows], down[:, :down_rows])
    second = (gate_up[:, :, gate_rows:], down[:, down_rows:])
    ring = lax.axis_size("x")
    ahead = [(i, (i + 1) % ring) for i in range(ring)]
    behind = [(i, (i + ring - 1) % ring) for i in range(ring)]
    from_behind = lax.ppermute(first, "x", ahead)
    from_ahead = lax.ppermute(second, "x", behind)
    is_two = kind == 2

    def pick(flag, left, right):
        return tuple(jnp.where(flag, l, r) for l, r in zip(left, right))

    send_ahead = pick(is_two, from_behind, second)
    send_behind = pick(is_two, from_ahead, first)
    got_behind = lax.ppermute(send_ahead, "x", ahead)
    got_ahead = lax.ppermute(send_behind, "x", behind)
    one_even = (kind == 1) & even
    one_odd = (kind == 1) & ~even
    new_first = pick(is_two, got_behind, pick(one_even, got_ahead, pick(one_odd, from_behind, first)))
    new_second = pick(is_two, got_ahead, pick(one_even, from_ahead, pick(one_odd, got_behind, second)))
    new_gate_up = jnp.concatenate([new_first[0], new_second[0]], axis=2)
    new_down = jnp.concatenate([new_first[1], new_second[1]], axis=1)
    return (new_gate_up, new_down)


def run_layer(tokens, expert_ids, route_weights, gate_up, down):
    rows_y, rows_x = lax.axis_size("y"), lax.axis_size("x")
    lines = rows_y * rows_x
    expert_count = 2 * lines
    chunks = lax.axis_size("zlo")
    token_rows, model_width = tokens.shape
    top_count = expert_ids.shape[1]
    capacity = min(token_rows, 3 * token_rows * top_count // (2 * expert_count))
    half_width = model_width // 2
    chunk_width = half_width // chunks
    side = lax.axis_index("core")
    zhi = lax.axis_index("zhi")
    own_half = lax.dynamic_slice_in_dim(tokens, side * half_width, half_width, 1)
    own_chunk = lax.dynamic_slice_in_dim(
        tokens, side * half_width + lax.axis_index("zlo") * chunk_width, chunk_width, 1
    )
    labels = jnp.arange(expert_count, dtype=jnp.int32)
    onehot = (expert_ids[:, :, None] == labels[None, None, :]).astype(jnp.int32)
    picked = jnp.sum(onehot, axis=1)
    slot_rank = jnp.cumsum(picked, axis=0) - picked
    slots = jnp.sum(onehot * slot_rank[:, None, :], axis=2)
    place = (expert_ids * capacity + slots).reshape(-1)
    row_ids = jnp.repeat(jnp.arange(token_rows, dtype=jnp.int32), top_count)
    source = jnp.full((expert_count * capacity,), token_rows, jnp.int32).at[place].set(row_ids)
    source = source.reshape(rows_y, 2, rows_x, capacity)
    near_source = lax.dynamic_index_in_dim(source, zhi, 1, keepdims=False).reshape(-1)
    far_source = lax.dynamic_index_in_dim(source, 1 - zhi, 1, keepdims=False).reshape(-1)
    padded_half = jnp.concatenate([own_half, jnp.zeros((1, half_width), tokens.dtype)], axis=0)
    padded_chunk = jnp.concatenate([own_chunk, jnp.zeros((1, chunk_width), tokens.dtype)], axis=0)
    near_out = padded_half[near_source].reshape(lines, capacity, half_width)
    far_out = padded_chunk[far_source].reshape(lines, capacity, chunk_width)
    near_in = lax.all_to_all(near_out, ("y", "x"), 0, 0, tiled=True)
    far_mid = lax.ppermute(far_out, "zhi", FLIP)
    far_in = lax.all_to_all(far_mid, ("y", "x"), 0, 0, tiled=True)
    far_full = lax.all_gather(far_in, "zlo", axis=0, tiled=False)
    part_rows = lines * capacity
    near_value = jnp.dot(near_in.reshape(part_rows, half_width), gate_up, preferred_element_type=jnp.float32)
    far_value = jnp.einsum(
        "cnf,cfu->nu",
        far_full.reshape(chunks, part_rows, chunk_width),
        gate_up.reshape(chunks, chunk_width, gate_up.shape[1]),
        preferred_element_type=jnp.float32,
    )
    keep_near = side == 0
    mine = jnp.where(keep_near, near_value, far_value)
    other = jnp.where(keep_near, far_value, near_value)
    summed = mine + lax.ppermute(other, "core", FLIP)
    block_units = gate_up.shape[1] // 2
    hidden = (jax.nn.silu(summed[:, :block_units]) * summed[:, block_units:]).astype(jnp.bfloat16)
    gathered = lax.all_gather(hidden, "zlo", axis=0, tiled=False)
    partner_part = lax.ppermute(gathered, "core", FLIP)
    near_hidden = jnp.where(keep_near, gathered, partner_part)
    far_hidden = jnp.where(keep_near, partner_part, gathered)
    out_columns = down.shape[1]
    down_blocks = down.reshape(chunks, block_units, out_columns)

    def project(hidden_part):
        value = jnp.einsum("qrk,qkc->rc", hidden_part, down_blocks, preferred_element_type=jnp.float32)
        return value.astype(jnp.bfloat16).reshape(lines, capacity, out_columns)

    near_back = lax.all_to_all(project(near_hidden), ("y", "x"), 0, 0, tiled=True)
    far_back = lax.ppermute(lax.all_to_all(project(far_hidden), ("y", "x"), 0, 0, tiled=True), "zhi", FLIP)
    near_back = near_back.reshape(rows_y, rows_x, capacity, out_columns)
    far_back = far_back.reshape(rows_y, rows_x, capacity, out_columns)
    low_first = zhi == 0
    returned = jnp.stack(
        [jnp.where(low_first, near_back, far_back), jnp.where(low_first, far_back, near_back)], axis=1
    )
    chosen = returned.reshape(expert_count * capacity, out_columns)[place].reshape(
        token_rows, top_count, out_columns
    )
    mixed = jnp.sum(chosen.astype(jnp.float32) * route_weights[:, :, None], axis=1)
    return mixed.astype(jnp.bfloat16)


def per_device(tokens, expert_ids, route_weights, gate_up_panels, down_panels, partner):
    moe_out = run_layer(tokens, expert_ids, route_weights, gate_up_panels[0, 0], down_panels[0])
    new_gate_up, new_down = swap_panels(gate_up_panels, down_panels, partner)
    return (moe_out, new_gate_up, new_down)


def solution(mesh):
    experts, dps = mesh.devices.shape
    layout = mesh.devices.reshape(experts // 8, 2, 4, dps // 2, 2)
    split = Mesh(layout, EXPERT + DP)
    return jax.shard_map(
        per_device,
        mesh=split,
        in_specs=(
            P(EXPERT, None),
            P(EXPERT, None),
            P(EXPERT, None),
            P(EXPERT, DP, None, None),
            P(EXPERT, None, DP),
            P(),
        ),
        out_specs=(P(EXPERT, DP), P(EXPERT, DP, None, None), P(EXPERT, None, DP)),
        check_vma=False,
    )
```

time: 495 us -> 341 us (0.69); the launches traced: 487 us -> 340 us
  waiting for transfers between devices: 369 us -> 192 us
  blocking collectives: 0 us -> 15.9 us
  starting transfers between devices: 60 us -> 71.5 us
    all_gather x1 -> x2, waiting for transfers between devices: 242 us -> 98.3 us  [the longest x1 58.1 us: run_layer(): far_full = lax.all_gather(far_in, 'zlo', axis=0, tiled=False)]
    all_to_all x2 -> x3, waiting for transfers between devices: 108 us -> 37.6 us  [the longest x1 34 us: run_layer(): near_in = lax.all_to_all(near_out, ('y', 'x'), 0, 0, tiled=True)]
    ppermute x9 -> x12, waiting for transfers between devices: 18.7 us -> 56.3 us  [the longest x1 30.6 us: run_layer(): lax.ppermute(lax.all_to_all(project(far_hidden), ('y', 'x'), 0, 0, tiled=...]
    ppermute x9 -> x12, starting transfers between devices: 28.2 us -> 58.5 us  [the longest x1 16.3 us: run_layer(): far_mid = lax.ppermute(far_out, 'zhi', FLIP)]
    all_to_all x2 -> x3, starting transfers between devices: 31.7 us -> 12.9 us  [the longest x1 4.59 us: run_layer(): near_in = lax.all_to_all(near_out, ('y', 'x'), 0, 0, tiled=True)]
    all_to_all x0 -> x1, blocking collectives: none -> 15.9 us  [run_layer(): far_in = lax.all_to_all(far_mid, ('y', 'x'), 0, 0, tiled=True)]
    gather x2 -> x3, local copies, waits for them, and re-layouts: 10.7 us -> 10.7 us  [the longest x1 4.13 us: run_layer(): near_out = padded_half[near_source].reshape(lines, capacity, half_width)]
  transfers between devices with their start and end apart: 12 -> 17, of which waited for: 6 -> 9; matrix products, arithmetic and copies ran while one was open for 2% -> 7% of each run, Pallas kernels for 0% -> 0%
where the time goes in v2:
time: 341 us; the launch traced here: 340 us
  waiting for transfers between devices  192 us (56%)
  starting transfers between devices  71.5 us (21%)
  local copies, waits for them, and re-layouts  22.9 us (7%)
  blocking collectives  15.9 us (5%)
  between operations  15.2 us (4%)
  other arithmetic  12.7 us (4%)
  matrix products  9.7 us (3%)
    all_gather x1, waiting for transfers between devices, run_layer(): far_full = lax.all_gather(far_in, 'zlo', axis=0, tiled=False)  58.1 us
    all_gather x1, waiting for transfers between devices, run_layer(): gathered = lax.all_gather(hidden, 'zlo', axis=0, tiled=False)  40.2 us
    all_to_all x1, waiting for transfers between devices, run_layer(): near_in = lax.all_to_all(near_out, ('y', 'x'), 0, 0, tiled=True)  34 us
    ppermute x1, waiting for transfers between devices, run_layer(): lax.ppermute(lax.all_to_all(project(far_hidden), ('y', 'x'), 0, 0, tiled=...  30.6 us
    ppermute x1, starting transfers between devices, run_layer(): far_mid = lax.ppermute(far_out, 'zhi', FLIP)  16.3 us
    all_to_all x1, blocking collectives, run_layer(): far_in = lax.all_to_all(far_mid, ('y', 'x'), 0, 0, tiled=True)  15.9 us
    ppermute x1, waiting for transfers between devices, run_layer(): far_mid = lax.ppermute(far_out, 'zhi', FLIP)  12.1 us
    ppermute x1, starting transfers between devices, run_layer(): partner_part = lax.ppermute(gathered, 'core', FLIP)  8.27 us
  transfers between devices with their start and end apart: 17, of which 9 were waited for; matrix products, arithmetic and copies ran while one was open for 7% of the time, Pallas kernels for 0%

profile of v2, /device:TPU:1, one launch (start us, length us, event | category | flops | bytes accessed | tf_op | source)
XLA Modules:
  0.0 340.1 jit_solution(12017352504271716204)
XLA Ops:
  10.1 4.3 %scatter_custom_fusion = s32[1536]{0:T(1024)S(1)} fusion(s32[1024]{0:T(1024)S(1)} %bitcast.51, s32[1024]{0:T(1024)S(1)} %reshape.223, s32[]{:T(128)} %constant.28.clone.1), kind=kCustom, calls=%fused_computation.47 | custom fusion | bytes 6148 | tf_op jit(solution)/shard_map/scatter | solution.py:66
  17.5 16.3 %collective-permute-start = (bf16[16,48,224]{2,1,0:T(8,128)(2,1)S(1)}, bf16[16,48,224]{2,1,0:T(8,128)(2,1)S(1)}, u32[]{:S(2)}, u32[]{:S(2)}) collective-permute-start(bf16[16,48,224]{2,1,0:T(8,128)(2,1)S(1)} %bitcast.50), channel_id=1, source_target_pairs={{0,64},{64,0},{1,65},{65,1},{2,66},{66,2},{3,67},{67,3},{4,68},{68... | collective-permute-start | bytes 1032200 | tf_op jit(solution)/shard_map/ppermute | solution.py:75
  33.7 12.1 %collective-permute-done = bf16[16,48,224]{2,1,0:T(8,128)(2,1)S(1)} collective-permute-done((bf16[16,48,224]{2,1,0:T(8,128)(2,1)S(1)}, bf16[16,48,224]{2,1,0:T(8,128)(2,1)S(1)}, u32[]{:S(2)}, u32[]{:S(2)}) %collective-permute-start) | collective-permute-done | bytes 344096 | tf_op jit(solution)/shard_map/ppermute | solution.py:75
  45.8 15.9 %all_to_all.20 = bf16[16,48,224]{2,1,0:T(8,128)(2,1)} all-to-all(bf16[16,48,224]{2,1,0:T(8,128)(2,1)S(1)} %collective-permute-done), channel_id=1, replica_groups=mesh['y'=4,'zhi'=2,'x'=4,'zlo'=8,'core'=2] {'y','x'}, dimensions={0} | all-to-all | bytes 688128 | tf_op jit(solution)/shard_map/all_to_all | solution.py:76
  61.9 4.1 %gather_fusion = bf16[768,1792]{1,0:T(8,128)(2,1)} fusion(bf16[129,1792]{1,0:T(8,128)(2,1)S(1)} %concatenate.12, s32[1024]{0:T(1024)S(1)} %pad_clamp_fusion.1), kind=kCustom, calls=%fused_computation | custom fusion | bytes 5508096 | tf_op jit(solution)/shard_map/gather | solution.py:72
  66.0 4.6 %all-to-all-start = ((bf16[16,48,1792]{2,1,0:T(8,128)(2,1)}), bf16[16,48,1792]{2,1,0:T(8,128)(2,1)}, u32[]{:S(2)}, u32[]{:S(2)}) async-start(bf16[16,48,1792]{2,1,0:T(8,128)(2,1)} %bitcast.43), calls=%async_computation | async-start | bytes 5505024 | tf_op jit(solution)/shard_map/all_to_all | solution.py:74
  70.7 34.0 %all-to-all-done = bf16[16,48,1792]{2,1,0:T(8,128)(2,1)} async-done(((bf16[16,48,1792]{2,1,0:T(8,128)(2,1)}), bf16[16,48,1792]{2,1,0:T(8,128)(2,1)}, u32[]{:S(2)}, u32[]{:S(2)}) %all-to-all-start) | async-done | bytes 2752544 | tf_op jit(solution)/shard_map/all_to_all | solution.py:74
  107.3 58.1 %all-gather.5.cloned.1.call-done = bf16[128,48,224]{2,1,0:T(8,128)(2,1)} async-done(((bf16[16,48,224]{2,1,0:T(8,128)(2,1)}), bf16[128,48,224]{2,1,0:T(8,128)(2,1)}) %all-gather.5.cloned.1.call-update) | async-done | bytes 2752528 | tf_op jit(solution)/shard_map/all_gather | solution.py:77
  174.3 3.1 collective-permute-start.8
  178.6 5.5 %collective-permute-done.8 = bf16[1,512,224]{1,2,0:T(8,128)(2,1)S(1)} collective-permute-done((bf16[1,512,224]{1,2,0:T(8,128)(2,1)S(1)}, bf16[1,512,224]{1,2,0:T(8,128)(2,1)S(1)}, u32[]{:S(2)}, u32[]{:S(2)}) %collective-permute-start.8) | collective-permute-done | bytes 229408 | tf_op jit(solution)/shard_map/ppermute | solution.py:23
  184.9 3.1 collective-permute-start.10
  191.1 40.2 %all-gather.7.cloned.1.call-done = bf16[6144,128]{1,0:T(8,128)(2,1)} async-done(((bf16[768,128]{1,0:T(8,128)(2,1)}), bf16[6144,128]{1,0:T(8,128)(2,1)}) %all-gather.7.cloned.1.call-update) | async-done | bytes 1572880 | tf_op jit(solution)/shard_map/all_gather | solution.py:92
  231.3 8.3 %collective-permute-start.2 = (bf16[8,768,128]{2,1,0:T(8,128)(2,1)}, bf16[8,768,128]{2,1,0:T(8,128)(2,1)}, u32[]{:S(2)}, u32[]{:S(2)}) collective-permute-start(bf16[8,768,128]{2,1,0:T(8,128)(2,1)} %bitcast.53), channel_id=1, source_target_pairs={{0,1},{1,0},{2,3},{3,2},{4,5},{5,4},{6,7},{7,6},{8,9},{9,8},{10,11... | collective-permute-start | bytes 4718600 | tf_op jit(solution)/shard_map/ppermute | solution.py:93
  239.6 3.1 collective-permute-start.9
  243.5 3.3 collective-permute-start.11
  247.9 3.1 collective-permute-start.6
  256.4 6.2 %collective-permute-done.6 = bf16[1,1,896,256]{3,2,1,0:T(8,128)(2,1)S(1)} collective-permute-done((bf16[1,1,896,256]{3,2,1,0:T(8,128)(2,1)}, bf16[1,1,896,256]{3,2,1,0:T(8,128)(2,1)S(1)}, u32[]{:S(2)}, u32[]{:S(2)}) %collective-permute-start.6) | collective-permute-done | bytes 458784 | tf_op jit(solution)/shard_map/ppermute | solution.py:24
  263.5 4.3 %collective-permute-start.7 = (bf16[1,1,896,256]{3,2,1,0:T(8,128)(2,1)}, bf16[1,1,896,256]{3,2,1,0:T(8,128)(2,1)}, u32[]{:S(2)}, u32[]{:S(2)}) collective-permute-start(bf16[1,1,896,256]{3,2,1,0:T(8,128)(2,1)} %broadcast_select_fusion), channel_id=1, source_target_pairs={{0,48},{16,0},{32,16},{48,32},{1,49},{17,1},{33,17},{49,33},{2,50}... | collective-permute-start | bytes 1376264 | tf_op jit(solution)/shard_map/ppermute | solution.py:33
  271.1 4.3 %all-to-all-start.3 = ((bf16[16,48,224]{2,1,0:T(8,128)(2,1)}), bf16[16,48,224]{2,1,0:T(8,128)(2,1)}, u32[]{:S(2)}, u32[]{:S(2)}) async-start(bf16[16,48,224]{2,1,0:T(8,128)(2,1)} %bitcast.12), calls=%async_computation.3 | async-start | bytes 786432 | tf_op jit(solution)/shard_map/all_to_all | solution.py:104
  280.1 3.7 %all-to-all-done.3 = bf16[16,48,224]{2,1,0:T(8,128)(2,1)} async-done(((bf16[16,48,224]{2,1,0:T(8,128)(2,1)}), bf16[16,48,224]{2,1,0:T(8,128)(2,1)}, u32[]{:S(2)}, u32[]{:S(2)}) %all-to-all-start.3) | async-done | bytes 344096 | tf_op jit(solution)/shard_map/all_to_all | solution.py:104
  283.8 4.0 %all-to-all-start.2 = ((bf16[16,48,224]{2,1,0:T(8,128)(2,1)}), bf16[16,48,224]{2,1,0:T(8,128)(2,1)S(1)}, u32[]{:S(2)}, u32[]{:S(2)}) async-start(bf16[16,48,224]{2,1,0:T(8,128)(2,1)} %bitcast.10), calls=%async_computation.2 | async-start | bytes 786432 | tf_op jit(solution)/shard_map/all_to_all | solution.py:103
  287.9 6.3 %collective-permute-start.3 = (bf16[16,48,224]{2,1,0:T(8,128)(2,1)}, bf16[16,48,224]{2,1,0:T(8,128)(2,1)}, u32[]{:S(2)}, u32[]{:S(2)}) collective-permute-start(bf16[16,48,224]{2,1,0:T(8,128)(2,1)} %all-to-all-done.3), channel_id=1, source_target_pairs={{0,64},{64,0},{1,65},{65,1},{2,66},{66,2},{3,67},{67,3},{4,68},{68... | collective-permute-start | bytes 1032200 | tf_op jit(solution)/shard_map/ppermute | solution.py:104
  296.4 30.6 %collective-permute-done.3 = bf16[16,48,224]{2,1,0:T(8,128)(2,1)} collective-permute-done((bf16[16,48,224]{2,1,0:T(8,128)(2,1)}, bf16[16,48,224]{2,1,0:T(8,128)(2,1)}, u32[]{:S(2)}, u32[]{:S(2)}) %collective-permute-start.3) | collective-permute-done | bytes 344096 | tf_op jit(solution)/shard_map/ppermute | solution.py:104
  328.2 3.9 %gather_fusion.2 = bf16[1024,224]{1,0:T(8,128)(2,1)S(1)} fusion(bf16[1536,224]{1,0:T(8,128)(2,1)S(1)} %bitcast.41, s32[1024]{0:T(1024)S(1)} %broadcast_clamp_fusion), kind=kCustom, calls=%fused_computation.2 | custom fusion | bytes 921600 | tf_op jit(solution)/shard_map/gather | solution.py:111
  (85 shorter events, 42.6 us)
Async XLA Ops:
  7.2 7.5 %copy-start = (bf16[128,3584]{1,0:T(8,128)(2,1)S(1)}, bf16[128,3584]{1,0:T(8,128)(2,1)}, u32[]{:S(2)}) copy-start(bf16[128,3584]{1,0:T(8,128)(2,1)} %param.6) | copy-start | bytes 2752516
  7.2 158.2 %all-gather.5.cloned.1.call-start = ((), (), s32[]{:S(2)}) async-start(), calls=%async_computation.4 | async-start | bytes 3538944 | tf_op jit(solution)/shard_map/all_gather | solution.py:77
  17.5 28.3 %collective-permute-start = (bf16[16,48,224]{2,1,0:T(8,128)(2,1)S(1)}, bf16[16,48,224]{2,1,0:T(8,128)(2,1)S(1)}, u32[]{:S(2)}, u32[]{:S(2)}) collective-permute-start(bf16[16,48,224]{2,1,0:T(8,128)(2,1)S(1)} %bitcast.50), channel_id=1, source_target_pairs={{0,64},{64,0},{1,65},{65,1},{2,66},{66,2},{3,67},{67,3},{4,68},{68... | collective-permute-start | bytes 1032200 | tf_op jit(solution)/shard_map/ppermute | solution.py:75
  66.0 38.6 %copy-start.1 = (bf16[1,1,1792,256]{3,2,1,0:T(8,128)(2,1)S(1)}, bf16[1,1,1792,256]{3,2,1,0:T(8,128)(2,1)}, u32[]{:S(2)}) copy-start(bf16[1,1,1792,256]{3,2,1,0:T(8,128)(2,1)} %param.9) | copy-start | bytes 2752516
  66.0 38.6 %all-to-all-start = ((bf16[16,48,1792]{2,1,0:T(8,128)(2,1)}), bf16[16,48,1792]{2,1,0:T(8,128)(2,1)}, u32[]{:S(2)}, u32[]{:S(2)}) async-start(bf16[16,48,1792]{2,1,0:T(8,128)(2,1)} %bitcast.43), calls=%async_computation | async-start | bytes 5505024 | tf_op jit(solution)/shard_map/all_to_all | solution.py:74
  70.6 160.7 %all-gather.7.cloned.1.call-start = ((), (), s32[]{:S(2)}) async-start(), calls=%async_computation.5 | async-start | bytes 1769472 | tf_op jit(solution)/shard_map/all_gather | solution.py:92
  168.2 5.0 %collective-permute-start.1 = (f32[768,256]{1,0:T(8,128)S(1)}, f32[768,256]{1,0:T(8,128)S(1)}, u32[]{:S(2)}, u32[]{:S(2)}) collective-permute-start(f32[768,256]{1,0:T(8,128)S(1)} %get-tuple-element.21), channel_id=1, source_target_pairs={{0,1},{1,0},{2,3},{3,2},{4,5},{5,4},{6,7},{7,6},{8,9},{9,8},{10,11... | collective-permute-start | bytes 2359304 | tf_op jit(solution)/shard_map/ppermute | solution.py:89
  174.3 9.9 %collective-permute-start.8 = (bf16[1,512,224]{1,2,0:T(8,128)(2,1)S(1)}, bf16[1,512,224]{1,2,0:T(8,128)(2,1)S(1)}, u32[]{:S(2)}, u32[]{:S(2)}) collective-permute-start(bf16[1,512,224]{1,2,0:T(8,128)(2,1)S(1)} %slice.22), channel_id=1, source_target_pairs={{0,16},{16,32},{32,48},{48,0},{1,17},{17,33},{33,49},{49,1},{2,18}... | collective-permute-start | bytes 688136 | tf_op jit(solution)/shard_map/ppermute | solution.py:23
  184.9 57.9 %collective-permute-start.10 = (bf16[1,512,224]{1,2,0:T(8,128)(2,1)S(1)}, bf16[1,512,224]{1,2,0:T(8,128)(2,1)S(1)}, u32[]{:S(2)}, u32[]{:S(2)}) collective-permute-start(bf16[1,512,224]{1,2,0:T(8,128)(2,1)S(1)} %get-tuple-element.18), channel_id=1, source_target_pairs={{0,48},{16,0},{32,16},{48,32},{1,49},{17,1},{33,17},{49,33},{2,50}... | collective-permute-start | bytes 688136 | tf_op jit(solution)/shard_map/ppermute | solution.py:24
  188.8 63.1 %copy-start.6 = (f32[128,8]{0,1:T(8,128)S(1)}, f32[128,8]{0,1:T(8,128)}, u32[]{:S(2)}) copy-start(f32[128,8]{0,1:T(8,128)} %param.8) | copy-start | bytes 12292
  188.8 58.1 %collective-permute-start.4 = (bf16[1,1,896,256]{3,2,1,0:T(8,128)(2,1)}, bf16[1,1,896,256]{3,2,1,0:T(8,128)(2,1)S(1)}, u32[]{:S(2)}, u32[]{:S(2)}) collective-permute-start(bf16[1,1,896,256]{3,2,1,0:T(8,128)(2,1)} %slice.20), channel_id=1, source_target_pairs={{0,16},{16,32},{32,48},{48,0},{1,17},{17,33},{33,49},{49,1},{2,18}... | collective-permute-start | bytes 1376264 | tf_op jit(solution)/shard_map/ppermute | solution.py:23
  231.3 36.4 %collective-permute-start.2 = (bf16[8,768,128]{2,1,0:T(8,128)(2,1)}, bf16[8,768,128]{2,1,0:T(8,128)(2,1)}, u32[]{:S(2)}, u32[]{:S(2)}) collective-permute-start(bf16[8,768,128]{2,1,0:T(8,128)(2,1)} %bitcast.53), channel_id=1, source_target_pairs={{0,1},{1,0},{2,3},{3,2},{4,5},{5,4},{6,7},{7,6},{8,9},{9,8},{10,11... | collective-permute-start | bytes 4718600 | tf_op jit(solution)/shard_map/ppermute | solution.py:93
  239.6 14.7 %collective-permute-start.9 = (bf16[1,512,224]{1,2,0:T(8,128)(2,1)}, bf16[1,512,224]{1,2,0:T(8,128)(2,1)}, u32[]{:S(2)}, u32[]{:S(2)}) collective-permute-start(bf16[1,512,224]{1,2,0:T(8,128)(2,1)} %get-tuple-element.17), channel_id=1, source_target_pairs={{0,16},{16,32},{32,48},{48,0},{1,17},{17,33},{33,49},{49,1},{2,18}... | collective-permute-start | bytes 688136 | tf_op jit(solution)/shard_map/ppermute | solution.py:32
  242.8 5.1 %copy-start.3 = (bf16[1,512,224]{1,2,0:T(8,128)(2,1)}, bf16[1,512,224]{1,2,0:T(8,128)(2,1)S(1)}, u32[]{:S(2)}) copy-start(bf16[1,512,224]{1,2,0:T(8,128)(2,1)S(1)} %collective-permute-done.10) | copy-start | bytes 688132
  243.5 10.8 %collective-permute-start.11 = (bf16[1,512,224]{1,2,0:T(8,128)(2,1)}, bf16[1,512,224]{1,2,0:T(8,128)(2,1)}, u32[]{:S(2)}, u32[]{:S(2)}) collective-permute-start(bf16[1,512,224]{1,2,0:T(8,128)(2,1)} %broadcast_select_fusion.5), channel_id=1, source_target_pairs={{0,48},{16,0},{32,16},{48,32},{1,49},{17,1},{33,17},{49,33},{2,50}... | collective-permute-start | bytes 688136 | tf_op jit(solution)/shard_map/ppermute | solution.py:33
  247.9 14.7 %collective-permute-start.6 = (bf16[1,1,896,256]{3,2,1,0:T(8,128)(2,1)}, bf16[1,1,896,256]{3,2,1,0:T(8,128)(2,1)S(1)}, u32[]{:S(2)}, u32[]{:S(2)}) collective-permute-start(bf16[1,1,896,256]{3,2,1,0:T(8,128)(2,1)} %get-tuple-element.14), channel_id=1, source_target_pairs={{0,48},{16,0},{32,16},{48,32},{1,49},{17,1},{33,17},{49,33},{2,50}... | collective-permute-start | bytes 1376264 | tf_op jit(solution)/shard_map/ppermute | solution.py:24
  252.0 15.7 %copy-start.4 = (bf16[28,8,8,128]{3,2,1,0:T(8,128)(2,1)S(1)}, bf16[28,8,8,128]{3,2,1,0:T(8,128)(2,1)}, u32[]{:S(2)}) copy-start(bf16[28,8,8,128]{3,2,1,0:T(8,128)(2,1)} %copy.50) | copy-start | bytes 1376260
  252.1 15.7 %copy-start.7 = (bf16[6144,128]{1,0:T(8,128)(2,1)S(1)}, bf16[6144,128]{1,0:T(8,128)(2,1)}, u32[]{:S(2)}) copy-start(bf16[6144,128]{1,0:T(8,128)(2,1)} %all-gather.7.cloned.1.call-done) | copy-start | bytes 4718596
  252.1 42.1 %collective-permute-start.5 = (bf16[1,1,896,256]{3,2,1,0:T(8,128)(2,1)}, bf16[1,1,896,256]{3,2,1,0:T(8,128)(2,1)}, u32[]{:S(2)}, u32[]{:S(2)}) collective-permute-start(bf16[1,1,896,256]{3,2,1,0:T(8,128)(2,1)} %get-tuple-element.13), channel_id=1, source_target_pairs={{0,16},{16,32},{32,48},{48,0},{1,17},{17,33},{33,49},{49,1},{2,18}... | collective-permute-start | bytes 1376264 | tf_op jit(solution)/shard_map/ppermute | solution.py:32
  263.5 30.7 %collective-permute-start.7 = (bf16[1,1,896,256]{3,2,1,0:T(8,128)(2,1)}, bf16[1,1,896,256]{3,2,1,0:T(8,128)(2,1)}, u32[]{:S(2)}, u32[]{:S(2)}) collective-permute-start(bf16[1,1,896,256]{3,2,1,0:T(8,128)(2,1)} %broadcast_select_fusion), channel_id=1, source_target_pairs={{0,48},{16,0},{32,16},{48,32},{1,49},{17,1},{33,17},{49,33},{2,50}... | collective-permute-start | bytes 1376264 | tf_op jit(solution)/shard_map/ppermute | solution.py:33
  267.8 7.6 %copy-start.5 = (bf16[28,8,8,128]{3,2,1,0:T(8,128)(2,1)S(1)}, bf16[28,8,8,128]{3,2,1,0:T(8,128)(2,1)}, u32[]{:S(2)}) copy-start(bf16[28,8,8,128]{3,2,1,0:T(8,128)(2,1)} %copy.50) | copy-start | bytes 1376260
  271.1 12.7 %all-to-all-start.3 = ((bf16[16,48,224]{2,1,0:T(8,128)(2,1)}), bf16[16,48,224]{2,1,0:T(8,128)(2,1)}, u32[]{:S(2)}, u32[]{:S(2)}) async-start(bf16[16,48,224]{2,1,0:T(8,128)(2,1)} %bitcast.12), calls=%async_computation.3 | async-start | bytes 786432 | tf_op jit(solution)/shard_map/all_to_all | solution.py:104
  283.8 12.6 %all-to-all-start.2 = ((bf16[16,48,224]{2,1,0:T(8,128)(2,1)}), bf16[16,48,224]{2,1,0:T(8,128)(2,1)S(1)}, u32[]{:S(2)}, u32[]{:S(2)}) async-start(bf16[16,48,224]{2,1,0:T(8,128)(2,1)} %bitcast.10), calls=%async_computation.2 | async-start | bytes 786432 | tf_op jit(solution)/shard_map/all_to_all | solution.py:103
  287.9 39.2 %collective-permute-start.3 = (bf16[16,48,224]{2,1,0:T(8,128)(2,1)}, bf16[16,48,224]{2,1,0:T(8,128)(2,1)}, u32[]{:S(2)}, u32[]{:S(2)}) collective-permute-start(bf16[16,48,224]{2,1,0:T(8,128)(2,1)} %all-to-all-done.3), channel_id=1, source_target_pairs={{0,64},{64,0},{1,65},{65,1},{2,66},{66,2},{3,67},{67,3},{4,68},{68... | collective-permute-start | bytes 1032200 | tf_op jit(solution)/shard_map/ppermute | solution.py:104
  (2 other events, 5.2 us)
Sparse Core Ops, SparseCore 0:
  61.8 103.5 all-gather.4
  174.3 56.9 all-gather.6

commit v3 on v2

v3 whole, which is shorter than its diff:
```python
import jax
import jax.numpy as jnp
from jax import lax
from jax.sharding import Mesh
from jax.sharding import PartitionSpec as P

EXPERT = ("y", "zhi", "x")
DP = ("zlo", "core")
FLIP = [(0, 1), (1, 0)]


def swap_panels(gate_up, down, partner):
    here = lax.axis_index(EXPERT)
    kind = jnp.bitwise_xor(partner[here], here)
    even = (lax.axis_index("x") & 1) == 0
    gate_rows = gate_up.shape[2] // 2
    down_rows = down.shape[1] // 2
    first = (gate_up[:, :, :gate_rows], down[:, :down_rows])
    second = (gate_up[:, :, gate_rows:], down[:, down_rows:])
    ring = lax.axis_size("x")
    ahead = [(i, (i + 1) % ring) for i in range(ring)]
    behind = [(i, (i + ring - 1) % ring) for i in range(ring)]
    from_behind = lax.ppermute(first, "x", ahead)
    from_ahead = lax.ppermute(second, "x", behind)
    is_two = kind == 2

    def pick(flag, left, right):
        return tuple(jnp.where(flag, l, r) for l, r in zip(left, right))

    send_ahead = pick(is_two, from_behind, second)
    send_behind = pick(is_two, from_ahead, first)
    got_behind = lax.ppermute(send_ahead, "x", ahead)
    got_ahead = lax.ppermute(send_behind, "x", behind)
    one_even = (kind == 1) & even
    one_odd = (kind == 1) & ~even
    new_first = pick(is_two, got_behind, pick(one_even, got_ahead, pick(one_odd, from_behind, first)))
    new_second = pick(is_two, got_ahead, pick(one_even, from_ahead, pick(one_odd, got_behind, second)))
    new_gate_up = jnp.concatenate([new_first[0], new_second[0]], axis=2)
    new_down = jnp.concatenate([new_first[1], new_second[1]], axis=1)
    return (new_gate_up, new_down)


def routing(expert_ids, expert_count, capacity):
    token_rows, top_count = expert_ids.shape
    labels = jnp.arange(expert_count, dtype=jnp.int32)
    onehot = (expert_ids[:, :, None] == labels[None, None, :]).astype(jnp.int32)
    picked = jnp.sum(onehot, axis=1)
    slot_rank = jnp.cumsum(picked, axis=0) - picked
    slots = jnp.sum(onehot * slot_rank[:, None, :], axis=2)
    place = (expert_ids * capacity + slots).reshape(-1)
    row_ids = jnp.repeat(jnp.arange(token_rows, dtype=jnp.int32), top_count)
    source = jnp.full((expert_count * capacity,), token_rows, jnp.int32).at[place].set(row_ids)
    return slots, source


def combine(table, expert_ids, slots, weights, zhi, rows_x, capacity):
    in_half = (expert_ids // rows_x) % 2 == zhi
    line = (expert_ids // (2 * rows_x)) * rows_x + expert_ids % rows_x
    blank = table.shape[0]
    index = jnp.where(in_half, line * capacity + slots, blank)
    padded = jnp.concatenate([table, jnp.zeros((1, table.shape[1]), table.dtype)], axis=0)
    chosen = padded[index.reshape(-1)].reshape(index.shape + (table.shape[1],))
    return jnp.sum(chosen.astype(jnp.float32) * weights[:, :, None], axis=1)


def run_layer(tokens, expert_ids, route_weights, gate_up, down):
    rows_y, rows_x = lax.axis_size("y"), lax.axis_size("x")
    lines = rows_y * rows_x
    expert_count = 2 * lines
    chunks = lax.axis_size("zlo")
    token_rows, model_width = tokens.shape
    top_count = expert_ids.shape[1]
    capacity = min(token_rows, 3 * token_rows * top_count // (2 * expert_count))
    half_width = model_width // 2
    side = lax.axis_index("core")
    zhi = lax.axis_index("zhi")
    own_half = lax.dynamic_slice_in_dim(tokens, side * half_width, half_width, 1)
    far_half, far_ids, far_weights = lax.ppermute((own_half, expert_ids, route_weights), "zhi", FLIP)
    own_slots, own_source = routing(expert_ids, expert_count, capacity)
    far_slots, far_source = routing(far_ids, expert_count, capacity)

    def outgoing(rows, source):
        near = lax.dynamic_index_in_dim(source.reshape(rows_y, 2, rows_x, capacity), zhi, 1, keepdims=False)
        padded = jnp.concatenate([rows, jnp.zeros((1, half_width), rows.dtype)], axis=0)
        return padded[near.reshape(-1)].reshape(lines, 1, capacity, half_width)

    sent = jnp.concatenate([outgoing(own_half, own_source), outgoing(far_half, far_source)], axis=1)
    arrived = lax.all_to_all(sent, ("y", "x"), 0, 0, tiled=True)
    total_rows = lines * 2 * capacity
    half_rows = total_rows // 2
    partial_value = jnp.dot(arrived.reshape(total_rows, half_width), gate_up, preferred_element_type=jnp.float32)
    mine = lax.dynamic_slice_in_dim(partial_value, side * half_rows, half_rows, 0)
    other = lax.dynamic_slice_in_dim(partial_value, (1 - side) * half_rows, half_rows, 0)
    summed = mine + lax.ppermute(other, "core", FLIP)
    block_units = gate_up.shape[1] // 2
    hidden = (jax.nn.silu(summed[:, :block_units]) * summed[:, block_units:]).astype(jnp.bfloat16)
    gathered = lax.all_gather(hidden, "zlo", axis=0, tiled=False)
    partner_part = lax.ppermute(gathered, "core", FLIP)
    keep_first = side == 0
    first_hidden = jnp.where(keep_first, gathered, partner_part)
    second_hidden = jnp.where(keep_first, partner_part, gathered)
    out_columns = down.shape[1]
    down_blocks = down.reshape(chunks, block_units, out_columns)

    def project(hidden_part):
        value = jnp.einsum("qrk,qkc->rc", hidden_part, down_blocks, preferred_element_type=jnp.float32)
        return value.astype(jnp.bfloat16)

    expert_out = jnp.concatenate([project(first_hidden), project(second_hidden)], axis=0)
    returned = lax.all_to_all(expert_out.reshape(lines, 2, capacity, out_columns), ("y", "x"), 0, 0, tiled=True)
    own_table = returned[:, 0].reshape(lines * capacity, out_columns)
    far_table = returned[:, 1].reshape(lines * capacity, out_columns)
    far_sum = combine(far_table, far_ids, far_slots, far_weights, zhi, rows_x, capacity)
    own_sum = combine(own_table, expert_ids, own_slots, route_weights, zhi, rows_x, capacity)
    mixed = own_sum + lax.ppermute(far_sum, "zhi", FLIP)
    return mixed.astype(jnp.bfloat16)


def per_device(tokens, expert_ids, route_weights, gate_up_panels, down_panels, partner):
    moe_out = run_layer(tokens, expert_ids, route_weights, gate_up_panels[0, 0], down_panels[0])
    new_gate_up, new_down = swap_panels(gate_up_panels, down_panels, partner)
    return (moe_out, new_gate_up, new_down)


def solution(mesh):
    experts, dps = mesh.devices.shape
    layout = mesh.devices.reshape(experts // 8, 2, 4, dps // 2, 2)
    split = Mesh(layout, EXPERT + DP)
    return jax.shard_map(
        per_device,
        mesh=split,
        in_specs=(
            P(EXPERT, None),
            P(EXPERT, None),
            P(EXPERT, None),
            P(EXPERT, DP, None, None),
            P(EXPERT, None, DP),
            P(),
        ),
        out_specs=(P(EXPERT, DP), P(EXPERT, DP, None, None), P(EXPERT, None, DP)),
        check_vma=False,
    )
```

time: 341 us -> 333 us (0.977)
  waiting for transfers between devices: 192 us -> 175 us
  blocking collectives: 15.9 us -> 0 us
  local copies, waits for them, and re-layouts: 22.9 us -> 34.2 us
  starting transfers between devices: 71.5 us -> 80.3 us
  other arithmetic: 12.7 us -> 19.4 us
    all_gather x1 -> x0, waiting for transfers between devices: 58.1 us -> none  [run_layer(): far_full = lax.all_gather(far_in, 'zlo', axis=0, tiled=False)]
    all_to_all x3 -> x2, waiting for transfers between devices: 37.6 us -> 86.4 us  [the longest x1 77.9 us: run_layer(): arrived = lax.all_to_all(sent, ('y', 'x'), 0, 0, tiled=True)]
    ppermute x2 -> x4, waiting for transfers between devices: 42.6 us -> 15.8 us  [the longest x1 8.33 us: run_layer(): mixed = own_sum + lax.ppermute(far_sum, 'zhi', FLIP)]
    all_gather x1, waiting for transfers between devices: 40.2 us -> 63 us  [run_layer(): gathered = lax.all_gather(hidden, 'zlo', axis=0, tiled=False)]
    all_to_all x1 -> x0, blocking collectives: 15.9 us -> none  [run_layer(): far_in = lax.all_to_all(far_mid, ('y', 'x'), 0, 0, tiled=True)]
    ppermute x2 -> x4, starting transfers between devices: 22.5 us -> 30.3 us  [the longest x3 24.5 us: run_layer(): lax.ppermute((own_half, expert_ids, route_weights), 'zhi', FLIP)]
    concatenate x0 -> x2, other arithmetic: none -> 5.56 us  [the longest x1 5.51 us: run_layer(): jnp.concatenate([outgoing(own_half, own_source), outgoing(far_half, far_s...]
    ppermute x2, waiting for transfers between devices: 5.53 us -> 0.01 us  [swap_panels(): from_behind = lax.ppermute(first, 'x', ahead)]
  transfers between devices with their start and end apart: 17 -> 17, of which waited for: 9 -> 7; matrix products, arithmetic and copies ran while one was open for 7% -> 11% of each run, Pallas kernels for 0% -> 0%
where the time goes in v3:
time: 333 us; the launch traced here: 332 us
  waiting for transfers between devices  175 us (53%)
  starting transfers between devices  80.3 us (24%)
  local copies, waits for them, and re-layouts  34.2 us (10%)
  other arithmetic  19.4 us (6%)
  between operations  15.3 us (5%)
  matrix products  8.07 us (2%)
    all_to_all x1, waiting for transfers between devices, run_layer(): arrived = lax.all_to_all(sent, ('y', 'x'), 0, 0, tiled=True)  77.9 us
    all_gather x1, waiting for transfers between devices, run_layer(): gathered = lax.all_gather(hidden, 'zlo', axis=0, tiled=False)  63 us
    ppermute x3, starting transfers between devices, run_layer(): lax.ppermute((own_half, expert_ids, route_weights), 'zhi', FLIP)  24.5 us
    scatter x2, local copies, waits for them, and re-layouts, routing(): jnp.full((expert_count * capacity,), token_rows, jnp.int32).at[place]  8.63 us
    all_to_all x1, waiting for transfers between devices, run_layer(): lax.all_to_all(expert_out.reshape(lines, 2, capacity, out_columns), ('y',...  8.51 us
    ppermute x1, waiting for transfers between devices, run_layer(): mixed = own_sum + lax.ppermute(far_sum, 'zhi', FLIP)  8.33 us
    ppermute x1, starting transfers between devices, run_layer(): partner_part = lax.ppermute(gathered, 'core', FLIP)  8.3 us
    gather x2, local copies, waits for them, and re-layouts, outgoing(): return padded[near.reshape(-1)].reshape(lines, 1, capacity, half_width)  8.2 us
  transfers between devices with their start and end apart: 17, of which 7 were waited for; matrix products, arithmetic and copies ran while one was open for 11% of the time, Pallas kernels for 0%

profile of v3, /device:TPU:1, one launch (start us, length us, event | category | flops | bytes accessed | tf_op | source)
XLA Modules:
  0.0 332.1 jit_solution(14493302000355538173)
XLA Ops:
  7.2 16.4 %collective-permute-start.1 = (s32[128,8]{0,1:T(8,128)}, s32[128,8]{0,1:T(8,128)S(1)}, u32[]{:S(2)}, u32[]{:S(2)}) collective-permute-start(s32[128,8]{0,1:T(8,128)} %param.7), channel_id=1, source_target_pairs={{0,64},{64,0},{1,65},{65,1},{2,66},{66,2},{3,67},{67,3},{4,68},{68... | collective-permute-start | bytes 12296 | tf_op jit(solution)/shard_map/ppermute | solution.py:78
  28.4 4.3 %scatter_custom_fusion = s32[1536]{0:T(1024)S(1)} fusion(s32[1024]{0:T(1024)S(1)} %bitcast.48, s32[1024]{0:T(1024)S(1)} %reshape.305, s32[]{:T(128)} %constant.114.clone.1), kind=kCustom, calls=%fused_computation.102 | custom fusion | bytes 6148 | tf_op jit(solution)/shard_map/scatter | solution.py:52
  33.5 4.3 %scatter_custom_fusion.1 = s32[1536]{0:T(1024)S(1)} fusion(s32[1024]{0:T(1024)S(1)} %bitcast.49, s32[1024]{0:T(1024)S(1)} %reshape.305, s32[]{:T(128)} %constant.114.clone.1), kind=kCustom, calls=%fused_computation.100 | custom fusion | bytes 6148 | tf_op jit(solution)/shard_map/scatter | solution.py:52
  38.2 4.1 %gather_fusion = bf16[768,1792]{1,0:T(8,128)(2,1)} fusion(bf16[129,1792]{1,0:T(8,128)(2,1)S(1)} %concatenate.24, s32[1024]{0:T(1024)S(1)} %pad_clamp_fusion.1), kind=kCustom, calls=%fused_computation | custom fusion | bytes 5508096 | tf_op jit(solution)/shard_map/gather | solution.py:85
  42.3 7.5 %collective-permute-done = bf16[128,1792]{1,0:T(8,128)(2,1)S(1)} collective-permute-done((bf16[128,1792]{1,0:T(8,128)(2,1)S(1)}, bf16[128,1792]{1,0:T(8,128)(2,1)S(1)}, u32[]{:S(2)}, u32[]{:S(2)}) %collective-permute-start) | collective-permute-done | bytes 458784 | tf_op jit(solution)/shard_map/ppermute | solution.py:78
  49.9 4.1 %gather_fusion.1 = bf16[768,1792]{1,0:T(8,128)(2,1)} fusion(bf16[129,1792]{1,0:T(8,128)(2,1)S(1)} %concatenate.25, s32[1024]{0:T(1024)S(1)} %pad_clamp_fusion), kind=kCustom, calls=%fused_computation.1 | custom fusion | bytes 5508096 | tf_op jit(solution)/shard_map/gather | solution.py:85
  53.9 5.5 %pad_maximum_fusion = bf16[16,2,48,1792]{3,2,1,0:T(8,128)(2,1)} fusion(bf16[16,1,48,1792]{3,2,1,0:T(8,128)(2,1)} %bitcast.40, bf16[16,1,48,1792]{3,2,1,0:T(8,128)(2,1)} %bitcast.39), kind=kLoop, calls=%fused_computation.6 | loop fusion | flops 2752512 | bytes 11010048 | tf_op jit(solution)/shard_map/concatenate | solution.py:87
  59.4 6.9 %all-to-all-start = ((bf16[16,2,48,1792]{3,2,1,0:T(8,128)(2,1)}), bf16[16,2,48,1792]{3,2,1,0:T(8,128)(2,1)}, u32[]{:S(2)}, u32[]{:S(2)}) async-start(bf16[16,2,48,1792]{3,2,1,0:T(8,128)(2,1)} %pad_maximum_fusion), calls=%async_computation | async-start | bytes 11010048 | tf_op jit(solution)/shard_map/all_to_all | solution.py:88
  66.4 77.9 %all-to-all-done = bf16[16,2,48,1792]{3,2,1,0:T(8,128)(2,1)} async-done(((bf16[16,2,48,1792]{3,2,1,0:T(8,128)(2,1)}), bf16[16,2,48,1792]{3,2,1,0:T(8,128)(2,1)}, u32[]{:S(2)}, u32[]{:S(2)}) %all-to-all-start) | async-done | bytes 5505056 | tf_op jit(solution)/shard_map/all_to_all | solution.py:88
  144.4 5.3 %fusion.20 = f32[1536,256]{1,0:T(8,128)} fusion(bf16[1536,1792]{1,0:T(8,128)(2,1)} %bitcast.6, bf16[1,1,1792,256]{3,2,1,0:T(8,128)(2,1)S(1)} %copy-done.1), kind=kOutput, calls=%fused_computation.22 | convolution fusion | flops 1409286144 | bytes 7995392 | tf_op jit(solution)/shard_map/dot_general | solution.py:91
  151.8 5.2 %collective-permute-start.2 = (f32[768,256]{1,0:T(8,128)}, f32[768,256]{1,0:T(8,128)S(1)}, u32[]{:S(2)}, u32[]{:S(2)}) collective-permute-start(f32[768,256]{1,0:T(8,128)} %constant_dynamic-slice_fusion), channel_id=1, source_target_pairs={{0,1},{1,0},{2,3},{3,2},{4,5},{5,4},{6,7},{7,6},{8,9},{9,8},{10,11... | collective-permute-start | bytes 2359304 | tf_op jit(solution)/shard_map/ppermute | solution.py:94
  163.1 6.2 %collective-permute-start.4 = (f32[128,8]{0,1:T(8,128)S(1)}, f32[128,8]{0,1:T(8,128)S(1)}, u32[]{:S(2)}, u32[]{:S(2)}) collective-permute-start(f32[128,8]{0,1:T(8,128)S(1)} %copy-done.7), channel_id=1, source_target_pairs={{0,64},{64,0},{1,65},{65,1},{2,66},{66,2},{3,67},{67,3},{4,68},{68... | collective-permute-start | bytes 12296 | tf_op jit(solution)/shard_map/ppermute | solution.py:78
  174.3 4.6 %collective-permute-start.12 = (bf16[1,512,224]{1,2,0:T(8,128)(2,1)S(1)}, bf16[1,512,224]{1,2,0:T(8,128)(2,1)S(1)}, u32[]{:S(2)}, u32[]{:S(2)}) collective-permute-start(bf16[1,512,224]{1,2,0:T(8,128)(2,1)S(1)} %get-tuple-element.18), channel_id=1, source_target_pairs={{0,48},{16,0},{32,16},{48,32},{1,49},{17,1},{33,17},{49,33},{2,50}... | collective-permute-start | bytes 688136 | tf_op jit(solution)/shard_map/ppermute | solution.py:24
  178.9 63.0 %all-gather.3.cloned.1.call-done = bf16[6144,128]{1,0:T(8,128)(2,1)} async-done(((bf16[768,128]{1,0:T(8,128)(2,1)}), bf16[6144,128]{1,0:T(8,128)(2,1)}) %all-gather.3.cloned.1.call-update) | async-done | bytes 1572880 | tf_op jit(solution)/shard_map/all_gather | solution.py:97
  241.9 8.3 %collective-permute-start.3 = (bf16[8,768,128]{2,1,0:T(8,128)(2,1)}, bf16[8,768,128]{2,1,0:T(8,128)(2,1)}, u32[]{:S(2)}, u32[]{:S(2)}) collective-permute-start(bf16[8,768,128]{2,1,0:T(8,128)(2,1)} %bitcast.50), channel_id=1, source_target_pairs={{0,1},{1,0},{2,3},{3,2},{4,5},{5,4},{6,7},{7,6},{8,9},{9,8},{10,11... | collective-permute-start | bytes 4718600 | tf_op jit(solution)/shard_map/ppermute | solution.py:98
  256.0 3.3 collective-permute-start.13
  267.3 7.4 %collective-permute-done.8 = bf16[1,1,896,256]{3,2,1,0:T(8,128)(2,1)S(1)} collective-permute-done((bf16[1,1,896,256]{3,2,1,0:T(8,128)(2,1)S(1)}, bf16[1,1,896,256]{3,2,1,0:T(8,128)(2,1)S(1)}, u32[]{:S(2)}, u32[]{:S(2)}) %collective-permute-start.8) | collective-permute-done | bytes 458784 | tf_op jit(solution)/shard_map/ppermute | solution.py:24
  275.6 4.3 %collective-permute-start.9 = (bf16[1,1,896,256]{3,2,1,0:T(8,128)(2,1)}, bf16[1,1,896,256]{3,2,1,0:T(8,128)(2,1)}, u32[]{:S(2)}, u32[]{:S(2)}) collective-permute-start(bf16[1,1,896,256]{3,2,1,0:T(8,128)(2,1)} %broadcast_select_fusion), channel_id=1, source_target_pairs={{0,48},{16,0},{32,16},{48,32},{1,49},{17,1},{33,17},{49,33},{2,50}... | collective-permute-start | bytes 1376264 | tf_op jit(solution)/shard_map/ppermute | solution.py:33
  283.9 4.9 %all-to-all-start.1 = ((bf16[16,2,48,224]{3,2,1,0:T(8,128)(2,1)}), bf16[16,2,48,224]{3,2,1,0:T(8,128)(2,1)S(1)}, u32[]{:S(2)}, u32[]{:S(2)}) async-start(bf16[16,2,48,224]{3,2,1,0:T(8,128)(2,1)} %bitcast.11), calls=%async_computation.1 | async-start | bytes 1572864 | tf_op jit(solution)/shard_map/all_to_all | solution.py:110
  292.9 8.5 %all-to-all-done.1 = bf16[16,2,48,224]{3,2,1,0:T(8,128)(2,1)S(1)} async-done(((bf16[16,2,48,224]{3,2,1,0:T(8,128)(2,1)}), bf16[16,2,48,224]{3,2,1,0:T(8,128)(2,1)S(1)}, u32[]{:S(2)}, u32[]{:S(2)}) %all-to-all-start.1) | async-done | bytes 688160 | tf_op jit(solution)/shard_map/all_to_all | solution.py:110
  301.6 3.9 %gather_fusion.3 = bf16[1024,224]{1,0:T(8,128)(2,1)S(1)} fusion(bf16[769,224]{1,0:T(8,128)(2,1)S(1)} %concatenate.29, s32[1024]{0:T(1024)S(1)} %broadcast_clamp_fusion), kind=kCustom, calls=%fused_computation.3 | custom fusion | bytes 921600 | tf_op jit(solution)/shard_map/gather | solution.py:62
  305.9 5.8 %collective-permute-start.5 = (f32[128,224]{1,0:T(8,128)S(1)}, f32[128,224]{1,0:T(8,128)S(1)}, u32[]{:S(2)}, u32[]{:S(2)}) collective-permute-start(f32[128,224]{1,0:T(8,128)S(1)} %fusion.18), channel_id=1, source_target_pairs={{0,64},{64,0},{1,65},{65,1},{2,66},{66,2},{3,67},{67,3},{4,68},{68... | collective-permute-start | bytes 344072 | tf_op jit(solution)/shard_map/ppermute | solution.py:115
  311.8 3.9 %gather_fusion.2 = bf16[1024,224]{1,0:T(8,128)(2,1)S(1)} fusion(bf16[769,224]{1,0:T(8,128)(2,1)S(1)} %concatenate.28, s32[1024]{0:T(1024)S(1)} %broadcast_clamp_fusion.1), kind=kCustom, calls=%fused_computation.2 | custom fusion | bytes 921600 | tf_op jit(solution)/shard_map/gather | solution.py:62
  316.2 8.3 %collective-permute-done.5 = f32[128,224]{1,0:T(8,128)S(1)} collective-permute-done((f32[128,224]{1,0:T(8,128)S(1)}, f32[128,224]{1,0:T(8,128)S(1)}, u32[]{:S(2)}, u32[]{:S(2)}) %collective-permute-start.5) | collective-permute-done | bytes 114720 | tf_op jit(solution)/shard_map/ppermute | solution.py:115
  (109 shorter events, 42.7 us)
Async XLA Ops:
  7.2 16.4 %copy-start = (bf16[128,3584]{1,0:T(8,128)(2,1)S(1)}, bf16[128,3584]{1,0:T(8,128)(2,1)}, u32[]{:S(2)}) copy-start(bf16[128,3584]{1,0:T(8,128)(2,1)} %param.6) | copy-start | bytes 2752516
  7.2 25.7 %collective-permute-start.1 = (s32[128,8]{0,1:T(8,128)}, s32[128,8]{0,1:T(8,128)S(1)}, u32[]{:S(2)}, u32[]{:S(2)}) collective-permute-start(s32[128,8]{0,1:T(8,128)} %param.7), channel_id=1, source_target_pairs={{0,64},{64,0},{1,65},{65,1},{2,66},{66,2},{3,67},{67,3},{4,68},{68... | collective-permute-start | bytes 12296 | tf_op jit(solution)/shard_map/ppermute | solution.py:78
  23.6 26.2 %collective-permute-start = (bf16[128,1792]{1,0:T(8,128)(2,1)S(1)}, bf16[128,1792]{1,0:T(8,128)(2,1)S(1)}, u32[]{:S(2)}, u32[]{:S(2)}) collective-permute-start(bf16[128,1792]{1,0:T(8,128)(2,1)S(1)} %constant_dynamic-slice_fusion.3), channel_id=1, source_target_pairs={{0,64},{64,0},{1,65},{65,1},{2,66},{66,2},{3,67},{67,3},{4,68},{68... | collective-permute-start | bytes 1376264 | tf_op jit(solution)/shard_map/ppermute | solution.py:78
  59.4 84.9 %copy-start.1 = (bf16[1,1,1792,256]{3,2,1,0:T(8,128)(2,1)S(1)}, bf16[1,1,1792,256]{3,2,1,0:T(8,128)(2,1)}, u32[]{:S(2)}) copy-start(bf16[1,1,1792,256]{3,2,1,0:T(8,128)(2,1)} %param.9) | copy-start | bytes 2752516
  59.4 84.9 %all-to-all-start = ((bf16[16,2,48,1792]{3,2,1,0:T(8,128)(2,1)}), bf16[16,2,48,1792]{3,2,1,0:T(8,128)(2,1)}, u32[]{:S(2)}, u32[]{:S(2)}) async-start(bf16[16,2,48,1792]{3,2,1,0:T(8,128)(2,1)} %pad_maximum_fusion), calls=%async_computation | async-start | bytes 11010048 | tf_op jit(solution)/shard_map/all_to_all | solution.py:88
  66.4 175.5 %all-gather.3.cloned.1.call-start = ((), (), s32[]{:S(2)}) async-start(), calls=%async_computation.2 | async-start | bytes 1769472 | tf_op jit(solution)/shard_map/all_gather | solution.py:97
  151.7 9.4 %copy-start.2 = (bf16[1,1024,224]{1,2,0:T(8,128)(2,1)S(1)}, bf16[1,1024,224]{1,2,0:T(8,128)(2,1)}, u32[]{:S(2)}) copy-start(bf16[1,1024,224]{1,2,0:T(8,128)(2,1)} %param.10) | copy-start | bytes 1376260
  151.8 7.3 %collective-permute-start.2 = (f32[768,256]{1,0:T(8,128)}, f32[768,256]{1,0:T(8,128)S(1)}, u32[]{:S(2)}, u32[]{:S(2)}) collective-permute-start(f32[768,256]{1,0:T(8,128)} %constant_dynamic-slice_fusion), channel_id=1, source_target_pairs={{0,1},{1,0},{2,3},{3,2},{4,5},{5,4},{6,7},{7,6},{8,9},{9,8},{10,11... | collective-permute-start | bytes 2359304 | tf_op jit(solution)/shard_map/ppermute | solution.py:94
  157.0 6.1 %copy-start.7 = (f32[128,8]{0,1:T(8,128)S(1)}, f32[128,8]{0,1:T(8,128)}, u32[]{:S(2)}) copy-start(f32[128,8]{0,1:T(8,128)} %param.8) | copy-start | bytes 12292
  160.3 12.0 %copy-start.9 = (s32[32]{0:T(128)S(1)}, s32[32]{0:T(128)}, u32[]{:S(2)}) copy-start(s32[32]{0:T(128)} %param.11) | copy-start | bytes 388
  161.2 12.4 %collective-permute-start.10 = (bf16[1,512,224]{1,2,0:T(8,128)(2,1)S(1)}, bf16[1,512,224]{1,2,0:T(8,128)(2,1)S(1)}, u32[]{:S(2)}, u32[]{:S(2)}) collective-permute-start(bf16[1,512,224]{1,2,0:T(8,128)(2,1)S(1)} %slice.30), channel_id=1, source_target_pairs={{0,16},{16,32},{32,48},{48,0},{1,17},{17,33},{33,49},{49,1},{2,18}... | collective-permute-start | bytes 688136 | tf_op jit(solution)/shard_map/ppermute | solution.py:23
  163.1 88.8 %collective-permute-start.4 = (f32[128,8]{0,1:T(8,128)S(1)}, f32[128,8]{0,1:T(8,128)S(1)}, u32[]{:S(2)}, u32[]{:S(2)}) collective-permute-start(f32[128,8]{0,1:T(8,128)S(1)} %copy-done.7), channel_id=1, source_target_pairs={{0,64},{64,0},{1,65},{65,1},{2,66},{66,2},{3,67},{67,3},{4,68},{68... | collective-permute-start | bytes 12296 | tf_op jit(solution)/shard_map/ppermute | solution.py:78
  170.2 89.1 %collective-permute-start.6 = (bf16[1,1,896,256]{3,2,1,0:T(8,128)(2,1)}, bf16[1,1,896,256]{3,2,1,0:T(8,128)(2,1)S(1)}, u32[]{:S(2)}, u32[]{:S(2)}) collective-permute-start(bf16[1,1,896,256]{3,2,1,0:T(8,128)(2,1)} %slice.28), channel_id=1, source_target_pairs={{0,16},{16,32},{32,48},{48,0},{1,17},{17,33},{33,49},{49,1},{2,18}... | collective-permute-start | bytes 1376264 | tf_op jit(solution)/shard_map/ppermute | solution.py:23
  174.3 81.6 %collective-permute-start.12 = (bf16[1,512,224]{1,2,0:T(8,128)(2,1)S(1)}, bf16[1,512,224]{1,2,0:T(8,128)(2,1)S(1)}, u32[]{:S(2)}, u32[]{:S(2)}) collective-permute-start(bf16[1,512,224]{1,2,0:T(8,128)(2,1)S(1)} %get-tuple-element.18), channel_id=1, source_target_pairs={{0,48},{16,0},{32,16},{48,32},{1,49},{17,1},{33,17},{49,33},{2,50}... | collective-permute-start | bytes 688136 | tf_op jit(solution)/shard_map/ppermute | solution.py:24
  241.9 38.0 %collective-permute-start.3 = (bf16[8,768,128]{2,1,0:T(8,128)(2,1)}, bf16[8,768,128]{2,1,0:T(8,128)(2,1)}, u32[]{:S(2)}, u32[]{:S(2)}) collective-permute-start(bf16[8,768,128]{2,1,0:T(8,128)(2,1)} %bitcast.50), channel_id=1, source_target_pairs={{0,1},{1,0},{2,3},{3,2},{4,5},{5,4},{6,7},{7,6},{8,9},{9,8},{10,11... | collective-permute-start | bytes 4718600 | tf_op jit(solution)/shard_map/ppermute | solution.py:98
  252.7 12.8 %collective-permute-start.11 = (bf16[1,512,224]{1,2,0:T(8,128)(2,1)}, bf16[1,512,224]{1,2,0:T(8,128)(2,1)S(1)}, u32[]{:S(2)}, u32[]{:S(2)}) collective-permute-start(bf16[1,512,224]{1,2,0:T(8,128)(2,1)} %get-tuple-element.17), channel_id=1, source_target_pairs={{0,16},{16,32},{32,48},{48,0},{1,17},{17,33},{33,49},{49,1},{2,18}... | collective-permute-start | bytes 688136 | tf_op jit(solution)/shard_map/ppermute | solution.py:32
  256.0 9.6 %collective-permute-start.13 = (bf16[1,512,224]{1,2,0:T(8,128)(2,1)S(1)}, bf16[1,512,224]{1,2,0:T(8,128)(2,1)S(1)}, u32[]{:S(2)}, u32[]{:S(2)}) collective-permute-start(bf16[1,512,224]{1,2,0:T(8,128)(2,1)S(1)} %broadcast_select_fusion.2), channel_id=1, source_target_pairs={{0,48},{16,0},{32,16},{48,32},{1,49},{17,1},{33,17},{49,33},{2,50}... | collective-permute-start | bytes 688136 | tf_op jit(solution)/shard_map/ppermute | solution.py:33
  260.1 19.8 %copy-start.4 = (bf16[28,8,8,128]{3,2,1,0:T(8,128)(2,1)S(1)}, bf16[28,8,8,128]{3,2,1,0:T(8,128)(2,1)}, u32[]{:S(2)}) copy-start(bf16[28,8,8,128]{3,2,1,0:T(8,128)(2,1)} %copy.75) | copy-start | bytes 1376260
  260.1 19.8 %copy-start.8 = (bf16[6144,128]{1,0:T(8,128)(2,1)S(1)}, bf16[6144,128]{1,0:T(8,128)(2,1)}, u32[]{:S(2)}) copy-start(bf16[6144,128]{1,0:T(8,128)(2,1)} %all-gather.3.cloned.1.call-done) | copy-start | bytes 4718596
  260.1 14.7 %collective-permute-start.8 = (bf16[1,1,896,256]{3,2,1,0:T(8,128)(2,1)S(1)}, bf16[1,1,896,256]{3,2,1,0:T(8,128)(2,1)S(1)}, u32[]{:S(2)}, u32[]{:S(2)}) collective-permute-start(bf16[1,1,896,256]{3,2,1,0:T(8,128)(2,1)S(1)} %get-tuple-element.14), channel_id=1, source_target_pairs={{0,48},{16,0},{32,16},{48,32},{1,49},{17,1},{33,17},{49,33},{2,50}... | collective-permute-start | bytes 1376264 | tf_op jit(solution)/shard_map/ppermute | solution.py:24
  263.3 27.4 %collective-permute-start.7 = (bf16[1,1,896,256]{3,2,1,0:T(8,128)(2,1)}, bf16[1,1,896,256]{3,2,1,0:T(8,128)(2,1)}, u32[]{:S(2)}, u32[]{:S(2)}) collective-permute-start(bf16[1,1,896,256]{3,2,1,0:T(8,128)(2,1)} %get-tuple-element.13), channel_id=1, source_target_pairs={{0,16},{16,32},{32,48},{48,0},{1,17},{17,33},{33,49},{49,1},{2,18}... | collective-permute-start | bytes 1376264 | tf_op jit(solution)/shard_map/ppermute | solution.py:32
  275.6 15.1 %collective-permute-start.9 = (bf16[1,1,896,256]{3,2,1,0:T(8,128)(2,1)}, bf16[1,1,896,256]{3,2,1,0:T(8,128)(2,1)}, u32[]{:S(2)}, u32[]{:S(2)}) collective-permute-start(bf16[1,1,896,256]{3,2,1,0:T(8,128)(2,1)} %broadcast_select_fusion), channel_id=1, source_target_pairs={{0,48},{16,0},{32,16},{48,32},{1,49},{17,1},{33,17},{49,33},{2,50}... | collective-permute-start | bytes 1376264 | tf_op jit(solution)/shard_map/ppermute | solution.py:33
  283.9 17.6 %all-to-all-start.1 = ((bf16[16,2,48,224]{3,2,1,0:T(8,128)(2,1)}), bf16[16,2,48,224]{3,2,1,0:T(8,128)(2,1)S(1)}, u32[]{:S(2)}, u32[]{:S(2)}) async-start(bf16[16,2,48,224]{3,2,1,0:T(8,128)(2,1)} %bitcast.11), calls=%async_computation.1 | async-start | bytes 1572864 | tf_op jit(solution)/shard_map/all_to_all | solution.py:110
  305.9 18.5 %collective-permute-start.5 = (f32[128,224]{1,0:T(8,128)S(1)}, f32[128,224]{1,0:T(8,128)S(1)}, u32[]{:S(2)}, u32[]{:S(2)}) collective-permute-start(f32[128,224]{1,0:T(8,128)S(1)} %fusion.18), channel_id=1, source_target_pairs={{0,64},{64,0},{1,65},{65,1},{2,66},{66,2},{3,67},{67,3},{4,68},{68... | collective-permute-start | bytes 344072 | tf_op jit(solution)/shard_map/ppermute | solution.py:115
  (3 other events, 12.1 us)
Sparse Core Ops, SparseCore 0:
  161.3 80.5 all-gather.2

commit v4 on v3

--- a/solution.py
+++ b/solution.py
@@ -75,50 +75,55 @@
     side = lax.axis_index("core")
     zhi = lax.axis_index("zhi")
     own_half = lax.dynamic_slice_in_dim(tokens, side * half_width, half_width, 1)
-    far_half, far_ids, far_weights = lax.ppermute((own_half, expert_ids, route_weights), "zhi", FLIP)
+    mirror = [(high * chunks + low, (1 - high) * chunks + chunks - 1 - low) for high in range(2) for low in range(chunks)]
+    far_half, far_ids, far_weights = lax.ppermute((own_half, expert_ids, route_weights), ("zhi", "zlo"), mirror)
     own_slots, own_source = routing(expert_ids, expert_count, capacity)
     far_slots, far_source = routing(far_ids, expert_count, capacity)
-
-    def outgoing(rows, source):
-        near = lax.dynamic_index_in_dim(source.reshape(rows_y, 2, rows_x, capacity), zhi, 1, keepdims=False)
-        padded = jnp.concatenate([rows, jnp.zeros((1, half_width), rows.dtype)], axis=0)
-        return padded[near.reshape(-1)].reshape(lines, 1, capacity, half_width)
-
-    sent = jnp.concatenate([outgoing(own_half, own_source), outgoing(far_half, far_source)], axis=1)
-    arrived = lax.all_to_all(sent, ("y", "x"), 0, 0, tiled=True)
-    total_rows = lines * 2 * capacity
-    half_rows = total_rows // 2
-    partial_value = jnp.dot(arrived.reshape(total_rows, half_width), gate_up, preferred_element_type=jnp.float32)
-    mine = lax.dynamic_slice_in_dim(partial_value, side * half_rows, half_rows, 0)
-    other = lax.dynamic_slice_in_dim(partial_value, (1 - side) * half_rows, half_rows, 0)
-    summed = mine + lax.ppermute(other, "core", FLIP)
+    out_columns = down.shape[1]
     block_units = gate_up.shape[1] // 2
-    hidden = (jax.nn.silu(summed[:, :block_units]) * summed[:, block_units:]).astype(jnp.bfloat16)
-    gathered = lax.all_gather(hidden, "zlo", axis=0, tiled=False)
-    partner_part = lax.ppermute(gathered, "core", FLIP)
+    down_blocks = down.reshape(chunks, block_units, out_columns)
     keep_first = side == 0
-    first_hidden = jnp.where(keep_first, gathered, partner_part)
-    second_hidden = jnp.where(keep_first, partner_part, gathered)
-    out_columns = down.shape[1]
-    down_blocks = down.reshape(chunks, block_units, out_columns)
 
     def project(hidden_part):
         value = jnp.einsum("qrk,qkc->rc", hidden_part, down_blocks, preferred_element_type=jnp.float32)
         return value.astype(jnp.bfloat16)
 
-    expert_out = jnp.concatenate([project(first_hidden), project(second_hidden)], axis=0)
-    returned = lax.all_to_all(expert_out.reshape(lines, 2, capacity, out_columns), ("y", "x"), 0, 0, tiled=True)
-    own_table = returned[:, 0].reshape(lines * capacity, out_columns)
-    far_table = returned[:, 1].reshape(lines * capacity, out_columns)
+    def dispatch(rows, source):
+        near = lax.dynamic_index_in_dim(source.reshape(rows_y, 2, rows_x, capacity), zhi, 1, keepdims=False)
+        padded = jnp.concatenate([rows, jnp.zeros((1, half_width), rows.dtype)], axis=0)
+        sent = padded[near.reshape(-1)].reshape(lines, capacity, half_width)
+        return lax.all_to_all(sent, ("y", "x"), 0, 0, tiled=True)
+
+    def experts(arrived):
+        part_rows = lines * capacity
+        half_rows = part_rows // 2
+        partial_value = jnp.dot(arrived.reshape(part_rows, half_width), gate_up, preferred_element_type=jnp.float32)
+        mine = lax.dynamic_slice_in_dim(partial_value, side * half_rows, half_rows, 0)
+        other = lax.dynamic_slice_in_dim(partial_value, (1 - side) * half_rows, half_rows, 0)
+        summed = mine + lax.ppermute(other, "core", FLIP)
+        hidden = (jax.nn.silu(summed[:, :block_units]) * summed[:, block_units:]).astype(jnp.bfloat16)
+        gathered = lax.all_gather(hidden, "zlo", axis=0, tiled=False)
+        partner_part = lax.ppermute(gathered, "core", FLIP)
+        first_hidden = jnp.where(keep_first, gathered, partner_part)
+        second_hidden = jnp.where(keep_first, partner_part, gathered)
+        expert_out = jnp.concatenate([project(first_hidden), project(second_hidden)], axis=0)
+        back = lax.all_to_all(expert_out.reshape(lines, capacity, out_columns), ("y", "x"), 0, 0, tiled=True)
+        return back.reshape(lines * capacity, out_columns)
+
+    own_arrived = dispatch(own_half, own_source)
+    far_arrived = dispatch(far_half, far_source)
+    own_table = experts(own_arrived)
+    far_table = experts(far_arrived)
     far_sum = combine(far_table, far_ids, far_slots, far_weights, zhi, rows_x, capacity)
     own_sum = combine(own_table, expert_ids, own_slots, route_weights, zhi, rows_x, capacity)
     mixed = own_sum + lax.ppermute(far_sum, "zhi", FLIP)
-    return mixed.astype(jnp.bfloat16)
+    return mixed.astype(jnp.bfloat16), far_arrived
 
 
 def per_device(tokens, expert_ids, route_weights, gate_up_panels, down_panels, partner):
-    moe_out = run_layer(tokens, expert_ids, route_weights, gate_up_panels[0, 0], down_panels[0])
-    new_gate_up, new_down = swap_panels(gate_up_panels, down_panels, partner)
+    moe_out, anchor = run_layer(tokens, expert_ids, route_weights, gate_up_panels[0, 0], down_panels[0])
+    gate_up_late, down_late, _ = lax.optimization_barrier((gate_up_panels, down_panels, anchor))
+    new_gate_up, new_down = swap_panels(gate_up_late, down_late, partner)
     return (moe_out, new_gate_up, new_down)
 
 

time: 333 us -> 326 us (0.979)
  waiting for transfers between devices: 175 us -> 79.5 us
  blocking collectives: 0 us -> 88.8 us
  starting transfers between devices: 80.3 us -> 100 us
  between operations: 15.3 us -> 1.99 us
  other arithmetic: 19.4 us -> 10.6 us
    all_gather x0 -> x2, blocking collectives: none -> 88.8 us  [experts(): gathered = lax.all_gather(hidden, 'zlo', axis=0, tiled=False)]
    all_gather x1 -> x0, waiting for transfers between devices: 63 us -> none  [run_layer(): gathered = lax.all_gather(hidden, 'zlo', axis=0, tiled=False)]
    all_to_all x2 -> x4, waiting for transfers between devices: 86.4 us -> 26.3 us  [the longest x2 19.7 us: dispatch(): return lax.all_to_all(sent, ('y', 'x'), 0, 0, tiled=True)]
    ppermute x5 -> x7, waiting for transfers between devices: 9.6 us -> 43.1 us  [the longest x3 41.8 us: run_layer(): lax.ppermute((own_half, expert_ids, route_weights), ('zhi', 'zlo'), mirror)]
    all_to_all x2 -> x4, starting transfers between devices: 11.9 us -> 21.1 us  [the longest x2 13.3 us: dispatch(): return lax.all_to_all(sent, ('y', 'x'), 0, 0, tiled=True)]
    ppermute x5 -> x7, starting transfers between devices: 38.1 us -> 44.3 us  [the longest x3 16.5 us: run_layer(): lax.ppermute((own_half, expert_ids, route_weights), ('zhi', 'zlo'), mirror)]
    concatenate x2, other arithmetic: 5.56 us -> 0.07 us  [experts(): jnp.concatenate([project(first_hidden), project(second_hidden)], axis=0)]
    ppermute x2, waiting for transfers between devices: 7.41 us -> 2.26 us  [swap_panels(): from_ahead = lax.ppermute(second, 'x', behind)]
  transfers between devices with their start and end apart: 17 -> 20, of which waited for: 7 -> 7; matrix products, arithmetic and copies ran while one was open for 11% -> 11% of each run, Pallas kernels for 0% -> 0%
where the time goes in v4:
time: 326 us; the launch traced here: 322 us
  starting transfers between devices  100 us (31%)
  blocking collectives  88.8 us (27%)
  waiting for transfers between devices  79.5 us (24%)
  local copies, waits for them, and re-layouts  31.8 us (10%)
  other arithmetic  10.6 us (3%)
  matrix products  9.66 us (3%)
    all_gather x2, blocking collectives, experts(): gathered = lax.all_gather(hidden, 'zlo', axis=0, tiled=False)  88.8 us
    ppermute x3, waiting for transfers between devices, run_layer(): lax.ppermute((own_half, expert_ids, route_weights), ('zhi', 'zlo'), mirror)  41.8 us
    all_to_all x2, waiting for transfers between devices, dispatch(): return lax.all_to_all(sent, ('y', 'x'), 0, 0, tiled=True)  19.7 us
    ppermute x3, starting transfers between devices, run_layer(): lax.ppermute((own_half, expert_ids, route_weights), ('zhi', 'zlo'), mirror)  16.5 us
    ppermute x2, starting transfers between devices, experts(): partner_part = lax.ppermute(gathered, 'core', FLIP)  15.8 us
    all_to_all x2, starting transfers between devices, dispatch(): return lax.all_to_all(sent, ('y', 'x'), 0, 0, tiled=True)  13.3 us
    ppermute x2, starting transfers between devices, experts(): summed = mine + lax.ppermute(other, 'core', FLIP)  12.1 us
    ppermute x2, starting transfers between devices, swap_panels(): from_ahead = lax.ppermute(second, 'x', behind)  9.15 us
  transfers between devices with their start and end apart: 20, of which 7 were waited for; matrix products, arithmetic and copies ran while one was open for 11% of the time, Pallas kernels for 0%

profile of v4, /device:TPU:1, one launch (start us, length us, event | category | flops | bytes accessed | tf_op | source)
XLA Modules:
  0.0 322.3 jit_solution(18252811483731845290)
XLA Ops:
  0.6 12.1 %collective-permute-start.3 = (s32[128,8]{0,1:T(8,128)}, s32[128,8]{0,1:T(8,128)S(1)}, u32[]{:S(2)}, u32[]{:S(2)}) collective-permute-start(s32[128,8]{0,1:T(8,128)} %param.7), channel_id=1, source_target_pairs={{0,78},{2,76},{4,74},{6,72},{8,70},{10,68},{12,66},{14,64},{64,14}... | collective-permute-start | bytes 12296 | tf_op jit(solution)/shard_map/ppermute | solution.py:79
  15.6 4.3 %scatter_custom_fusion = s32[1536]{0:T(1024)S(1)} fusion(s32[1024]{0:T(1024)S(1)} %bitcast.62, s32[1024]{0:T(1024)S(1)} %reshape.321, s32[]{:T(128)} %constant.115.clone.1), kind=kCustom, calls=%fused_computation.115 | custom fusion | bytes 6148 | tf_op jit(solution)/shard_map/scatter | solution.py:52
  20.7 4.3 %scatter_custom_fusion.1 = s32[1536]{0:T(1024)S(1)} fusion(s32[1024]{0:T(1024)S(1)} %bitcast.63, s32[1024]{0:T(1024)S(1)} %reshape.321, s32[]{:T(128)} %constant.115.clone.1), kind=kCustom, calls=%fused_computation.113 | custom fusion | bytes 6148 | tf_op jit(solution)/shard_map/scatter | solution.py:52
  25.3 4.1 %gather_fusion = bf16[768,1792]{1,0:T(8,128)(2,1)} fusion(bf16[129,1792]{1,0:T(8,128)(2,1)S(1)} %concatenate.24, s32[1024]{0:T(1024)S(1)} %pad_clamp_fusion.1), kind=kCustom, calls=%fused_computation | custom fusion | bytes 5508096 | tf_op jit(solution)/shard_map/gather | solution.py:94
  29.4 6.8 %all-to-all-start = ((bf16[16,48,1792]{2,1,0:T(8,128)(2,1)}), bf16[16,48,1792]{2,1,0:T(8,128)(2,1)}, u32[]{:S(2)}, u32[]{:S(2)}) async-start(bf16[16,48,1792]{2,1,0:T(8,128)(2,1)} %bitcast.50), calls=%async_computation | async-start | bytes 5505024 | tf_op jit(solution)/shard_map/all_to_all | solution.py:95
  38.2 41.4 %collective-permute-done.2 = bf16[128,1792]{1,0:T(8,128)(2,1)S(1)} collective-permute-done((bf16[128,1792]{1,0:T(8,128)(2,1)S(1)}, bf16[128,1792]{1,0:T(8,128)(2,1)S(1)}, u32[]{:S(2)}, u32[]{:S(2)}) %collective-permute-start.2) | collective-permute-done | bytes 458784 | tf_op jit(solution)/shard_map/ppermute | solution.py:79
  79.6 4.1 %gather_fusion.2 = bf16[768,1792]{1,0:T(8,128)(2,1)} fusion(bf16[129,1792]{1,0:T(8,128)(2,1)S(1)} %concatenate.27, s32[1024]{0:T(1024)S(1)} %pad_clamp_fusion), kind=kCustom, calls=%fused_computation.2 | custom fusion | bytes 5508096 | tf_op jit(solution)/shard_map/gather | solution.py:94
  83.7 6.5 %all-to-all-start.2 = ((bf16[16,48,1792]{2,1,0:T(8,128)(2,1)}), bf16[16,48,1792]{2,1,0:T(8,128)(2,1)}, u32[]{:S(2)}, u32[]{:S(2)}) async-start(bf16[16,48,1792]{2,1,0:T(8,128)(2,1)} %bitcast.49), calls=%async_computation.2 | async-start | bytes 5505024 | tf_op jit(solution)/shard_map/all_to_all | solution.py:95
  98.6 5.7 %collective-permute-start = (f32[384,256]{1,0:T(8,128)S(1)}, f32[384,256]{1,0:T(8,128)S(1)}, u32[]{:S(2)}, u32[]{:S(2)}) collective-permute-start(f32[384,256]{1,0:T(8,128)S(1)} %constant_dynamic-slice_fusion.2), channel_id=1, source_target_pairs={{0,1},{1,0},{2,3},{3,2},{4,5},{5,4},{6,7},{7,6},{8,9},{9,8},{10,11... | collective-permute-start | bytes 1179656 | tf_op jit(solution)/shard_map/ppermute | solution.py:103
  105.8 19.7 %all-to-all-done.2 = bf16[16,48,1792]{2,1,0:T(8,128)(2,1)} async-done(((bf16[16,48,1792]{2,1,0:T(8,128)(2,1)}), bf16[16,48,1792]{2,1,0:T(8,128)(2,1)}, u32[]{:S(2)}, u32[]{:S(2)}) %all-to-all-start.2) | async-done | bytes 2752544 | tf_op jit(solution)/shard_map/all_to_all | solution.py:95
  128.2 6.3 %collective-permute-start.4 = (f32[384,256]{1,0:T(8,128)S(1)}, f32[384,256]{1,0:T(8,128)S(1)}, u32[]{:S(2)}, u32[]{:S(2)}) collective-permute-start(f32[384,256]{1,0:T(8,128)S(1)} %constant_dynamic-slice_fusion), channel_id=1, source_target_pairs={{0,1},{1,0},{2,3},{3,2},{4,5},{5,4},{6,7},{7,6},{8,9},{9,8},{10,11... | collective-permute-start | bytes 1179656 | tf_op jit(solution)/shard_map/ppermute | solution.py:103
  136.5 43.2 %all-gather = bf16[3072,128]{1,0:T(8,128)(2,1)S(1)} all-gather(bf16[384,128]{1,0:T(8,128)(2,1)S(1)} %fusion.23), channel_id=2, replica_groups=mesh['y'=4,'zhi'=2,'x'=4,'zlo'=8,'core'=2] {'zlo'}, dimensions={0}, use_global_device_ids=true | all-gather | bytes 884736 | tf_op jit(solution)/shard_map/all_gather | solution.py:105
  179.7 8.0 %collective-permute-start.1 = (bf16[8,384,128]{2,1,0:T(8,128)(2,1)S(1)}, bf16[8,384,128]{2,1,0:T(8,128)(2,1)S(1)}, u32[]{:S(2)}, u32[]{:S(2)}) collective-permute-start(bf16[8,384,128]{2,1,0:T(8,128)(2,1)S(1)} %bitcast.53), channel_id=1, source_target_pairs={{0,1},{1,0},{2,3},{3,2},{4,5},{5,4},{6,7},{7,6},{8,9},{9,8},{10,11... | collective-permute-start | bytes 2359304 | tf_op jit(solution)/shard_map/ppermute | solution.py:106
  191.7 4.7 %collective-permute-start.14 = (bf16[1,512,224]{1,2,0:T(8,128)(2,1)S(1)}, bf16[1,512,224]{1,2,0:T(8,128)(2,1)S(1)}, u32[]{:S(2)}, u32[]{:S(2)}) collective-permute-start(bf16[1,512,224]{1,2,0:T(8,128)(2,1)S(1)} %get-tuple-element.20), channel_id=1, source_target_pairs={{0,48},{16,0},{32,16},{48,32},{1,49},{17,1},{33,17},{49,33},{2,50}... | collective-permute-start | bytes 688136 | tf_op jit(solution)/shard_map/ppermute | solution.py:24
  196.5 45.6 %all-gather.1 = bf16[3072,128]{1,0:T(8,128)(2,1)} all-gather(bf16[384,128]{1,0:T(8,128)(2,1)S(1)} %fusion.22), channel_id=3, replica_groups=mesh['y'=4,'zhi'=2,'x'=4,'zlo'=8,'core'=2] {'zlo'}, dimensions={0}, use_global_device_ids=true | all-gather | bytes 884736 | tf_op jit(solution)/shard_map/all_gather | solution.py:105
  242.2 7.8 %collective-permute-start.5 = (bf16[8,384,128]{2,1,0:T(8,128)(2,1)}, bf16[8,384,128]{2,1,0:T(8,128)(2,1)}, u32[]{:S(2)}, u32[]{:S(2)}) collective-permute-start(bf16[8,384,128]{2,1,0:T(8,128)(2,1)} %bitcast.14), channel_id=1, source_target_pairs={{0,1},{1,0},{2,3},{3,2},{4,5},{5,4},{6,7},{7,6},{8,9},{9,8},{10,11... | collective-permute-start | bytes 2359304 | tf_op jit(solution)/shard_map/ppermute | solution.py:106
  256.4 4.4 %collective-permute-start.10 = (bf16[1,1,896,256]{3,2,1,0:T(8,128)(2,1)}, bf16[1,1,896,256]{3,2,1,0:T(8,128)(2,1)S(1)}, u32[]{:S(2)}, u32[]{:S(2)}) collective-permute-start(bf16[1,1,896,256]{3,2,1,0:T(8,128)(2,1)} %get-tuple-element.18), channel_id=1, source_target_pairs={{0,48},{16,0},{32,16},{48,32},{1,49},{17,1},{33,17},{49,33},{2,50}... | collective-permute-start | bytes 1376264 | tf_op jit(solution)/shard_map/ppermute | solution.py:24
  271.9 5.6 %collective-permute-start.11 = (bf16[1,1,896,256]{3,2,1,0:T(8,128)(2,1)}, bf16[1,1,896,256]{3,2,1,0:T(8,128)(2,1)}, u32[]{:S(2)}, u32[]{:S(2)}) collective-permute-start(bf16[1,1,896,256]{3,2,1,0:T(8,128)(2,1)} %broadcast_select_fusion), channel_id=1, source_target_pairs={{0,48},{16,0},{32,16},{48,32},{1,49},{17,1},{33,17},{49,33},{2,50}... | collective-permute-start | bytes 1376264 | tf_op jit(solution)/shard_map/ppermute | solution.py:33
  277.6 3.9 %gather_fusion.1 = bf16[1024,224]{1,0:T(8,128)(2,1)S(1)} fusion(bf16[769,224]{1,0:T(8,128)(2,1)S(1)} %concatenate.26, s32[1024]{0:T(1024)S(1)} %broadcast_clamp_fusion.1), kind=kCustom, calls=%fused_computation.1 | custom fusion | bytes 921600 | tf_op jit(solution)/shard_map/gather | solution.py:62
  285.9 4.2 %all-to-all-start.3 = ((bf16[16,48,224]{2,1,0:T(8,128)(2,1)}), bf16[16,48,224]{2,1,0:T(8,128)(2,1)}, u32[]{:S(2)}, u32[]{:S(2)}) async-start(bf16[16,48,224]{2,1,0:T(8,128)(2,1)} %bitcast.17), calls=%async_computation.3 | async-start | bytes 786432 | tf_op jit(solution)/shard_map/all_to_all | solution.py:110
  291.9 6.6 %all-to-all-done.3 = bf16[16,48,224]{2,1,0:T(8,128)(2,1)} async-done(((bf16[16,48,224]{2,1,0:T(8,128)(2,1)}), bf16[16,48,224]{2,1,0:T(8,128)(2,1)}, u32[]{:S(2)}, u32[]{:S(2)}) %all-to-all-start.3) | async-done | bytes 344096 | tf_op jit(solution)/shard_map/all_to_all | solution.py:110
  299.5 3.9 %gather_fusion.3 = bf16[1024,224]{1,0:T(8,128)(2,1)S(1)} fusion(bf16[769,224]{1,0:T(8,128)(2,1)S(1)} %concatenate.29, s32[1024]{0:T(1024)S(1)} %broadcast_clamp_fusion), kind=kCustom, calls=%fused_computation.3 | custom fusion | bytes 921600 | tf_op jit(solution)/shard_map/gather | solution.py:62
  303.8 8.9 %collective-permute-start.7 = (f32[128,224]{1,0:T(8,128)S(1)}, f32[128,224]{1,0:T(8,128)S(1)}, u32[]{:S(2)}, u32[]{:S(2)}) collective-permute-start(f32[128,224]{1,0:T(8,128)S(1)} %fusion.4), channel_id=1, source_target_pairs={{0,64},{64,0},{1,65},{65,1},{2,66},{66,2},{3,67},{67,3},{4,68},{68... | collective-permute-start | bytes 344072 | tf_op jit(solution)/shard_map/ppermute | solution.py:119
  313.7 7.8 %collective-permute-done.7 = f32[128,224]{1,0:T(8,128)S(1)} collective-permute-done((f32[128,224]{1,0:T(8,128)S(1)}, f32[128,224]{1,0:T(8,128)S(1)}, u32[]{:S(2)}, u32[]{:S(2)}) %collective-permute-start.7) | collective-permute-done | bytes 114720 | tf_op jit(solution)/shard_map/ppermute | solution.py:119
  (116 shorter events, 50.4 us)
Async XLA Ops:
  0.6 14.8 %copy-start = (bf16[128,3584]{1,0:T(8,128)(2,1)S(1)}, bf16[128,3584]{1,0:T(8,128)(2,1)}, u32[]{:S(2)}) copy-start(bf16[128,3584]{1,0:T(8,128)(2,1)} %param.6) | copy-start | bytes 2752516
  0.6 19.4 %collective-permute-start.3 = (s32[128,8]{0,1:T(8,128)}, s32[128,8]{0,1:T(8,128)S(1)}, u32[]{:S(2)}, u32[]{:S(2)}) collective-permute-start(s32[128,8]{0,1:T(8,128)} %param.7), channel_id=1, source_target_pairs={{0,78},{2,76},{4,74},{6,72},{8,70},{10,68},{12,66},{14,64},{64,14}... | collective-permute-start | bytes 12296 | tf_op jit(solution)/shard_map/ppermute | solution.py:79
  29.4 54.3 %all-to-all-start = ((bf16[16,48,1792]{2,1,0:T(8,128)(2,1)}), bf16[16,48,1792]{2,1,0:T(8,128)(2,1)}, u32[]{:S(2)}, u32[]{:S(2)}) async-start(bf16[16,48,1792]{2,1,0:T(8,128)(2,1)} %bitcast.50), calls=%async_computation | async-start | bytes 5505024 | tf_op jit(solution)/shard_map/all_to_all | solution.py:95
  36.2 43.4 %collective-permute-start.2 = (bf16[128,1792]{1,0:T(8,128)(2,1)S(1)}, bf16[128,1792]{1,0:T(8,128)(2,1)S(1)}, u32[]{:S(2)}, u32[]{:S(2)}) collective-permute-start(bf16[128,1792]{1,0:T(8,128)(2,1)S(1)} %constant_dynamic-slice_fusion.4), channel_id=1, source_target_pairs={{0,78},{2,76},{4,74},{6,72},{8,70},{10,68},{12,66},{14,64},{64,14}... | collective-permute-start | bytes 1376264 | tf_op jit(solution)/shard_map/ppermute | solution.py:79
  83.7 10.6 %copy-start.2 = (bf16[1,1024,224]{1,2,0:T(8,128)(2,1)S(1)}, bf16[1,1024,224]{1,2,0:T(8,128)(2,1)}, u32[]{:S(2)}) copy-start(bf16[1,1024,224]{1,2,0:T(8,128)(2,1)} %param.10) | copy-start | bytes 1376260
  83.7 12.2 %copy-start.1 = (bf16[1,1,1792,256]{3,2,1,0:T(8,128)(2,1)S(1)}, bf16[1,1,1792,256]{3,2,1,0:T(8,128)(2,1)}, u32[]{:S(2)}) copy-start(bf16[1,1,1792,256]{3,2,1,0:T(8,128)(2,1)} %param.9) | copy-start | bytes 2752516
  83.7 41.8 %all-to-all-start.2 = ((bf16[16,48,1792]{2,1,0:T(8,128)(2,1)}), bf16[16,48,1792]{2,1,0:T(8,128)(2,1)}, u32[]{:S(2)}, u32[]{:S(2)}) async-start(bf16[16,48,1792]{2,1,0:T(8,128)(2,1)} %bitcast.49), calls=%async_computation.2 | async-start | bytes 5505024 | tf_op jit(solution)/shard_map/all_to_all | solution.py:95
  90.3 5.6 %collective-permute-start.6 = (f32[128,8]{0,1:T(8,128)S(1)}, f32[128,8]{0,1:T(8,128)S(1)}, u32[]{:S(2)}, u32[]{:S(2)}) collective-permute-start(f32[128,8]{0,1:T(8,128)S(1)} %copy-done.5), channel_id=1, source_target_pairs={{0,78},{2,76},{4,74},{6,72},{8,70},{10,68},{12,66},{14,64},{64,14}... | collective-permute-start | bytes 12296 | tf_op jit(solution)/shard_map/ppermute | solution.py:79
  98.6 7.0 %collective-permute-start = (f32[384,256]{1,0:T(8,128)S(1)}, f32[384,256]{1,0:T(8,128)S(1)}, u32[]{:S(2)}, u32[]{:S(2)}) collective-permute-start(f32[384,256]{1,0:T(8,128)S(1)} %constant_dynamic-slice_fusion.2), channel_id=1, source_target_pairs={{0,1},{1,0},{2,3},{3,2},{4,5},{5,4},{6,7},{7,6},{8,9},{9,8},{10,11... | collective-permute-start | bytes 1179656 | tf_op jit(solution)/shard_map/ppermute | solution.py:103
  128.2 68.2 %collective-permute-start.4 = (f32[384,256]{1,0:T(8,128)S(1)}, f32[384,256]{1,0:T(8,128)S(1)}, u32[]{:S(2)}, u32[]{:S(2)}) collective-permute-start(f32[384,256]{1,0:T(8,128)S(1)} %constant_dynamic-slice_fusion), channel_id=1, source_target_pairs={{0,1},{1,0},{2,3},{3,2},{4,5},{5,4},{6,7},{7,6},{8,9},{9,8},{10,11... | collective-permute-start | bytes 1179656 | tf_op jit(solution)/shard_map/ppermute | solution.py:103
  134.6 55.1 %collective-permute-start.12 = (bf16[1,512,224]{1,2,0:T(8,128)(2,1)S(1)}, bf16[1,512,224]{1,2,0:T(8,128)(2,1)S(1)}, u32[]{:S(2)}, u32[]{:S(2)}) collective-permute-start(bf16[1,512,224]{1,2,0:T(8,128)(2,1)S(1)} %slice.30), channel_id=1, source_target_pairs={{0,16},{16,32},{32,48},{48,0},{1,17},{17,33},{33,49},{49,1},{2,18}... | collective-permute-start | bytes 688136 | tf_op jit(solution)/shard_map/ppermute | solution.py:23
  179.7 81.9 %collective-permute-start.1 = (bf16[8,384,128]{2,1,0:T(8,128)(2,1)S(1)}, bf16[8,384,128]{2,1,0:T(8,128)(2,1)S(1)}, u32[]{:S(2)}, u32[]{:S(2)}) collective-permute-start(bf16[8,384,128]{2,1,0:T(8,128)(2,1)S(1)} %bitcast.53), channel_id=1, source_target_pairs={{0,1},{1,0},{2,3},{3,2},{4,5},{5,4},{6,7},{7,6},{8,9},{9,8},{10,11... | collective-permute-start | bytes 2359304 | tf_op jit(solution)/shard_map/ppermute | solution.py:106
  187.7 65.4 %collective-permute-start.8 = (bf16[1,1,896,256]{3,2,1,0:T(8,128)(2,1)S(1)}, bf16[1,1,896,256]{3,2,1,0:T(8,128)(2,1)S(1)}, u32[]{:S(2)}, u32[]{:S(2)}) collective-permute-start(bf16[1,1,896,256]{3,2,1,0:T(8,128)(2,1)S(1)} %slice.28), channel_id=1, source_target_pairs={{0,16},{16,32},{32,48},{48,0},{1,17},{17,33},{33,49},{49,1},{2,18}... | collective-permute-start | bytes 1376264 | tf_op jit(solution)/shard_map/ppermute | solution.py:23
  189.7 66.7 %collective-permute-start.13 = (bf16[1,512,224]{1,2,0:T(8,128)(2,1)S(1)}, bf16[1,512,224]{1,2,0:T(8,128)(2,1)S(1)}, u32[]{:S(2)}, u32[]{:S(2)}) collective-permute-start(bf16[1,512,224]{1,2,0:T(8,128)(2,1)S(1)} %get-tuple-element.19), channel_id=1, source_target_pairs={{0,16},{16,32},{32,48},{48,0},{1,17},{17,33},{33,49},{49,1},{2,18}... | collective-permute-start | bytes 688136 | tf_op jit(solution)/shard_map/ppermute | solution.py:32
  191.7 58.3 %collective-permute-start.14 = (bf16[1,512,224]{1,2,0:T(8,128)(2,1)S(1)}, bf16[1,512,224]{1,2,0:T(8,128)(2,1)S(1)}, u32[]{:S(2)}, u32[]{:S(2)}) collective-permute-start(bf16[1,512,224]{1,2,0:T(8,128)(2,1)S(1)} %get-tuple-element.20), channel_id=1, source_target_pairs={{0,48},{16,0},{32,16},{48,32},{1,49},{17,1},{33,17},{49,33},{2,50}... | collective-permute-start | bytes 688136 | tf_op jit(solution)/shard_map/ppermute | solution.py:24
  196.5 65.2 %copy-start.4 = (bf16[28,8,8,128]{3,2,1,0:T(8,128)(2,1)S(1)}, bf16[28,8,8,128]{3,2,1,0:T(8,128)(2,1)}, u32[]{:S(2)}) copy-start(bf16[28,8,8,128]{3,2,1,0:T(8,128)(2,1)} %copy.81) | copy-start | bytes 1376260
  242.2 39.4 %collective-permute-start.5 = (bf16[8,384,128]{2,1,0:T(8,128)(2,1)}, bf16[8,384,128]{2,1,0:T(8,128)(2,1)}, u32[]{:S(2)}, u32[]{:S(2)}) collective-permute-start(bf16[8,384,128]{2,1,0:T(8,128)(2,1)} %bitcast.14), channel_id=1, source_target_pairs={{0,1},{1,0},{2,3},{3,2},{4,5},{5,4},{6,7},{7,6},{8,9},{9,8},{10,11... | collective-permute-start | bytes 2359304 | tf_op jit(solution)/shard_map/ppermute | solution.py:106
  250.0 10.9 %collective-permute-start.15 = (bf16[1,512,224]{1,2,0:T(8,128)(2,1)S(1)}, bf16[1,512,224]{1,2,0:T(8,128)(2,1)S(1)}, u32[]{:S(2)}, u32[]{:S(2)}) collective-permute-start(bf16[1,512,224]{1,2,0:T(8,128)(2,1)S(1)} %broadcast_select_fusion.2), channel_id=1, source_target_pairs={{0,48},{16,0},{32,16},{48,32},{1,49},{17,1},{33,17},{49,33},{2,50}... | collective-permute-start | bytes 688136 | tf_op jit(solution)/shard_map/ppermute | solution.py:33
  254.3 36.2 %collective-permute-start.9 = (bf16[1,1,896,256]{3,2,1,0:T(8,128)(2,1)}, bf16[1,1,896,256]{3,2,1,0:T(8,128)(2,1)}, u32[]{:S(2)}, u32[]{:S(2)}) collective-permute-start(bf16[1,1,896,256]{3,2,1,0:T(8,128)(2,1)} %get-tuple-element.17), channel_id=1, source_target_pairs={{0,16},{16,32},{32,48},{48,0},{1,17},{17,33},{33,49},{49,1},{2,18}... | collective-permute-start | bytes 1376264 | tf_op jit(solution)/shard_map/ppermute | solution.py:32
  256.4 14.7 %collective-permute-start.10 = (bf16[1,1,896,256]{3,2,1,0:T(8,128)(2,1)}, bf16[1,1,896,256]{3,2,1,0:T(8,128)(2,1)S(1)}, u32[]{:S(2)}, u32[]{:S(2)}) collective-permute-start(bf16[1,1,896,256]{3,2,1,0:T(8,128)(2,1)} %get-tuple-element.18), channel_id=1, source_target_pairs={{0,48},{16,0},{32,16},{48,32},{1,49},{17,1},{33,17},{49,33},{2,50}... | collective-permute-start | bytes 1376264 | tf_op jit(solution)/shard_map/ppermute | solution.py:24
  263.5 14.0 %all-to-all-start.1 = ((bf16[16,48,224]{2,1,0:T(8,128)(2,1)}), bf16[16,48,224]{2,1,0:T(8,128)(2,1)S(1)}, u32[]{:S(2)}, u32[]{:S(2)}) async-start(bf16[16,48,224]{2,1,0:T(8,128)(2,1)} %bitcast.7), calls=%async_computation.1 | async-start | bytes 786432 | tf_op jit(solution)/shard_map/all_to_all | solution.py:110
  271.9 18.7 %collective-permute-start.11 = (bf16[1,1,896,256]{3,2,1,0:T(8,128)(2,1)}, bf16[1,1,896,256]{3,2,1,0:T(8,128)(2,1)}, u32[]{:S(2)}, u32[]{:S(2)}) collective-permute-start(bf16[1,1,896,256]{3,2,1,0:T(8,128)(2,1)} %broadcast_select_fusion), channel_id=1, source_target_pairs={{0,48},{16,0},{32,16},{48,32},{1,49},{17,1},{33,17},{49,33},{2,50}... | collective-permute-start | bytes 1376264 | tf_op jit(solution)/shard_map/ppermute | solution.py:33
  285.9 12.5 %all-to-all-start.3 = ((bf16[16,48,224]{2,1,0:T(8,128)(2,1)}), bf16[16,48,224]{2,1,0:T(8,128)(2,1)}, u32[]{:S(2)}, u32[]{:S(2)}) async-start(bf16[16,48,224]{2,1,0:T(8,128)(2,1)} %bitcast.17), calls=%async_computation.3 | async-start | bytes 786432 | tf_op jit(solution)/shard_map/all_to_all | solution.py:110
  303.8 17.7 %collective-permute-start.7 = (f32[128,224]{1,0:T(8,128)S(1)}, f32[128,224]{1,0:T(8,128)S(1)}, u32[]{:S(2)}, u32[]{:S(2)}) collective-permute-start(f32[128,224]{1,0:T(8,128)S(1)} %fusion.4), channel_id=1, source_target_pairs={{0,64},{64,0},{1,65},{65,1},{2,66},{66,2},{3,67},{67,3},{4,68},{68... | collective-permute-start | bytes 344072 | tf_op jit(solution)/shard_map/ppermute | solution.py:119
  (3 other events, 24.8 us)

commit v5 on v4

--- a/solution.py
+++ b/solution.py
@@ -40,6 +40,12 @@
     return (new_gate_up, new_down)
 
 
+def gather_line(block):
+    count = lax.axis_size("zlo")
+    spread = jnp.broadcast_to(block[None], (count,) + block.shape)
+    return lax.all_to_all(spread, "zlo", 0, 0, tiled=True)
+
+
 def routing(expert_ids, expert_count, capacity):
     token_rows, top_count = expert_ids.shape
     labels = jnp.arange(expert_count, dtype=jnp.int32)
@@ -63,7 +69,7 @@
     return jnp.sum(chosen.astype(jnp.float32) * weights[:, :, None], axis=1)
 
 
-def run_layer(tokens, expert_ids, route_weights, gate_up, down):
+def run_layer(tokens, expert_ids, route_weights, gate_up, down, swapped):
     rows_y, rows_x = lax.axis_size("y"), lax.axis_size("x")
     lines = rows_y * rows_x
     expert_count = 2 * lines
@@ -74,9 +80,15 @@
     half_width = model_width // 2
     side = lax.axis_index("core")
     zhi = lax.axis_index("zhi")
+    chunk_width = half_width // chunks
     own_half = lax.dynamic_slice_in_dim(tokens, side * half_width, half_width, 1)
+    own_chunk = lax.dynamic_slice_in_dim(
+        tokens, side * half_width + lax.axis_index("zlo") * chunk_width, chunk_width, 1
+    )
     mirror = [(high * chunks + low, (1 - high) * chunks + chunks - 1 - low) for high in range(2) for low in range(chunks)]
-    far_half, far_ids, far_weights = lax.ppermute((own_half, expert_ids, route_weights), ("zhi", "zlo"), mirror)
+    far_chunk, far_ids, far_weights = lax.ppermute((own_chunk, expert_ids, route_weights), ("zhi", "zlo"), mirror)
+    far_chunks = gather_line(far_chunk)[::-1]
+    far_half = jnp.transpose(far_chunks, (1, 0, 2)).reshape(token_rows, half_width)
     own_slots, own_source = routing(expert_ids, expert_count, capacity)
     far_slots, far_source = routing(far_ids, expert_count, capacity)
     out_columns = down.shape[1]
@@ -102,7 +114,7 @@
         other = lax.dynamic_slice_in_dim(partial_value, (1 - side) * half_rows, half_rows, 0)
         summed = mine + lax.ppermute(other, "core", FLIP)
         hidden = (jax.nn.silu(summed[:, :block_units]) * summed[:, block_units:]).astype(jnp.bfloat16)
-        gathered = lax.all_gather(hidden, "zlo", axis=0, tiled=False)
+        gathered = gather_line(hidden)
         partner_part = lax.ppermute(gathered, "core", FLIP)
         first_hidden = jnp.where(keep_first, gathered, partner_part)
         second_hidden = jnp.where(keep_first, partner_part, gathered)
@@ -112,18 +124,20 @@
 
     own_arrived = dispatch(own_half, own_source)
     far_arrived = dispatch(far_half, far_source)
+    own_arrived, swapped = lax.optimization_barrier((own_arrived, swapped))
     own_table = experts(own_arrived)
     far_table = experts(far_arrived)
     far_sum = combine(far_table, far_ids, far_slots, far_weights, zhi, rows_x, capacity)
     own_sum = combine(own_table, expert_ids, own_slots, route_weights, zhi, rows_x, capacity)
     mixed = own_sum + lax.ppermute(far_sum, "zhi", FLIP)
-    return mixed.astype(jnp.bfloat16), far_arrived
+    return mixed.astype(jnp.bfloat16), swapped
 
 
 def per_device(tokens, expert_ids, route_weights, gate_up_panels, down_panels, partner):
-    moe_out, anchor = run_layer(tokens, expert_ids, route_weights, gate_up_panels[0, 0], down_panels[0])
-    gate_up_late, down_late, _ = lax.optimization_barrier((gate_up_panels, down_panels, anchor))
-    new_gate_up, new_down = swap_panels(gate_up_late, down_late, partner)
+    swapped = swap_panels(gate_up_panels, down_panels, partner)
+    moe_out, (new_gate_up, new_down) = run_layer(
+        tokens, expert_ids, route_weights, gate_up_panels[0, 0], down_panels[0], swapped
+    )
     return (moe_out, new_gate_up, new_down)
 
 

time: 326 us -> 347 us (1.064)
  blocking collectives: 88.8 us -> 0 us
  waiting for transfers between devices: 79.5 us -> 156 us
  starting transfers between devices: 100 us -> 125 us
  local copies, waits for them, and re-layouts: 31.8 us -> 38 us
    all_gather x2 -> x0, blocking collectives: 88.8 us -> none  [experts(): gathered = lax.all_gather(hidden, 'zlo', axis=0, tiled=False)]
    all_to_all x0 -> x3, waiting for transfers between devices: none -> 59.4 us  [gather_line(): return lax.all_to_all(spread, 'zlo', 0, 0, tiled=True)]
    ppermute x3, waiting for transfers between devices: 41.8 us -> 2.5 us  [run_layer(): lax.ppermute((own_chunk, expert_ids, route_weights), ('zhi', 'zlo'), mirror)]
    ppermute x2, waiting for transfers between devices: 0.01 us -> 35.7 us  [swap_panels(): from_behind = lax.ppermute(first, 'x', ahead)]
    all_to_all x0 -> x3, starting transfers between devices: none -> 34.4 us  [gather_line(): return lax.all_to_all(spread, 'zlo', 0, 0, tiled=True)]
    ppermute x2, waiting for transfers between devices: 0.01 us -> 32.2 us  [swap_panels(): got_ahead = lax.ppermute(send_behind, 'x', behind)]
    all_to_all x2, waiting for transfers between devices: 19.7 us -> 0.01 us  [dispatch(): return lax.all_to_all(sent, ('y', 'x'), 0, 0, tiled=True)]
    ppermute x1, starting transfers between devices: 8.91 us -> 2.56 us  [run_layer(): mixed = own_sum + lax.ppermute(far_sum, 'zhi', FLIP)]
  transfers between devices with their start and end apart: 20 -> 23, of which waited for: 7 -> 12; matrix products, arithmetic and copies ran while one was open for 11% -> 15% of each run, Pallas kernels for 0% -> 0%
where the time goes in v5:
time: 347 us; the launch traced here: 342 us
  waiting for transfers between devices  156 us (45%)
  starting transfers between devices  125 us (36%)
  local copies, waits for them, and re-layouts  38 us (11%)
  other arithmetic  11.5 us (3%)
  matrix products  9.41 us (3%)
    all_to_all x3, waiting for transfers between devices, gather_line(): return lax.all_to_all(spread, 'zlo', 0, 0, tiled=True)  59.4 us
    ppermute x2, waiting for transfers between devices, swap_panels(): from_behind = lax.ppermute(first, 'x', ahead)  35.7 us
    all_to_all x3, starting transfers between devices, gather_line(): return lax.all_to_all(spread, 'zlo', 0, 0, tiled=True)  34.4 us
    ppermute x2, waiting for transfers between devices, swap_panels(): got_ahead = lax.ppermute(send_behind, 'x', behind)  32.2 us
    ppermute x3, starting transfers between devices, run_layer(): lax.ppermute((own_chunk, expert_ids, route_weights), ('zhi', 'zlo'), mirror)  17 us
    ppermute x2, starting transfers between devices, experts(): partner_part = lax.ppermute(gathered, 'core', FLIP)  16.7 us
    all_to_all x2, starting transfers between devices, dispatch(): return lax.all_to_all(sent, ('y', 'x'), 0, 0, tiled=True)  13.4 us
    ppermute x1, waiting for transfers between devices, run_layer(): mixed = own_sum + lax.ppermute(far_sum, 'zhi', FLIP)  12 us
  transfers between devices with their start and end apart: 23, of which 12 were waited for; matrix products, arithmetic and copies ran while one was open for 15% of the time, Pallas kernels for 0%

profile of v5, /device:TPU:1, one launch (start us, length us, event | category | flops | bytes accessed | tf_op | source)
XLA Modules:
  0.0 341.7 jit_solution(5721481290665623737)
XLA Ops:
  0.6 12.1 %collective-permute-start.11 = (s32[128,8]{0,1:T(8,128)}, s32[128,8]{0,1:T(8,128)S(1)}, u32[]{:S(2)}, u32[]{:S(2)}) collective-permute-start(s32[128,8]{0,1:T(8,128)} %param.7), channel_id=1, source_target_pairs={{0,78},{2,76},{4,74},{6,72},{8,70},{10,68},{12,66},{14,64},{64,14}... | collective-permute-start | bytes 12296 | tf_op jit(solution)/shard_map/ppermute | solution.py:89
  20.0 12.6 %all-to-all-start.3 = ((bf16[8,128,224]{1,2,0:T(8,128)(2,1)}), bf16[8,128,224]{1,2,0:T(8,128)(2,1)S(1)}, u32[]{:S(2)}, u32[]{:S(2)}) async-start(bf16[8,128,224]{1,2,0:T(8,128)(2,1)} %broadcast_in_dim.17), calls=%async_computation.3 | async-start | bytes 917504 | tf_op jit(solution)/shard_map/all_to_all | solution.py:46
  33.7 4.3 %scatter_custom_fusion = s32[1536]{0:T(1024)S(1)} fusion(s32[1024]{0:T(1024)S(1)} %bitcast.63, s32[1024]{0:T(1024)S(1)} %reshape.328, s32[]{:T(128)} %constant.119.clone.1), kind=kCustom, calls=%fused_computation.115 | custom fusion | bytes 6148 | tf_op jit(solution)/shard_map/scatter | solution.py:58
  38.9 4.3 %scatter_custom_fusion.1 = s32[1536]{0:T(1024)S(1)} fusion(s32[1024]{0:T(1024)S(1)} %bitcast.62, s32[1024]{0:T(1024)S(1)} %reshape.328, s32[]{:T(128)} %constant.119.clone.1), kind=kCustom, calls=%fused_computation.113 | custom fusion | bytes 6148 | tf_op jit(solution)/shard_map/scatter | solution.py:58
  43.5 4.1 %gather_fusion = bf16[768,1792]{1,0:T(8,128)(2,1)} fusion(bf16[129,1792]{1,0:T(8,128)(2,1)S(1)} %concatenate.24, s32[1024]{0:T(1024)S(1)} %pad_clamp_fusion.1), kind=kCustom, calls=%fused_computation | custom fusion | bytes 5508096 | tf_op jit(solution)/shard_map/gather | solution.py:106
  47.6 4.2 %all-to-all-done.3 = bf16[8,128,224]{1,2,0:T(8,128)(2,1)S(1)} async-done(((bf16[8,128,224]{1,2,0:T(8,128)(2,1)}), bf16[8,128,224]{1,2,0:T(8,128)(2,1)S(1)}, u32[]{:S(2)}, u32[]{:S(2)}) %all-to-all-start.3) | async-done | bytes 458784 | tf_op jit(solution)/shard_map/all_to_all | solution.py:46
  51.8 6.9 %all-to-all-start = ((bf16[16,48,1792]{2,1,0:T(8,128)(2,1)}), bf16[16,48,1792]{2,1,0:T(8,128)(2,1)}, u32[]{:S(2)}, u32[]{:S(2)}) async-start(bf16[16,48,1792]{2,1,0:T(8,128)(2,1)} %bitcast.50), calls=%async_computation | async-start | bytes 5505024 | tf_op jit(solution)/shard_map/all_to_all | solution.py:107
  67.8 26.8 %collective-permute-done.4 = bf16[1,512,224]{1,2,0:T(8,128)(2,1)S(1)} collective-permute-done((bf16[1,512,224]{1,2,0:T(8,128)(2,1)}, bf16[1,512,224]{1,2,0:T(8,128)(2,1)S(1)}, u32[]{:S(2)}, u32[]{:S(2)}) %collective-permute-start.4) | collective-permute-done | bytes 229408 | tf_op jit(solution)/shard_map/ppermute | solution.py:23
  97.2 8.9 %collective-permute-done = bf16[1,1,896,256]{3,2,1,0:T(8,128)(2,1)S(1)} collective-permute-done((bf16[1,1,896,256]{3,2,1,0:T(8,128)(2,1)}, bf16[1,1,896,256]{3,2,1,0:T(8,128)(2,1)S(1)}, u32[]{:S(2)}, u32[]{:S(2)}) %collective-permute-start) | collective-permute-done | bytes 458784 | tf_op jit(solution)/shard_map/ppermute | solution.py:23
  120.7 4.1 %gather_fusion.2 = bf16[768,1792]{1,0:T(8,128)(2,1)} fusion(bf16[129,1792]{1,0:T(8,128)(2,1)S(1)} %concatenate.29, s32[1024]{0:T(1024)S(1)} %pad_clamp_fusion), kind=kCustom, calls=%fused_computation.2 | custom fusion | bytes 5508096 | tf_op jit(solution)/shard_map/gather | solution.py:106
  124.8 6.5 %all-to-all-start.4 = ((bf16[16,48,1792]{2,1,0:T(8,128)(2,1)}), bf16[16,48,1792]{2,1,0:T(8,128)(2,1)}, u32[]{:S(2)}, u32[]{:S(2)}) async-start(bf16[16,48,1792]{2,1,0:T(8,128)(2,1)} %bitcast.51), calls=%async_computation.4 | async-start | bytes 5505024 | tf_op jit(solution)/shard_map/all_to_all | solution.py:107
  132.1 4.4 %collective-permute-start.3 = (bf16[1,1,896,256]{3,2,1,0:T(8,128)(2,1)}, bf16[1,1,896,256]{3,2,1,0:T(8,128)(2,1)}, u32[]{:S(2)}, u32[]{:S(2)}) collective-permute-start(bf16[1,1,896,256]{3,2,1,0:T(8,128)(2,1)} %broadcast_select_fusion), channel_id=1, source_target_pairs={{0,48},{16,0},{32,16},{48,32},{1,49},{17,1},{33,17},{49,33},{2,50}... | collective-permute-start | bytes 1376264 | tf_op jit(solution)/shard_map/ppermute | solution.py:33
  138.6 32.2 %collective-permute-done.3 = bf16[1,1,896,256]{3,2,1,0:T(8,128)(2,1)} collective-permute-done((bf16[1,1,896,256]{3,2,1,0:T(8,128)(2,1)}, bf16[1,1,896,256]{3,2,1,0:T(8,128)(2,1)}, u32[]{:S(2)}, u32[]{:S(2)}) %collective-permute-start.3) | collective-permute-done | bytes 458784 | tf_op jit(solution)/shard_map/ppermute | solution.py:33
  176.6 6.0 %collective-permute-start.8 = (f32[384,256]{1,0:T(8,128)}, f32[384,256]{1,0:T(8,128)S(1)}, u32[]{:S(2)}, u32[]{:S(2)}) collective-permute-start(f32[384,256]{1,0:T(8,128)} %constant_dynamic-slice_fusion.3), channel_id=1, source_target_pairs={{0,1},{1,0},{2,3},{3,2},{4,5},{5,4},{6,7},{7,6},{8,9},{9,8},{10,11... | collective-permute-start | bytes 1179656 | tf_op jit(solution)/shard_map/ppermute | solution.py:115
  185.3 16.5 %all-to-all-start.1 = ((bf16[8,384,128]{2,1,0:T(8,128)(2,1)}), bf16[8,384,128]{2,1,0:T(8,128)(2,1)S(1)}, u32[]{:S(2)}, u32[]{:S(2)}) async-start(bf16[8,384,128]{2,1,0:T(8,128)(2,1)} %broadcast_in_dim.15), calls=%async_computation.1 | async-start | bytes 1572864 | tf_op jit(solution)/shard_map/all_to_all | solution.py:46
  208.5 32.4 %all-to-all-done.1 = bf16[8,384,128]{2,1,0:T(8,128)(2,1)S(1)} async-done(((bf16[8,384,128]{2,1,0:T(8,128)(2,1)}), bf16[8,384,128]{2,1,0:T(8,128)(2,1)S(1)}, u32[]{:S(2)}, u32[]{:S(2)}) %all-to-all-start.1) | async-done | bytes 786464 | tf_op jit(solution)/shard_map/all_to_all | solution.py:46
  241.9 5.3 %all-to-all-start.5 = ((bf16[8,384,128]{2,1,0:T(8,128)(2,1)}), bf16[8,384,128]{2,1,0:T(8,128)(2,1)S(1)}, u32[]{:S(2)}, u32[]{:S(2)}) async-start(bf16[8,384,128]{2,1,0:T(8,128)(2,1)} %broadcast_in_dim.18), calls=%async_computation.5 | async-start | bytes 1572864 | tf_op jit(solution)/shard_map/all_to_all | solution.py:46
  253.1 22.9 %all-to-all-done.5 = bf16[8,384,128]{2,1,0:T(8,128)(2,1)S(1)} async-done(((bf16[8,384,128]{2,1,0:T(8,128)(2,1)}), bf16[8,384,128]{2,1,0:T(8,128)(2,1)S(1)}, u32[]{:S(2)}, u32[]{:S(2)}) %all-to-all-start.5) | async-done | bytes 786464 | tf_op jit(solution)/shard_map/all_to_all | solution.py:46
  276.0 14.1 %collective-permute-start.13 = (bf16[8,384,128]{2,1,0:T(8,128)(2,1)S(1)}, bf16[8,384,128]{2,1,0:T(8,128)(2,1)}, u32[]{:S(2)}, u32[]{:S(2)}) collective-permute-start(bf16[8,384,128]{2,1,0:T(8,128)(2,1)S(1)} %all-to-all-done.5), channel_id=1, source_target_pairs={{0,1},{1,0},{2,3},{3,2},{4,5},{5,4},{6,7},{7,6},{8,9},{9,8},{10,11... | collective-permute-start | bytes 2359304 | tf_op jit(solution)/shard_map/ppermute | solution.py:118
  294.1 5.5 %all-to-all-start.2 = ((bf16[16,48,224]{2,1,0:T(8,128)(2,1)}), bf16[16,48,224]{2,1,0:T(8,128)(2,1)S(1)}, u32[]{:S(2)}, u32[]{:S(2)}) async-start(bf16[16,48,224]{2,1,0:T(8,128)(2,1)} %bitcast.7), calls=%async_computation.2 | async-start | bytes 786432 | tf_op jit(solution)/shard_map/all_to_all | solution.py:122
  302.7 6.5 %all-to-all-done.2 = bf16[16,48,224]{2,1,0:T(8,128)(2,1)S(1)} async-done(((bf16[16,48,224]{2,1,0:T(8,128)(2,1)}), bf16[16,48,224]{2,1,0:T(8,128)(2,1)S(1)}, u32[]{:S(2)}, u32[]{:S(2)}) %all-to-all-start.2) | async-done | bytes 344096 | tf_op jit(solution)/shard_map/all_to_all | solution.py:122
  313.0 3.9 %gather_fusion.1 = bf16[1024,224]{1,0:T(8,128)(2,1)S(1)} fusion(bf16[769,224]{1,0:T(8,128)(2,1)S(1)} %concatenate.28, s32[1024]{0:T(1024)S(1)} %broadcast_clamp_fusion.1), kind=kCustom, calls=%fused_computation.1 | custom fusion | bytes 921600 | tf_op jit(solution)/shard_map/gather | solution.py:68
  317.0 4.5 %all-to-all-done.6 = bf16[16,48,224]{2,1,0:T(8,128)(2,1)S(1)} async-done(((bf16[16,48,224]{2,1,0:T(8,128)(2,1)}), bf16[16,48,224]{2,1,0:T(8,128)(2,1)S(1)}, u32[]{:S(2)}, u32[]{:S(2)}) %all-to-all-start.6) | async-done | bytes 344096 | tf_op jit(solution)/shard_map/all_to_all | solution.py:122
  328.9 12.0 %collective-permute-done.15 = f32[128,224]{1,0:T(8,128)S(1)} collective-permute-done((f32[128,224]{1,0:T(8,128)S(1)}, f32[128,224]{1,0:T(8,128)S(1)}, u32[]{:S(2)}, u32[]{:S(2)}) %collective-permute-start.15) | collective-permute-done | bytes 114720 | tf_op jit(solution)/shard_map/ppermute | solution.py:132
  (133 shorter events, 78.5 us)
Async XLA Ops:
  0.6 37.6 %collective-permute-start.11 = (s32[128,8]{0,1:T(8,128)}, s32[128,8]{0,1:T(8,128)S(1)}, u32[]{:S(2)}, u32[]{:S(2)}) collective-permute-start(s32[128,8]{0,1:T(8,128)} %param.7), channel_id=1, source_target_pairs={{0,78},{2,76},{4,74},{6,72},{8,70},{10,68},{12,66},{14,64},{64,14}... | collective-permute-start | bytes 12296 | tf_op jit(solution)/shard_map/ppermute | solution.py:89
  12.8 6.2 %collective-permute-start.10 = (bf16[128,224]{1,0:T(8,128)(2,1)S(1)}, bf16[128,224]{1,0:T(8,128)(2,1)S(1)}, u32[]{:S(2)}, u32[]{:S(2)}) collective-permute-start(bf16[128,224]{1,0:T(8,128)(2,1)S(1)} %constant_dynamic-slice_fusion.2), channel_id=1, source_target_pairs={{0,78},{2,76},{4,74},{6,72},{8,70},{10,68},{12,66},{14,64},{64,14}... | collective-permute-start | bytes 172040 | tf_op jit(solution)/shard_map/ppermute | solution.py:89
  20.0 31.8 %all-to-all-start.3 = ((bf16[8,128,224]{1,2,0:T(8,128)(2,1)}), bf16[8,128,224]{1,2,0:T(8,128)(2,1)S(1)}, u32[]{:S(2)}, u32[]{:S(2)}) async-start(bf16[8,128,224]{1,2,0:T(8,128)(2,1)} %broadcast_in_dim.17), calls=%async_computation.3 | async-start | bytes 917504 | tf_op jit(solution)/shard_map/all_to_all | solution.py:46
  51.8 73.0 %all-to-all-start = ((bf16[16,48,1792]{2,1,0:T(8,128)(2,1)}), bf16[16,48,1792]{2,1,0:T(8,128)(2,1)}, u32[]{:S(2)}, u32[]{:S(2)}) async-start(bf16[16,48,1792]{2,1,0:T(8,128)(2,1)} %bitcast.50), calls=%async_computation | async-start | bytes 5505024 | tf_op jit(solution)/shard_map/all_to_all | solution.py:107
  59.4 35.2 %collective-permute-start.4 = (bf16[1,512,224]{1,2,0:T(8,128)(2,1)}, bf16[1,512,224]{1,2,0:T(8,128)(2,1)S(1)}, u32[]{:S(2)}, u32[]{:S(2)}) collective-permute-start(bf16[1,512,224]{1,2,0:T(8,128)(2,1)} %slice.26), channel_id=1, source_target_pairs={{0,16},{16,32},{32,48},{48,0},{1,17},{17,33},{33,49},{49,1},{2,18}... | collective-permute-start | bytes 688136 | tf_op jit(solution)/shard_map/ppermute | solution.py:23
  63.5 42.7 %collective-permute-start = (bf16[1,1,896,256]{3,2,1,0:T(8,128)(2,1)}, bf16[1,1,896,256]{3,2,1,0:T(8,128)(2,1)S(1)}, u32[]{:S(2)}, u32[]{:S(2)}) collective-permute-start(bf16[1,1,896,256]{3,2,1,0:T(8,128)(2,1)} %slice.24), channel_id=1, source_target_pairs={{0,16},{16,32},{32,48},{48,0},{1,17},{17,33},{33,49},{49,1},{2,18}... | collective-permute-start | bytes 1376264 | tf_op jit(solution)/shard_map/ppermute | solution.py:23
  95.3 17.2 %collective-permute-start.6 = (bf16[1,512,224]{1,2,0:T(8,128)(2,1)S(1)}, bf16[1,512,224]{1,2,0:T(8,128)(2,1)S(1)}, u32[]{:S(2)}, u32[]{:S(2)}) collective-permute-start(bf16[1,512,224]{1,2,0:T(8,128)(2,1)S(1)} %get-tuple-element.22), channel_id=1, source_target_pairs={{0,48},{16,0},{32,16},{48,32},{1,49},{17,1},{33,17},{49,33},{2,50}... | collective-permute-start | bytes 688136 | tf_op jit(solution)/shard_map/ppermute | solution.py:24
  107.2 24.1 %collective-permute-start.2 = (bf16[1,1,896,256]{3,2,1,0:T(8,128)(2,1)}, bf16[1,1,896,256]{3,2,1,0:T(8,128)(2,1)}, u32[]{:S(2)}, u32[]{:S(2)}) collective-permute-start(bf16[1,1,896,256]{3,2,1,0:T(8,128)(2,1)} %get-tuple-element.20), channel_id=1, source_target_pairs={{0,48},{16,0},{32,16},{48,32},{1,49},{17,1},{33,17},{49,33},{2,50}... | collective-permute-start | bytes 1376264 | tf_op jit(solution)/shard_map/ppermute | solution.py:24
  109.1 27.5 %collective-permute-start.5 = (bf16[1,512,224]{1,2,0:T(8,128)(2,1)}, bf16[1,512,224]{1,2,0:T(8,128)(2,1)}, u32[]{:S(2)}, u32[]{:S(2)}) collective-permute-start(bf16[1,512,224]{1,2,0:T(8,128)(2,1)} %get-tuple-element.21), channel_id=1, source_target_pairs={{0,16},{16,32},{32,48},{48,0},{1,17},{17,33},{33,49},{49,1},{2,18}... | collective-permute-start | bytes 688136 | tf_op jit(solution)/shard_map/ppermute | solution.py:32
  113.3 23.3 %collective-permute-start.7 = (bf16[1,512,224]{1,2,0:T(8,128)(2,1)}, bf16[1,512,224]{1,2,0:T(8,128)(2,1)}, u32[]{:S(2)}, u32[]{:S(2)}) collective-permute-start(bf16[1,512,224]{1,2,0:T(8,128)(2,1)} %broadcast_select_fusion.2), channel_id=1, source_target_pairs={{0,48},{16,0},{32,16},{48,32},{1,49},{17,1},{33,17},{49,33},{2,50}... | collective-permute-start | bytes 688136 | tf_op jit(solution)/shard_map/ppermute | solution.py:33
  116.4 22.1 %collective-permute-start.1 = (bf16[1,1,896,256]{3,2,1,0:T(8,128)(2,1)}, bf16[1,1,896,256]{3,2,1,0:T(8,128)(2,1)}, u32[]{:S(2)}, u32[]{:S(2)}) collective-permute-start(bf16[1,1,896,256]{3,2,1,0:T(8,128)(2,1)} %get-tuple-element.19), channel_id=1, source_target_pairs={{0,16},{16,32},{32,48},{48,0},{1,17},{17,33},{33,49},{49,1},{2,18}... | collective-permute-start | bytes 1376264 | tf_op jit(solution)/shard_map/ppermute | solution.py:32
  124.8 59.5 %all-to-all-start.4 = ((bf16[16,48,1792]{2,1,0:T(8,128)(2,1)}), bf16[16,48,1792]{2,1,0:T(8,128)(2,1)}, u32[]{:S(2)}, u32[]{:S(2)}) async-start(bf16[16,48,1792]{2,1,0:T(8,128)(2,1)} %bitcast.51), calls=%async_computation.4 | async-start | bytes 5505024 | tf_op jit(solution)/shard_map/all_to_all | solution.py:107
  132.1 38.7 %collective-permute-start.3 = (bf16[1,1,896,256]{3,2,1,0:T(8,128)(2,1)}, bf16[1,1,896,256]{3,2,1,0:T(8,128)(2,1)}, u32[]{:S(2)}, u32[]{:S(2)}) collective-permute-start(bf16[1,1,896,256]{3,2,1,0:T(8,128)(2,1)} %broadcast_select_fusion), channel_id=1, source_target_pairs={{0,48},{16,0},{32,16},{48,32},{1,49},{17,1},{33,17},{49,33},{2,50}... | collective-permute-start | bytes 1376264 | tf_op jit(solution)/shard_map/ppermute | solution.py:33
  176.6 7.5 %collective-permute-start.8 = (f32[384,256]{1,0:T(8,128)}, f32[384,256]{1,0:T(8,128)S(1)}, u32[]{:S(2)}, u32[]{:S(2)}) collective-permute-start(f32[384,256]{1,0:T(8,128)} %constant_dynamic-slice_fusion.3), channel_id=1, source_target_pairs={{0,1},{1,0},{2,3},{3,2},{4,5},{5,4},{6,7},{7,6},{8,9},{9,8},{10,11... | collective-permute-start | bytes 1179656 | tf_op jit(solution)/shard_map/ppermute | solution.py:115
  185.3 55.6 %all-to-all-start.1 = ((bf16[8,384,128]{2,1,0:T(8,128)(2,1)}), bf16[8,384,128]{2,1,0:T(8,128)(2,1)S(1)}, u32[]{:S(2)}, u32[]{:S(2)}) async-start(bf16[8,384,128]{2,1,0:T(8,128)(2,1)} %broadcast_in_dim.15), calls=%async_computation.1 | async-start | bytes 1572864 | tf_op jit(solution)/shard_map/all_to_all | solution.py:46
  204.4 45.5 %copy-start.8 = (f32[128,8]{0,1:T(8,128)S(1)}, f32[128,8]{0,1:T(8,128)}, u32[]{:S(2)}) copy-start(f32[128,8]{0,1:T(8,128)} %param.8) | copy-start | bytes 12292
  204.5 3.9 %collective-permute-start.12 = (f32[384,256]{1,0:T(8,128)S(1)}, f32[384,256]{1,0:T(8,128)S(1)}, u32[]{:S(2)}, u32[]{:S(2)}) collective-permute-start(f32[384,256]{1,0:T(8,128)S(1)} %constant_dynamic-slice_fusion), channel_id=1, source_target_pairs={{0,1},{1,0},{2,3},{3,2},{4,5},{5,4},{6,7},{7,6},{8,9},{9,8},{10,11... | collective-permute-start | bytes 1179656 | tf_op jit(solution)/shard_map/ppermute | solution.py:115
  241.9 34.1 %all-to-all-start.5 = ((bf16[8,384,128]{2,1,0:T(8,128)(2,1)}), bf16[8,384,128]{2,1,0:T(8,128)(2,1)S(1)}, u32[]{:S(2)}, u32[]{:S(2)}) async-start(bf16[8,384,128]{2,1,0:T(8,128)(2,1)} %broadcast_in_dim.18), calls=%async_computation.5 | async-start | bytes 1572864 | tf_op jit(solution)/shard_map/all_to_all | solution.py:46
  247.2 43.9 %collective-permute-start.9 = (bf16[8,384,128]{2,1,0:T(8,128)(2,1)S(1)}, bf16[8,384,128]{2,1,0:T(8,128)(2,1)}, u32[]{:S(2)}, u32[]{:S(2)}) collective-permute-start(bf16[8,384,128]{2,1,0:T(8,128)(2,1)S(1)} %all-to-all-done.1), channel_id=1, source_target_pairs={{0,1},{1,0},{2,3},{3,2},{4,5},{5,4},{6,7},{7,6},{8,9},{9,8},{10,11... | collective-permute-start | bytes 2359304 | tf_op jit(solution)/shard_map/ppermute | solution.py:118
  249.9 62.9 %collective-permute-start.14 = (f32[128,8]{0,1:T(8,128)S(1)}, f32[128,8]{0,1:T(8,128)S(1)}, u32[]{:S(2)}, u32[]{:S(2)}) collective-permute-start(f32[128,8]{0,1:T(8,128)S(1)} %copy-done.8), channel_id=1, source_target_pairs={{0,78},{2,76},{4,74},{6,72},{8,70},{10,68},{12,66},{14,64},{64,14}... | collective-permute-start | bytes 12296 | tf_op jit(solution)/shard_map/ppermute | solution.py:89
  276.0 23.7 %collective-permute-start.13 = (bf16[8,384,128]{2,1,0:T(8,128)(2,1)S(1)}, bf16[8,384,128]{2,1,0:T(8,128)(2,1)}, u32[]{:S(2)}, u32[]{:S(2)}) collective-permute-start(bf16[8,384,128]{2,1,0:T(8,128)(2,1)S(1)} %all-to-all-done.5), channel_id=1, source_target_pairs={{0,1},{1,0},{2,3},{3,2},{4,5},{5,4},{6,7},{7,6},{8,9},{9,8},{10,11... | collective-permute-start | bytes 2359304 | tf_op jit(solution)/shard_map/ppermute | solution.py:118
  294.1 15.1 %all-to-all-start.2 = ((bf16[16,48,224]{2,1,0:T(8,128)(2,1)}), bf16[16,48,224]{2,1,0:T(8,128)(2,1)S(1)}, u32[]{:S(2)}, u32[]{:S(2)}) async-start(bf16[16,48,224]{2,1,0:T(8,128)(2,1)} %bitcast.7), calls=%async_computation.2 | async-start | bytes 786432 | tf_op jit(solution)/shard_map/all_to_all | solution.py:122
  309.3 12.3 %all-to-all-start.6 = ((bf16[16,48,224]{2,1,0:T(8,128)(2,1)}), bf16[16,48,224]{2,1,0:T(8,128)(2,1)S(1)}, u32[]{:S(2)}, u32[]{:S(2)}) async-start(bf16[16,48,224]{2,1,0:T(8,128)(2,1)} %bitcast.18), calls=%async_computation.6 | async-start | bytes 786432 | tf_op jit(solution)/shard_map/all_to_all | solution.py:122
  325.9 15.0 %collective-permute-start.15 = (f32[128,224]{1,0:T(8,128)S(1)}, f32[128,224]{1,0:T(8,128)S(1)}, u32[]{:S(2)}, u32[]{:S(2)}) collective-permute-start(f32[128,224]{1,0:T(8,128)S(1)} %fusion.4), channel_id=1, source_target_pairs={{0,64},{64,0},{1,65},{65,1},{2,66},{66,2},{3,67},{67,3},{4,68},{68... | collective-permute-start | bytes 344072 | tf_op jit(solution)/shard_map/ppermute | solution.py:132
  (9 other events, 117.2 us)

commit v6 on v3

--- a/solution.py
+++ b/solution.py
@@ -63,7 +63,7 @@
     return jnp.sum(chosen.astype(jnp.float32) * weights[:, :, None], axis=1)
 
 
-def run_layer(tokens, expert_ids, route_weights, gate_up, down):
+def run_layer(tokens, expert_ids, route_weights, gate_up, down, swap_in):
     rows_y, rows_x = lax.axis_size("y"), lax.axis_size("x")
     lines = rows_y * rows_x
     expert_count = 2 * lines
@@ -75,17 +75,18 @@
     side = lax.axis_index("core")
     zhi = lax.axis_index("zhi")
     own_half = lax.dynamic_slice_in_dim(tokens, side * half_width, half_width, 1)
-    far_half, far_ids, far_weights = lax.ppermute((own_half, expert_ids, route_weights), "zhi", FLIP)
+    mirror = [(high * chunks + low, (1 - high) * chunks + chunks - 1 - low) for high in range(2) for low in range(chunks)]
+    far_half, far_ids, far_weights = lax.ppermute((own_half, expert_ids, route_weights), ("zhi", "zlo"), mirror)
     own_slots, own_source = routing(expert_ids, expert_count, capacity)
     far_slots, far_source = routing(far_ids, expert_count, capacity)
 
-    def outgoing(rows, source):
+    def dispatch(rows, source):
         near = lax.dynamic_index_in_dim(source.reshape(rows_y, 2, rows_x, capacity), zhi, 1, keepdims=False)
         padded = jnp.concatenate([rows, jnp.zeros((1, half_width), rows.dtype)], axis=0)
-        return padded[near.reshape(-1)].reshape(lines, 1, capacity, half_width)
+        sent = padded[near.reshape(-1)].reshape(lines, capacity, half_width)
+        return lax.all_to_all(sent, ("y", "x"), 0, 0, tiled=True)
 
-    sent = jnp.concatenate([outgoing(own_half, own_source), outgoing(far_half, far_source)], axis=1)
-    arrived = lax.all_to_all(sent, ("y", "x"), 0, 0, tiled=True)
+    arrived = jnp.stack([dispatch(own_half, own_source), dispatch(far_half, far_source)], axis=0)
     total_rows = lines * 2 * capacity
     half_rows = total_rows // 2
     partial_value = jnp.dot(arrived.reshape(total_rows, half_width), gate_up, preferred_element_type=jnp.float32)
@@ -94,7 +95,10 @@
     summed = mine + lax.ppermute(other, "core", FLIP)
     block_units = gate_up.shape[1] // 2
     hidden = (jax.nn.silu(summed[:, :block_units]) * summed[:, block_units:]).astype(jnp.bfloat16)
+    hidden, swap_in = lax.optimization_barrier((hidden, swap_in))
+    swapped = swap_panels(*swap_in)
     gathered = lax.all_gather(hidden, "zlo", axis=0, tiled=False)
+    gathered, swapped = lax.optimization_barrier((gathered, swapped))
     partner_part = lax.ppermute(gathered, "core", FLIP)
     keep_first = side == 0
     first_hidden = jnp.where(keep_first, gathered, partner_part)
@@ -107,18 +111,21 @@
         return value.astype(jnp.bfloat16)
 
     expert_out = jnp.concatenate([project(first_hidden), project(second_hidden)], axis=0)
-    returned = lax.all_to_all(expert_out.reshape(lines, 2, capacity, out_columns), ("y", "x"), 0, 0, tiled=True)
+    by_line = jnp.transpose(expert_out.reshape(2, lines, capacity, out_columns), (1, 0, 2, 3))
+    returned = lax.all_to_all(by_line, ("y", "x"), 0, 0, tiled=True)
     own_table = returned[:, 0].reshape(lines * capacity, out_columns)
     far_table = returned[:, 1].reshape(lines * capacity, out_columns)
     far_sum = combine(far_table, far_ids, far_slots, far_weights, zhi, rows_x, capacity)
     own_sum = combine(own_table, expert_ids, own_slots, route_weights, zhi, rows_x, capacity)
     mixed = own_sum + lax.ppermute(far_sum, "zhi", FLIP)
-    return mixed.astype(jnp.bfloat16)
+    return mixed.astype(jnp.bfloat16), swapped
 
 
 def per_device(tokens, expert_ids, route_weights, gate_up_panels, down_panels, partner):
-    moe_out = run_layer(tokens, expert_ids, route_weights, gate_up_panels[0, 0], down_panels[0])
-    new_gate_up, new_down = swap_panels(gate_up_panels, down_panels, partner)
+    moe_out, (new_gate_up, new_down) = run_layer(
+        tokens, expert_ids, route_weights, gate_up_panels[0, 0], down_panels[0],
+        (gate_up_panels, down_panels, partner),
+    )
     return (moe_out, new_gate_up, new_down)
 
 

time: 333 us -> 271 us (0.81)
  waiting for transfers between devices: 175 us -> 125 us
  matrix products: 8.07 us -> 4.47 us
    all_gather x1, waiting for transfers between devices: 63 us -> 4.59 us  [run_layer(): gathered = lax.all_gather(hidden, 'zlo', axis=0, tiled=False)]
    all_to_all x2 -> x3, waiting for transfers between devices: 86.4 us -> 47.3 us  [the longest x2 35.2 us: dispatch(): return lax.all_to_all(sent, ('y', 'x'), 0, 0, tiled=True)]
    ppermute x3, waiting for transfers between devices: 7.51 us -> 41.4 us  [run_layer(): lax.ppermute((own_half, expert_ids, route_weights), ('zhi', 'zlo'), mirror)]
    ppermute x2, waiting for transfers between devices: 0.01 us -> 12.2 us  [swap_panels(): from_behind = lax.ppermute(first, 'x', ahead)]
    all_to_all x2 -> x3, starting transfers between devices: 11.9 us -> 19.9 us  [the longest x2 13.2 us: dispatch(): return lax.all_to_all(sent, ('y', 'x'), 0, 0, tiled=True)]
    ppermute x2, waiting for transfers between devices: 7.41 us -> 1.6 us  [swap_panels(): from_ahead = lax.ppermute(second, 'x', behind)]
    ppermute x3, starting transfers between devices: 24.5 us -> 18.8 us  [run_layer(): lax.ppermute((own_half, expert_ids, route_weights), ('zhi', 'zlo'), mirror)]
    concatenate x1 -> x0, other arithmetic: 5.51 us -> none  [run_layer(): jnp.concatenate([outgoing(own_half, own_source), outgoing(far_half, far_s...]
  transfers between devices with their start and end apart: 17 -> 18, of which waited for: 7 -> 12; matrix products, arithmetic and copies ran while one was open for 11% -> 11% of each run, Pallas kernels for 0% -> 0%
where the time goes in v6:
time: 271 us
  waiting for transfers between devices  125 us (46%)
  starting transfers between devices  77.8 us (29%)
  local copies, waits for them, and re-layouts  32.2 us (12%)
  other arithmetic  16.1 us (6%)
  between operations  15.3 us (6%)
  matrix products  4.47 us (2%)
    ppermute x3, waiting for transfers between devices, run_layer(): lax.ppermute((own_half, expert_ids, route_weights), ('zhi', 'zlo'), mirror)  41.4 us
    all_to_all x2, waiting for transfers between devices, dispatch(): return lax.all_to_all(sent, ('y', 'x'), 0, 0, tiled=True)  35.2 us
    ppermute x3, starting transfers between devices, run_layer(): lax.ppermute((own_half, expert_ids, route_weights), ('zhi', 'zlo'), mirror)  18.8 us
    all_to_all x2, starting transfers between devices, dispatch(): return lax.all_to_all(sent, ('y', 'x'), 0, 0, tiled=True)  13.2 us
    ppermute x2, waiting for transfers between devices, swap_panels(): from_behind = lax.ppermute(first, 'x', ahead)  12.2 us
    all_to_all x1, waiting for transfers between devices, run_layer(): returned = lax.all_to_all(by_line, ('y', 'x'), 0, 0, tiled=True)  12.1 us
    scatter x2, local copies, waits for them, and re-layouts, routing(): jnp.full((expert_count * capacity,), token_rows, jnp.int32).at[place]  8.63 us
    ppermute x1, starting transfers between devices, run_layer(): partner_part = lax.ppermute(gathered, 'core', FLIP)  8.53 us
  transfers between devices with their start and end apart: 18, of which 12 were waited for; matrix products, arithmetic and copies ran while one was open for 11% of the time, Pallas kernels for 0%

profile of v6, /device:TPU:1, one launch (start us, length us, event | category | flops | bytes accessed | tf_op | source)
XLA Modules:
  0.0 270.5 jit_solution(11842191290090919560)
XLA Ops:
  7.2 12.1 %collective-permute-start.1 = (s32[128,8]{0,1:T(8,128)}, s32[128,8]{0,1:T(8,128)S(1)}, u32[]{:S(2)}, u32[]{:S(2)}) collective-permute-start(s32[128,8]{0,1:T(8,128)} %param.7), channel_id=1, source_target_pairs={{0,78},{2,76},{4,74},{6,72},{8,70},{10,68},{12,66},{14,64},{64,14}... | collective-permute-start | bytes 12296 | tf_op jit(solution)/shard_map/ppermute | solution.py:79
  22.1 4.3 %scatter_custom_fusion = s32[1536]{0:T(1024)S(1)} fusion(s32[1024]{0:T(1024)S(1)} %bitcast.50, s32[1024]{0:T(1024)S(1)} %reshape.305, s32[]{:T(128)} %constant.114.clone.1), kind=kCustom, calls=%fused_computation.102 | custom fusion | bytes 6148 | tf_op jit(solution)/shard_map/scatter | solution.py:52
  27.3 4.3 %scatter_custom_fusion.1 = s32[1536]{0:T(1024)S(1)} fusion(s32[1024]{0:T(1024)S(1)} %bitcast.51, s32[1024]{0:T(1024)S(1)} %reshape.305, s32[]{:T(128)} %constant.114.clone.1), kind=kCustom, calls=%fused_computation.100 | custom fusion | bytes 6148 | tf_op jit(solution)/shard_map/scatter | solution.py:52
  31.8 4.1 %gather_fusion = bf16[768,1792]{1,0:T(8,128)(2,1)} fusion(bf16[129,1792]{1,0:T(8,128)(2,1)S(1)} %concatenate.21, s32[1024]{0:T(1024)S(1)} %pad_clamp_fusion.1), kind=kCustom, calls=%fused_computation | custom fusion | bytes 5508096 | tf_op jit(solution)/shard_map/gather | solution.py:86
  35.9 6.8 %all-to-all-start = ((bf16[16,48,1792]{2,1,0:T(8,128)(2,1)}), bf16[16,48,1792]{2,1,0:T(8,128)(2,1)}, u32[]{:S(2)}, u32[]{:S(2)}) async-start(bf16[16,48,1792]{2,1,0:T(8,128)(2,1)} %bitcast.39), calls=%async_computation | async-start | bytes 5505024 | tf_op jit(solution)/shard_map/all_to_all | solution.py:87
  44.7 41.4 %collective-permute-done = bf16[128,1792]{1,0:T(8,128)(2,1)S(1)} collective-permute-done((bf16[128,1792]{1,0:T(8,128)(2,1)S(1)}, bf16[128,1792]{1,0:T(8,128)(2,1)S(1)}, u32[]{:S(2)}, u32[]{:S(2)}) %collective-permute-start) | collective-permute-done | bytes 458784 | tf_op jit(solution)/shard_map/ppermute | solution.py:79
  86.2 4.1 %gather_fusion.1 = bf16[768,1792]{1,0:T(8,128)(2,1)} fusion(bf16[129,1792]{1,0:T(8,128)(2,1)S(1)} %concatenate.22, s32[1024]{0:T(1024)S(1)} %pad_clamp_fusion), kind=kCustom, calls=%fused_computation.1 | custom fusion | bytes 5508096 | tf_op jit(solution)/shard_map/gather | solution.py:86
  90.2 6.4 %all-to-all-start.1 = ((bf16[16,48,1792]{2,1,0:T(8,128)(2,1)}), bf16[16,48,1792]{2,1,0:T(8,128)(2,1)}, u32[]{:S(2)}, u32[]{:S(2)}) async-start(bf16[16,48,1792]{2,1,0:T(8,128)(2,1)} %bitcast.40), calls=%async_computation.1 | async-start | bytes 5505024 | tf_op jit(solution)/shard_map/all_to_all | solution.py:87
  96.7 35.2 %all-to-all-done.1 = bf16[16,48,1792]{2,1,0:T(8,128)(2,1)} async-done(((bf16[16,48,1792]{2,1,0:T(8,128)(2,1)}), bf16[16,48,1792]{2,1,0:T(8,128)(2,1)}, u32[]{:S(2)}, u32[]{:S(2)}) %all-to-all-start.1) | async-done | bytes 2752544 | tf_op jit(solution)/shard_map/all_to_all | solution.py:87
  131.9 3.2 %pad_maximum_fusion = bf16[2,16,48,1792]{3,2,1,0:T(8,128)(2,1)S(1)} fusion(bf16[1,16,48,1792]{3,2,1,0:T(8,128)(2,1)} %bitcast.5, bf16[1,16,48,1792]{3,2,1,0:T(8,128)(2,1)} %bitcast.2), kind=kLoop, calls=%fused_computation.6 | loop fusion | flops 2752512 | bytes 11010048 | tf_op jit(solution)/shard_map/stack | solution.py:89
  138.8 6.5 %collective-permute-start.2 = (f32[768,256]{1,0:T(8,128)}, f32[768,256]{1,0:T(8,128)S(1)}, u32[]{:S(2)}, u32[]{:S(2)}) collective-permute-start(f32[768,256]{1,0:T(8,128)} %constant_dynamic-slice_fusion), channel_id=1, source_target_pairs={{0,1},{1,0},{2,3},{3,2},{4,5},{5,4},{6,7},{7,6},{8,9},{9,8},{10,11... | collective-permute-start | bytes 2359304 | tf_op jit(solution)/shard_map/ppermute | solution.py:95
  155.3 4.9 %collective-permute-done.7 = bf16[1,512,224]{1,2,0:T(8,128)(2,1)S(1)} collective-permute-done((bf16[1,512,224]{1,2,0:T(8,128)(2,1)}, bf16[1,512,224]{1,2,0:T(8,128)(2,1)S(1)}, u32[]{:S(2)}, u32[]{:S(2)}) %collective-permute-start.7) | collective-permute-done | bytes 229408 | tf_op jit(solution)/shard_map/ppermute | solution.py:23
  162.9 7.3 %collective-permute-done.3 = bf16[1,1,896,256]{3,2,1,0:T(8,128)(2,1)S(1)} collective-permute-done((bf16[1,1,896,256]{3,2,1,0:T(8,128)(2,1)S(1)}, bf16[1,1,896,256]{3,2,1,0:T(8,128)(2,1)S(1)}, u32[]{:S(2)}, u32[]{:S(2)}) %collective-permute-start.3) | collective-permute-done | bytes 458784 | tf_op jit(solution)/shard_map/ppermute | solution.py:23
  172.9 3.4 %collective-permute-start.8 = (bf16[1,512,224]{1,2,0:T(8,128)(2,1)}, bf16[1,512,224]{1,2,0:T(8,128)(2,1)}, u32[]{:S(2)}, u32[]{:S(2)}) collective-permute-start(bf16[1,512,224]{1,2,0:T(8,128)(2,1)} %get-tuple-element.31), channel_id=1, source_target_pairs={{0,16},{16,32},{32,48},{48,0},{1,17},{17,33},{33,49},{49,1},{2,18}... | collective-permute-start | bytes 688136 | tf_op jit(solution)/shard_map/ppermute | solution.py:32
  184.8 3.4 %collective-permute-start.6 = (bf16[1,1,896,256]{3,2,1,0:T(8,128)(2,1)}, bf16[1,1,896,256]{3,2,1,0:T(8,128)(2,1)}, u32[]{:S(2)}, u32[]{:S(2)}) collective-permute-start(bf16[1,1,896,256]{3,2,1,0:T(8,128)(2,1)} %broadcast_select_fusion), channel_id=1, source_target_pairs={{0,48},{16,0},{32,16},{48,32},{1,49},{17,1},{33,17},{49,33},{2,50}... | collective-permute-start | bytes 1376264 | tf_op jit(solution)/shard_map/ppermute | solution.py:33
  199.4 4.6 %all-gather.3.cloned.1.call-done = bf16[6144,128]{1,0:T(8,128)(2,1)} async-done(((bf16[768,128]{1,0:T(8,128)(2,1)}), bf16[6144,128]{1,0:T(8,128)(2,1)}) %all-gather.3.cloned.1.call-update) | async-done | bytes 1572880 | tf_op jit(solution)/shard_map/all_gather | solution.py:100
  204.0 8.5 %collective-permute-start.11 = (bf16[8,768,128]{2,1,0:T(8,128)(2,1)}, bf16[8,768,128]{2,1,0:T(8,128)(2,1)}, u32[]{:S(2)}, u32[]{:S(2)}) collective-permute-start(bf16[8,768,128]{2,1,0:T(8,128)(2,1)} %bitcast.52), channel_id=1, source_target_pairs={{0,1},{1,0},{2,3},{3,2},{4,5},{5,4},{6,7},{7,6},{8,9},{9,8},{10,11... | collective-permute-start | bytes 4718600 | tf_op jit(solution)/shard_map/ppermute | solution.py:102
  212.6 4.8 %collective-permute-start.12 = (f32[128,8]{0,1:T(8,128)S(1)}, f32[128,8]{0,1:T(8,128)S(1)}, u32[]{:S(2)}, u32[]{:S(2)}) collective-permute-start(f32[128,8]{0,1:T(8,128)S(1)} %copy-done.5), channel_id=1, source_target_pairs={{0,78},{2,76},{4,74},{6,72},{8,70},{10,68},{12,66},{14,64},{64,14}... | collective-permute-start | bytes 12296 | tf_op jit(solution)/shard_map/ppermute | solution.py:79
  221.9 6.7 %all-to-all-start.2 = ((bf16[16,2,48,224]{3,2,1,0:T(8,128)(2,1)}), bf16[16,2,48,224]{3,2,1,0:T(8,128)(2,1)S(1)}, u32[]{:S(2)}, u32[]{:S(2)}) async-start(bf16[16,2,48,224]{3,2,1,0:T(8,128)(2,1)} %copy.63), calls=%async_computation.2 | async-start | bytes 1572864 | tf_op jit(solution)/shard_map/all_to_all | solution.py:115
  229.1 12.1 %all-to-all-done.2 = bf16[16,2,48,224]{3,2,1,0:T(8,128)(2,1)S(1)} async-done(((bf16[16,2,48,224]{3,2,1,0:T(8,128)(2,1)}), bf16[16,2,48,224]{3,2,1,0:T(8,128)(2,1)S(1)}, u32[]{:S(2)}, u32[]{:S(2)}) %all-to-all-start.2) | async-done | bytes 688160 | tf_op jit(solution)/shard_map/all_to_all | solution.py:115
  241.3 3.9 %gather_fusion.3 = bf16[1024,224]{1,0:T(8,128)(2,1)S(1)} fusion(bf16[769,224]{1,0:T(8,128)(2,1)S(1)} %concatenate.27, s32[1024]{0:T(1024)S(1)} %broadcast_clamp_fusion), kind=kCustom, calls=%fused_computation.3 | custom fusion | bytes 921600 | tf_op jit(solution)/shard_map/gather | solution.py:62
  245.6 4.4 %collective-permute-start.13 = (f32[128,224]{1,0:T(8,128)S(1)}, f32[128,224]{1,0:T(8,128)S(1)}, u32[]{:S(2)}, u32[]{:S(2)}) collective-permute-start(f32[128,224]{1,0:T(8,128)S(1)} %fusion.18), channel_id=1, source_target_pairs={{0,64},{64,0},{1,65},{65,1},{2,66},{66,2},{3,67},{67,3},{4,68},{68... | collective-permute-start | bytes 344072 | tf_op jit(solution)/shard_map/ppermute | solution.py:120
  250.1 3.9 %gather_fusion.2 = bf16[1024,224]{1,0:T(8,128)(2,1)S(1)} fusion(bf16[769,224]{1,0:T(8,128)(2,1)S(1)} %concatenate.26, s32[1024]{0:T(1024)S(1)} %broadcast_clamp_fusion.1), kind=kCustom, calls=%fused_computation.2 | custom fusion | bytes 921600 | tf_op jit(solution)/shard_map/gather | solution.py:62
  254.4 8.5 %collective-permute-done.13 = f32[128,224]{1,0:T(8,128)S(1)} collective-permute-done((f32[128,224]{1,0:T(8,128)S(1)}, f32[128,224]{1,0:T(8,128)S(1)}, u32[]{:S(2)}, u32[]{:S(2)}) %collective-permute-start.13) | collective-permute-done | bytes 114720 | tf_op jit(solution)/shard_map/ppermute | solution.py:120
  (108 shorter events, 50.5 us)
Async XLA Ops:
  7.2 14.8 %copy-start = (bf16[128,3584]{1,0:T(8,128)(2,1)S(1)}, bf16[128,3584]{1,0:T(8,128)(2,1)}, u32[]{:S(2)}) copy-start(bf16[128,3584]{1,0:T(8,128)(2,1)} %param.6) | copy-start | bytes 2752516
  7.2 19.4 %collective-permute-start.1 = (s32[128,8]{0,1:T(8,128)}, s32[128,8]{0,1:T(8,128)S(1)}, u32[]{:S(2)}, u32[]{:S(2)}) collective-permute-start(s32[128,8]{0,1:T(8,128)} %param.7), channel_id=1, source_target_pairs={{0,78},{2,76},{4,74},{6,72},{8,70},{10,68},{12,66},{14,64},{64,14}... | collective-permute-start | bytes 12296 | tf_op jit(solution)/shard_map/ppermute | solution.py:79
  35.9 54.4 %all-to-all-start = ((bf16[16,48,1792]{2,1,0:T(8,128)(2,1)}), bf16[16,48,1792]{2,1,0:T(8,128)(2,1)}, u32[]{:S(2)}, u32[]{:S(2)}) async-start(bf16[16,48,1792]{2,1,0:T(8,128)(2,1)} %bitcast.39), calls=%async_computation | async-start | bytes 5505024 | tf_op jit(solution)/shard_map/all_to_all | solution.py:87
  42.7 43.4 %collective-permute-start = (bf16[128,1792]{1,0:T(8,128)(2,1)S(1)}, bf16[128,1792]{1,0:T(8,128)(2,1)S(1)}, u32[]{:S(2)}, u32[]{:S(2)}) collective-permute-start(bf16[128,1792]{1,0:T(8,128)(2,1)S(1)} %constant_dynamic-slice_fusion.3), channel_id=1, source_target_pairs={{0,78},{2,76},{4,74},{6,72},{8,70},{10,68},{12,66},{14,64},{64,14}... | collective-permute-start | bytes 1376264 | tf_op jit(solution)/shard_map/ppermute | solution.py:79
  90.2 41.6 %all-to-all-start.1 = ((bf16[16,48,1792]{2,1,0:T(8,128)(2,1)}), bf16[16,48,1792]{2,1,0:T(8,128)(2,1)}, u32[]{:S(2)}, u32[]{:S(2)}) async-start(bf16[16,48,1792]{2,1,0:T(8,128)(2,1)} %bitcast.40), calls=%async_computation.1 | async-start | bytes 5505024 | tf_op jit(solution)/shard_map/all_to_all | solution.py:87
  96.6 107.4 %all-gather.3.cloned.1.call-start = ((), (), s32[]{:S(2)}) async-start(), calls=%async_computation.3 | async-start | bytes 1769472 | tf_op jit(solution)/shard_map/all_gather | solution.py:100
  131.9 3.2 %copy-start.1 = (bf16[1,1,1792,256]{3,2,1,0:T(8,128)(2,1)S(1)}, bf16[1,1,1792,256]{3,2,1,0:T(8,128)(2,1)}, u32[]{:S(2)}) copy-start(bf16[1,1,1792,256]{3,2,1,0:T(8,128)(2,1)} %param.9) | copy-start | bytes 2752516
  138.8 10.7 %copy-start.2 = (bf16[1,1024,224]{1,2,0:T(8,128)(2,1)S(1)}, bf16[1,1024,224]{1,2,0:T(8,128)(2,1)}, u32[]{:S(2)}) copy-start(bf16[1,1024,224]{1,2,0:T(8,128)(2,1)} %param.10) | copy-start | bytes 1376260
  138.8 8.6 %collective-permute-start.2 = (f32[768,256]{1,0:T(8,128)}, f32[768,256]{1,0:T(8,128)S(1)}, u32[]{:S(2)}, u32[]{:S(2)}) collective-permute-start(f32[768,256]{1,0:T(8,128)} %constant_dynamic-slice_fusion), channel_id=1, source_target_pairs={{0,1},{1,0},{2,3},{3,2},{4,5},{5,4},{6,7},{7,6},{8,9},{9,8},{10,11... | collective-permute-start | bytes 2359304 | tf_op jit(solution)/shard_map/ppermute | solution.py:95
  148.6 5.4 %copy-start.7 = (s32[32]{0:T(128)S(1)}, s32[32]{0:T(128)}, u32[]{:S(2)}) copy-start(s32[32]{0:T(128)} %param.11) | copy-start | bytes 388
  150.2 10.1 %collective-permute-start.7 = (bf16[1,512,224]{1,2,0:T(8,128)(2,1)}, bf16[1,512,224]{1,2,0:T(8,128)(2,1)S(1)}, u32[]{:S(2)}, u32[]{:S(2)}) collective-permute-start(bf16[1,512,224]{1,2,0:T(8,128)(2,1)} %slice.28), channel_id=1, source_target_pairs={{0,16},{16,32},{32,48},{48,0},{1,17},{17,33},{33,49},{49,1},{2,18}... | collective-permute-start | bytes 688136 | tf_op jit(solution)/shard_map/ppermute | solution.py:23
  152.1 18.1 %collective-permute-start.3 = (bf16[1,1,896,256]{3,2,1,0:T(8,128)(2,1)S(1)}, bf16[1,1,896,256]{3,2,1,0:T(8,128)(2,1)S(1)}, u32[]{:S(2)}, u32[]{:S(2)}) collective-permute-start(bf16[1,1,896,256]{3,2,1,0:T(8,128)(2,1)S(1)} %slice.26), channel_id=1, source_target_pairs={{0,16},{16,32},{32,48},{48,0},{1,17},{17,33},{33,49},{49,1},{2,18}... | collective-permute-start | bytes 1376264 | tf_op jit(solution)/shard_map/ppermute | solution.py:23
  161.0 15.3 %collective-permute-start.9 = (bf16[1,512,224]{1,2,0:T(8,128)(2,1)S(1)}, bf16[1,512,224]{1,2,0:T(8,128)(2,1)S(1)}, u32[]{:S(2)}, u32[]{:S(2)}) collective-permute-start(bf16[1,512,224]{1,2,0:T(8,128)(2,1)S(1)} %get-tuple-element.32), channel_id=1, source_target_pairs={{0,48},{16,0},{32,16},{48,32},{1,49},{17,1},{33,17},{49,33},{2,50}... | collective-permute-start | bytes 688136 | tf_op jit(solution)/shard_map/ppermute | solution.py:24
  171.0 12.9 %collective-permute-start.5 = (bf16[1,1,896,256]{3,2,1,0:T(8,128)(2,1)S(1)}, bf16[1,1,896,256]{3,2,1,0:T(8,128)(2,1)S(1)}, u32[]{:S(2)}, u32[]{:S(2)}) collective-permute-start(bf16[1,1,896,256]{3,2,1,0:T(8,128)(2,1)S(1)} %get-tuple-element.28), channel_id=1, source_target_pairs={{0,48},{16,0},{32,16},{48,32},{1,49},{17,1},{33,17},{49,33},{2,50}... | collective-permute-start | bytes 1376264 | tf_op jit(solution)/shard_map/ppermute | solution.py:24
  172.9 15.3 %collective-permute-start.8 = (bf16[1,512,224]{1,2,0:T(8,128)(2,1)}, bf16[1,512,224]{1,2,0:T(8,128)(2,1)}, u32[]{:S(2)}, u32[]{:S(2)}) collective-permute-start(bf16[1,512,224]{1,2,0:T(8,128)(2,1)} %get-tuple-element.31), channel_id=1, source_target_pairs={{0,16},{16,32},{32,48},{48,0},{1,17},{17,33},{33,49},{49,1},{2,18}... | collective-permute-start | bytes 688136 | tf_op jit(solution)/shard_map/ppermute | solution.py:32
  176.3 7.6 %copy-start.4 = (bf16[1,512,224]{1,2,0:T(8,128)(2,1)}, bf16[1,512,224]{1,2,0:T(8,128)(2,1)S(1)}, u32[]{:S(2)}) copy-start(bf16[1,512,224]{1,2,0:T(8,128)(2,1)S(1)} %collective-permute-done.9) | copy-start | bytes 688132
  177.1 11.8 %collective-permute-start.10 = (bf16[1,512,224]{1,2,0:T(8,128)(2,1)}, bf16[1,512,224]{1,2,0:T(8,128)(2,1)}, u32[]{:S(2)}, u32[]{:S(2)}) collective-permute-start(bf16[1,512,224]{1,2,0:T(8,128)(2,1)} %broadcast_select_fusion.2), channel_id=1, source_target_pairs={{0,48},{16,0},{32,16},{48,32},{1,49},{17,1},{33,17},{49,33},{2,50}... | collective-permute-start | bytes 688136 | tf_op jit(solution)/shard_map/ppermute | solution.py:33
  180.2 13.8 %collective-permute-start.4 = (bf16[1,1,896,256]{3,2,1,0:T(8,128)(2,1)}, bf16[1,1,896,256]{3,2,1,0:T(8,128)(2,1)}, u32[]{:S(2)}, u32[]{:S(2)}) collective-permute-start(bf16[1,1,896,256]{3,2,1,0:T(8,128)(2,1)} %get-tuple-element.27), channel_id=1, source_target_pairs={{0,16},{16,32},{32,48},{48,0},{1,17},{17,33},{33,49},{49,1},{2,18}... | collective-permute-start | bytes 1376264 | tf_op jit(solution)/shard_map/ppermute | solution.py:32
  184.8 12.4 %collective-permute-start.6 = (bf16[1,1,896,256]{3,2,1,0:T(8,128)(2,1)}, bf16[1,1,896,256]{3,2,1,0:T(8,128)(2,1)}, u32[]{:S(2)}, u32[]{:S(2)}) collective-permute-start(bf16[1,1,896,256]{3,2,1,0:T(8,128)(2,1)} %broadcast_select_fusion), channel_id=1, source_target_pairs={{0,48},{16,0},{32,16},{48,32},{1,49},{17,1},{33,17},{49,33},{2,50}... | collective-permute-start | bytes 1376264 | tf_op jit(solution)/shard_map/ppermute | solution.py:33
  198.4 14.1 %copy-start.5 = (f32[128,8]{0,1:T(8,128)S(1)}, f32[128,8]{0,1:T(8,128)}, u32[]{:S(2)}) copy-start(f32[128,8]{0,1:T(8,128)} %param.8) | copy-start | bytes 12292
  204.0 13.7 %collective-permute-start.11 = (bf16[8,768,128]{2,1,0:T(8,128)(2,1)}, bf16[8,768,128]{2,1,0:T(8,128)(2,1)}, u32[]{:S(2)}, u32[]{:S(2)}) collective-permute-start(bf16[8,768,128]{2,1,0:T(8,128)(2,1)} %bitcast.52), channel_id=1, source_target_pairs={{0,1},{1,0},{2,3},{3,2},{4,5},{5,4},{6,7},{7,6},{8,9},{9,8},{10,11... | collective-permute-start | bytes 4718600 | tf_op jit(solution)/shard_map/ppermute | solution.py:102
  212.6 16.4 %collective-permute-start.12 = (f32[128,8]{0,1:T(8,128)S(1)}, f32[128,8]{0,1:T(8,128)S(1)}, u32[]{:S(2)}, u32[]{:S(2)}) collective-permute-start(f32[128,8]{0,1:T(8,128)S(1)} %copy-done.5), channel_id=1, source_target_pairs={{0,78},{2,76},{4,74},{6,72},{8,70},{10,68},{12,66},{14,64},{64,14}... | collective-permute-start | bytes 12296 | tf_op jit(solution)/shard_map/ppermute | solution.py:79
  221.9 19.2 %all-to-all-start.2 = ((bf16[16,2,48,224]{3,2,1,0:T(8,128)(2,1)}), bf16[16,2,48,224]{3,2,1,0:T(8,128)(2,1)S(1)}, u32[]{:S(2)}, u32[]{:S(2)}) async-start(bf16[16,2,48,224]{3,2,1,0:T(8,128)(2,1)} %copy.63), calls=%async_computation.2 | async-start | bytes 1572864 | tf_op jit(solution)/shard_map/all_to_all | solution.py:115
  245.6 17.3 %collective-permute-start.13 = (f32[128,224]{1,0:T(8,128)S(1)}, f32[128,224]{1,0:T(8,128)S(1)}, u32[]{:S(2)}, u32[]{:S(2)}) collective-permute-start(f32[128,224]{1,0:T(8,128)S(1)} %fusion.18), channel_id=1, source_target_pairs={{0,64},{64,0},{1,65},{65,1},{2,66},{66,2},{3,67},{67,3},{4,68},{68... | collective-permute-start | bytes 344072 | tf_op jit(solution)/shard_map/ppermute | solution.py:120
  (2 other events, 3.4 us)
Sparse Core Ops, SparseCore 0:
  149.6 54.4 all-gather.2

commit v7 on v6

--- a/solution.py
+++ b/solution.py
@@ -15,28 +15,32 @@
     even = (lax.axis_index("x") & 1) == 0
     gate_rows = gate_up.shape[2] // 2
     down_rows = down.shape[1] // 2
-    first = (gate_up[:, :, :gate_rows], down[:, :down_rows])
-    second = (gate_up[:, :, gate_rows:], down[:, down_rows:])
+    lanes = gate_up.shape[3]
+    down_shape = (down.shape[0], down_rows, down.shape[2])
+
+    def pack(gate_part, down_part):
+        return jnp.concatenate([gate_part[0, 0], down_part.reshape(-1, lanes)], axis=0)
+
+    first = pack(gate_up[:, :, :gate_rows], down[:, :down_rows])
+    second = pack(gate_up[:, :, gate_rows:], down[:, down_rows:])
     ring = lax.axis_size("x")
     ahead = [(i, (i + 1) % ring) for i in range(ring)]
     behind = [(i, (i + ring - 1) % ring) for i in range(ring)]
     from_behind = lax.ppermute(first, "x", ahead)
     from_ahead = lax.ppermute(second, "x", behind)
     is_two = kind == 2
-
-    def pick(flag, left, right):
-        return tuple(jnp.where(flag, l, r) for l, r in zip(left, right))
-
-    send_ahead = pick(is_two, from_behind, second)
-    send_behind = pick(is_two, from_ahead, first)
+    send_ahead = jnp.where(is_two, from_behind, second)
+    send_behind = jnp.where(is_two, from_ahead, first)
     got_behind = lax.ppermute(send_ahead, "x", ahead)
     got_ahead = lax.ppermute(send_behind, "x", behind)
     one_even = (kind == 1) & even
     one_odd = (kind == 1) & ~even
-    new_first = pick(is_two, got_behind, pick(one_even, got_ahead, pick(one_odd, from_behind, first)))
-    new_second = pick(is_two, got_ahead, pick(one_even, from_ahead, pick(one_odd, got_behind, second)))
-    new_gate_up = jnp.concatenate([new_first[0], new_second[0]], axis=2)
-    new_down = jnp.concatenate([new_first[1], new_second[1]], axis=1)
+    new_first = jnp.where(is_two, got_behind, jnp.where(one_even, got_ahead, jnp.where(one_odd, from_behind, first)))
+    new_second = jnp.where(is_two, got_ahead, jnp.where(one_even, from_ahead, jnp.where(one_odd, got_behind, second)))
+    new_gate_up = jnp.concatenate([new_first[:gate_rows], new_second[:gate_rows]], axis=0)[None, None]
+    new_down = jnp.concatenate(
+        [new_first[gate_rows:].reshape(down_shape), new_second[gate_rows:].reshape(down_shape)], axis=1
+    )
     return (new_gate_up, new_down)
 
 
@@ -82,9 +86,9 @@
 
     def dispatch(rows, source):
         near = lax.dynamic_index_in_dim(source.reshape(rows_y, 2, rows_x, capacity), zhi, 1, keepdims=False)
-        padded = jnp.concatenate([rows, jnp.zeros((1, half_width), rows.dtype)], axis=0)
-        sent = padded[near.reshape(-1)].reshape(lines, capacity, half_width)
-        return lax.all_to_all(sent, ("y", "x"), 0, 0, tiled=True)
+        pick = (near.reshape(-1, 1) == jnp.arange(token_rows, dtype=jnp.int32)[None, :]).astype(rows.dtype)
+        sent = jnp.dot(pick, rows, preferred_element_type=jnp.float32).astype(rows.dtype)
+        return lax.all_to_all(sent.reshape(lines, capacity, half_width), ("y", "x"), 0, 0, tiled=True)
 
     arrived = jnp.stack([dispatch(own_half, own_source), dispatch(far_half, far_source)], axis=0)
     total_rows = lines * 2 * capacity

time: 271 us -> 289 us (1.066)
  waiting for transfers between devices: 125 us -> 156 us
  starting transfers between devices: 77.8 us -> 67.7 us
  local copies, waits for them, and re-layouts: 32.2 us -> 25.2 us
  matrix products: 4.47 us -> 9.51 us
    all_gather x1, waiting for transfers between devices: 4.59 us -> 19.8 us  [run_layer(): gathered = lax.all_gather(hidden, 'zlo', axis=0, tiled=False)]
    ppermute x2 -> x1, waiting for transfers between devices: 1.6 us -> 12.7 us  [swap_panels(): from_ahead = lax.ppermute(second, 'x', behind)]
    ppermute x2 -> x1, waiting for transfers between devices: 3.78 us -> 13.9 us  [swap_panels(): got_ahead = lax.ppermute(send_behind, 'x', behind)]
    gather x2 -> x0, local copies, waits for them, and re-layouts: 8.13 us -> none  [dispatch(): sent = padded[near.reshape(-1)].reshape(lines, capacity, half_width)]
    ppermute x3, waiting for transfers between devices: 41.4 us -> 36.3 us  [run_layer(): lax.ppermute((own_half, expert_ids, route_weights), ('zhi', 'zlo'), mirror)]
    dot_general x0 -> x2, matrix products: none -> 5.01 us  [dispatch(): jnp.dot(pick, rows, preferred_element_type=jnp.float32).astype(rows.dtype)]
    ppermute x2 -> x1, waiting for transfers between devices: 12.2 us -> 16.1 us  [swap_panels(): from_behind = lax.ppermute(first, 'x', ahead)]
    ppermute x2 -> x1, starting transfers between devices: 6.52 us -> 3.29 us  [swap_panels(): got_ahead = lax.ppermute(send_behind, 'x', behind)]
  transfers between devices with their start and end apart: 18 -> 14, of which waited for: 12 -> 9; matrix products, arithmetic and copies ran while one was open for 11% -> 8% of each run, Pallas kernels for 0% -> 0%
where the time goes in v7:
time: 289 us; the launch traced here: 288 us
  waiting for transfers between devices  156 us (54%)
  starting transfers between devices  67.7 us (23%)
  local copies, waits for them, and re-layouts  25.2 us (9%)
  between operations  15.3 us (5%)
  other arithmetic  15 us (5%)
  matrix products  9.51 us (3%)
    ppermute x3, waiting for transfers between devices, run_layer(): lax.ppermute((own_half, expert_ids, route_weights), ('zhi', 'zlo'), mirror)  36.3 us
    all_to_all x2, waiting for transfers between devices, dispatch(): lax.all_to_all(sent.reshape(lines, capacity, half_width), ('y', 'x'), 0,...  35.2 us
    all_gather x1, waiting for transfers between devices, run_layer(): gathered = lax.all_gather(hidden, 'zlo', axis=0, tiled=False)  19.8 us
    ppermute x3, starting transfers between devices, run_layer(): lax.ppermute((own_half, expert_ids, route_weights), ('zhi', 'zlo'), mirror)  17.8 us
    ppermute x1, waiting for transfers between devices, swap_panels(): from_behind = lax.ppermute(first, 'x', ahead)  16.1 us
    all_to_all x2, starting transfers between devices, dispatch(): lax.all_to_all(sent.reshape(lines, capacity, half_width), ('y', 'x'), 0,...  14.1 us
    ppermute x1, waiting for transfers between devices, swap_panels(): got_ahead = lax.ppermute(send_behind, 'x', behind)  13.9 us
    ppermute x1, waiting for transfers between devices, swap_panels(): from_ahead = lax.ppermute(second, 'x', behind)  12.7 us
  transfers between devices with their start and end apart: 14, of which 9 were waited for; matrix products, arithmetic and copies ran while one was open for 8% of the time, Pallas kernels for 0%

profile of v7, /device:TPU:1, one launch (start us, length us, event | category | flops | bytes accessed | tf_op | source)
XLA Modules:
  0.0 288.4 jit_solution(2280237122918539586)
XLA Ops:
  10.1 4.3 %scatter_custom_fusion = s32[1536]{0:T(1024)S(1)} fusion(s32[1024]{0:T(1024)S(1)} %bitcast.59, s32[1024]{0:T(1024)S(1)} %reshape.245, s32[]{:T(128)} %constant.108.clone.1), kind=kCustom, calls=%fused_computation.102 | custom fusion | bytes 6148 | tf_op jit(solution)/shard_map/scatter | solution.py:56
  14.6 2.5 convolution_convert_fusion.1
  17.2 7.7 %all-to-all-start = ((bf16[16,48,1792]{2,1,0:T(8,128)(2,1)}), bf16[16,48,1792]{2,1,0:T(8,128)(2,1)}, u32[]{:S(2)}, u32[]{:S(2)}) async-start(bf16[16,48,1792]{2,1,0:T(8,128)(2,1)} %bitcast.47), calls=%async_computation | async-start | bytes 5505024 | tf_op jit(solution)/shard_map/all_to_all | solution.py:91
  24.9 11.1 %collective-permute-start = (s32[128,8]{0,1:T(8,128)S(1)}, s32[128,8]{0,1:T(8,128)S(1)}, u32[]{:S(2)}, u32[]{:S(2)}) collective-permute-start(s32[128,8]{0,1:T(8,128)S(1)} %copy-done.6), channel_id=1, source_target_pairs={{0,78},{2,76},{4,74},{6,72},{8,70},{10,68},{12,66},{14,64},{64,14}... | collective-permute-start | bytes 12296 | tf_op jit(solution)/shard_map/ppermute | solution.py:83
  38.7 4.3 %scatter_custom_fusion.1 = s32[1536]{0:T(1024)S(1)} fusion(s32[1024]{0:T(1024)S(1)} %bitcast.58, s32[1024]{0:T(1024)S(1)} %reshape.245, s32[]{:T(128)} %constant.108.clone.1), kind=kCustom, calls=%fused_computation.100 | custom fusion | bytes 6148 | tf_op jit(solution)/shard_map/scatter | solution.py:56
  43.2 36.3 %collective-permute-done.1 = bf16[128,1792]{1,0:T(8,128)(2,1)S(1)} collective-permute-done((bf16[128,1792]{1,0:T(8,128)(2,1)S(1)}, bf16[128,1792]{1,0:T(8,128)(2,1)S(1)}, u32[]{:S(2)}, u32[]{:S(2)}) %collective-permute-start.1) | collective-permute-done | bytes 458784 | tf_op jit(solution)/shard_map/ppermute | solution.py:83
  82.0 6.4 %all-to-all-start.1 = ((bf16[16,48,1792]{2,1,0:T(8,128)(2,1)}), bf16[16,48,1792]{2,1,0:T(8,128)(2,1)}, u32[]{:S(2)}, u32[]{:S(2)}) async-start(bf16[16,48,1792]{2,1,0:T(8,128)(2,1)} %bitcast.48), calls=%async_computation.1 | async-start | bytes 5505024 | tf_op jit(solution)/shard_map/all_to_all | solution.py:91
  88.4 35.2 %all-to-all-done.1 = bf16[16,48,1792]{2,1,0:T(8,128)(2,1)} async-done(((bf16[16,48,1792]{2,1,0:T(8,128)(2,1)}), bf16[16,48,1792]{2,1,0:T(8,128)(2,1)}, u32[]{:S(2)}, u32[]{:S(2)}) %all-to-all-start.1) | async-done | bytes 2752544 | tf_op jit(solution)/shard_map/all_to_all | solution.py:91
  123.6 3.2 %pad_maximum_fusion = bf16[2,16,48,1792]{3,2,1,0:T(8,128)(2,1)S(1)} fusion(bf16[1,16,48,1792]{3,2,1,0:T(8,128)(2,1)} %bitcast.5, bf16[1,16,48,1792]{3,2,1,0:T(8,128)(2,1)} %bitcast.2), kind=kLoop, calls=%fused_computation.4 | loop fusion | flops 2752512 | bytes 11010048 | tf_op jit(solution)/shard_map/stack | solution.py:93
  129.4 6.3 %collective-permute-start.2 = (f32[768,256]{1,0:T(8,128)}, f32[768,256]{1,0:T(8,128)}, u32[]{:S(2)}, u32[]{:S(2)}) collective-permute-start(f32[768,256]{1,0:T(8,128)} %constant_dynamic-slice_fusion), channel_id=1, source_target_pairs={{0,1},{1,0},{2,3},{3,2},{4,5},{5,4},{6,7},{7,6},{8,9},{9,8},{10,11... | collective-permute-start | bytes 2359304 | tf_op jit(solution)/shard_map/ppermute | solution.py:99
  145.5 16.1 %collective-permute-done.3 = bf16[1344,256]{1,0:T(8,128)(2,1)S(1)} collective-permute-done((bf16[1344,256]{1,0:T(8,128)(2,1)}, bf16[1344,256]{1,0:T(8,128)(2,1)S(1)}, u32[]{:S(2)}, u32[]{:S(2)}) %collective-permute-start.3) | collective-permute-done | bytes 688160 | tf_op jit(solution)/shard_map/ppermute | solution.py:29
  164.8 3.4 %collective-permute-start.4 = (bf16[1344,256]{1,0:T(8,128)(2,1)}, bf16[1344,256]{1,0:T(8,128)(2,1)}, u32[]{:S(2)}, u32[]{:S(2)}) collective-permute-start(bf16[1344,256]{1,0:T(8,128)(2,1)} %get-tuple-element.32), channel_id=1, source_target_pairs={{0,16},{16,32},{32,48},{48,0},{1,17},{17,33},{33,49},{49,1},{2,18}... | collective-permute-start | bytes 2064392 | tf_op jit(solution)/shard_map/ppermute | solution.py:34
  168.2 12.7 %collective-permute-done.5 = bf16[1344,256]{1,0:T(8,128)(2,1)S(1)} collective-permute-done((bf16[1344,256]{1,0:T(8,128)(2,1)}, bf16[1344,256]{1,0:T(8,128)(2,1)S(1)}, u32[]{:S(2)}, u32[]{:S(2)}) %collective-permute-start.5) | collective-permute-done | bytes 688160 | tf_op jit(solution)/shard_map/ppermute | solution.py:30
  181.9 3.3 %collective-permute-start.6 = (bf16[1344,256]{1,0:T(8,128)(2,1)}, bf16[1344,256]{1,0:T(8,128)(2,1)}, u32[]{:S(2)}, u32[]{:S(2)}) collective-permute-start(bf16[1344,256]{1,0:T(8,128)(2,1)} %broadcast_select_fusion), channel_id=1, source_target_pairs={{0,48},{16,0},{32,16},{48,32},{1,49},{17,1},{33,17},{49,33},{2,50}... | collective-permute-start | bytes 2064392 | tf_op jit(solution)/shard_map/ppermute | solution.py:35
  185.2 13.9 %collective-permute-done.6 = bf16[1344,256]{1,0:T(8,128)(2,1)} collective-permute-done((bf16[1344,256]{1,0:T(8,128)(2,1)}, bf16[1344,256]{1,0:T(8,128)(2,1)}, u32[]{:S(2)}, u32[]{:S(2)}) %collective-permute-start.6) | collective-permute-done | bytes 688160 | tf_op jit(solution)/shard_map/ppermute | solution.py:35
  203.0 19.8 %all-gather.3.cloned.1.call-done = bf16[6144,128]{1,0:T(8,128)(2,1)} async-done(((bf16[768,128]{1,0:T(8,128)(2,1)}), bf16[6144,128]{1,0:T(8,128)(2,1)}) %all-gather.3.cloned.1.call-update) | async-done | bytes 1572880 | tf_op jit(solution)/shard_map/all_gather | solution.py:104
  222.8 8.8 %collective-permute-start.7 = (bf16[8,768,128]{2,1,0:T(8,128)(2,1)}, bf16[8,768,128]{2,1,0:T(8,128)(2,1)}, u32[]{:S(2)}, u32[]{:S(2)}) collective-permute-start(bf16[8,768,128]{2,1,0:T(8,128)(2,1)} %bitcast.60), channel_id=1, source_target_pairs={{0,1},{1,0},{2,3},{3,2},{4,5},{5,4},{6,7},{7,6},{8,9},{9,8},{10,11... | collective-permute-start | bytes 4718600 | tf_op jit(solution)/shard_map/ppermute | solution.py:106
  231.6 4.8 %collective-permute-start.8 = (f32[128,8]{0,1:T(8,128)S(1)}, f32[128,8]{0,1:T(8,128)S(1)}, u32[]{:S(2)}, u32[]{:S(2)}) collective-permute-start(f32[128,8]{0,1:T(8,128)S(1)} %copy-done.7), channel_id=1, source_target_pairs={{0,78},{2,76},{4,74},{6,72},{8,70},{10,68},{12,66},{14,64},{64,14}... | collective-permute-start | bytes 12296 | tf_op jit(solution)/shard_map/ppermute | solution.py:83
  240.9 6.6 %all-to-all-start.2 = ((bf16[16,2,48,224]{3,2,1,0:T(8,128)(2,1)}), bf16[16,2,48,224]{3,2,1,0:T(8,128)(2,1)S(1)}, u32[]{:S(2)}, u32[]{:S(2)}) async-start(bf16[16,2,48,224]{3,2,1,0:T(8,128)(2,1)} %copy.62), calls=%async_computation.2 | async-start | bytes 1572864 | tf_op jit(solution)/shard_map/all_to_all | solution.py:119
  248.9 11.1 %all-to-all-done.2 = bf16[16,2,48,224]{3,2,1,0:T(8,128)(2,1)S(1)} async-done(((bf16[16,2,48,224]{3,2,1,0:T(8,128)(2,1)}), bf16[16,2,48,224]{3,2,1,0:T(8,128)(2,1)S(1)}, u32[]{:S(2)}, u32[]{:S(2)}) %all-to-all-start.2) | async-done | bytes 688160 | tf_op jit(solution)/shard_map/all_to_all | solution.py:119
  260.1 3.9 %gather_fusion.1 = bf16[1024,224]{1,0:T(8,128)(2,1)S(1)} fusion(bf16[769,224]{1,0:T(8,128)(2,1)S(1)} %concatenate.27, s32[1024]{0:T(1024)S(1)} %broadcast_clamp_fusion), kind=kCustom, calls=%fused_computation.1 | custom fusion | bytes 921600 | tf_op jit(solution)/shard_map/gather | solution.py:66
  264.5 3.6 %collective-permute-start.9 = (f32[128,224]{1,0:T(8,128)S(1)}, f32[128,224]{1,0:T(8,128)S(1)}, u32[]{:S(2)}, u32[]{:S(2)}) collective-permute-start(f32[128,224]{1,0:T(8,128)S(1)} %fusion.18), channel_id=1, source_target_pairs={{0,64},{64,0},{1,65},{65,1},{2,66},{66,2},{3,67},{67,3},{4,68},{68... | collective-permute-start | bytes 344072 | tf_op jit(solution)/shard_map/ppermute | solution.py:124
  268.1 3.9 %gather_fusion = bf16[1024,224]{1,0:T(8,128)(2,1)S(1)} fusion(bf16[769,224]{1,0:T(8,128)(2,1)S(1)} %concatenate.26, s32[1024]{0:T(1024)S(1)} %broadcast_clamp_fusion.1), kind=kCustom, calls=%fused_computation | custom fusion | bytes 921600 | tf_op jit(solution)/shard_map/gather | solution.py:66
  272.5 8.3 %collective-permute-done.9 = f32[128,224]{1,0:T(8,128)S(1)} collective-permute-done((f32[128,224]{1,0:T(8,128)S(1)}, f32[128,224]{1,0:T(8,128)S(1)}, u32[]{:S(2)}, u32[]{:S(2)}) %collective-permute-start.9) | collective-permute-done | bytes 114720 | tf_op jit(solution)/shard_map/ppermute | solution.py:124
  (108 shorter events, 35.5 us)
Async XLA Ops:
  7.2 7.4 %copy-start = (bf16[128,3584]{1,0:T(8,128)(2,1)S(1)}, bf16[128,3584]{1,0:T(8,128)(2,1)}, u32[]{:S(2)}) copy-start(bf16[128,3584]{1,0:T(8,128)(2,1)} %param.6) | copy-start | bytes 2752516
  17.2 7.8 %copy-start.6 = (s32[128,8]{0,1:T(8,128)S(1)}, s32[128,8]{0,1:T(8,128)}, u32[]{:S(2)}) copy-start(s32[128,8]{0,1:T(8,128)} %param.7) | copy-start | bytes 12292
  17.2 64.8 %all-to-all-start = ((bf16[16,48,1792]{2,1,0:T(8,128)(2,1)}), bf16[16,48,1792]{2,1,0:T(8,128)(2,1)}, u32[]{:S(2)}, u32[]{:S(2)}) async-start(bf16[16,48,1792]{2,1,0:T(8,128)(2,1)} %bitcast.47), calls=%async_computation | async-start | bytes 5505024 | tf_op jit(solution)/shard_map/all_to_all | solution.py:91
  24.9 13.1 %collective-permute-start = (s32[128,8]{0,1:T(8,128)S(1)}, s32[128,8]{0,1:T(8,128)S(1)}, u32[]{:S(2)}, u32[]{:S(2)}) collective-permute-start(s32[128,8]{0,1:T(8,128)S(1)} %copy-done.6), channel_id=1, source_target_pairs={{0,78},{2,76},{4,74},{6,72},{8,70},{10,68},{12,66},{14,64},{64,14}... | collective-permute-start | bytes 12296 | tf_op jit(solution)/shard_map/ppermute | solution.py:83
  36.1 43.4 %collective-permute-start.1 = (bf16[128,1792]{1,0:T(8,128)(2,1)S(1)}, bf16[128,1792]{1,0:T(8,128)(2,1)S(1)}, u32[]{:S(2)}, u32[]{:S(2)}) collective-permute-start(bf16[128,1792]{1,0:T(8,128)(2,1)S(1)} %constant_dynamic-slice_fusion.2), channel_id=1, source_target_pairs={{0,78},{2,76},{4,74},{6,72},{8,70},{10,68},{12,66},{14,64},{64,14}... | collective-permute-start | bytes 1376264 | tf_op jit(solution)/shard_map/ppermute | solution.py:83
  82.0 41.6 %all-to-all-start.1 = ((bf16[16,48,1792]{2,1,0:T(8,128)(2,1)}), bf16[16,48,1792]{2,1,0:T(8,128)(2,1)}, u32[]{:S(2)}, u32[]{:S(2)}) async-start(bf16[16,48,1792]{2,1,0:T(8,128)(2,1)} %bitcast.48), calls=%async_computation.1 | async-start | bytes 5505024 | tf_op jit(solution)/shard_map/all_to_all | solution.py:91
  88.4 134.4 %all-gather.3.cloned.1.call-start = ((), (), s32[]{:S(2)}) async-start(), calls=%async_computation.3 | async-start | bytes 1769472 | tf_op jit(solution)/shard_map/all_gather | solution.py:104
  123.6 3.2 %copy-start.4 = (bf16[1,1,1792,256]{3,2,1,0:T(8,128)(2,1)S(1)}, bf16[1,1,1792,256]{3,2,1,0:T(8,128)(2,1)}, u32[]{:S(2)}) copy-start(bf16[1,1,1792,256]{3,2,1,0:T(8,128)(2,1)} %param.9) | copy-start | bytes 2752516
  129.4 8.6 %collective-permute-start.2 = (f32[768,256]{1,0:T(8,128)}, f32[768,256]{1,0:T(8,128)}, u32[]{:S(2)}, u32[]{:S(2)}) collective-permute-start(f32[768,256]{1,0:T(8,128)} %constant_dynamic-slice_fusion), channel_id=1, source_target_pairs={{0,1},{1,0},{2,3},{3,2},{4,5},{5,4},{6,7},{7,6},{8,9},{9,8},{10,11... | collective-permute-start | bytes 2359304 | tf_op jit(solution)/shard_map/ppermute | solution.py:99
  135.8 4.3 %copy-start.2 = (bf16[1,1024,224]{1,2,0:T(8,128)(2,1)S(1)}, bf16[1,1024,224]{1,2,0:T(8,128)(2,1)}, u32[]{:S(2)}) copy-start(bf16[1,1024,224]{1,2,0:T(8,128)(2,1)} %param.10) | copy-start | bytes 1376260
  139.2 1.5 copy-start.5
  140.8 3.5 %copy-start.9 = (s32[32]{0:T(128)S(1)}, s32[32]{0:T(128)}, u32[]{:S(2)}) copy-start(s32[32]{0:T(128)} %param.11) | copy-start | bytes 388
  141.7 19.9 %collective-permute-start.3 = (bf16[1344,256]{1,0:T(8,128)(2,1)}, bf16[1344,256]{1,0:T(8,128)(2,1)S(1)}, u32[]{:S(2)}, u32[]{:S(2)}) collective-permute-start(bf16[1344,256]{1,0:T(8,128)(2,1)} %pad_maximum_fusion.1), channel_id=1, source_target_pairs={{0,16},{16,32},{32,48},{48,0},{1,17},{17,33},{33,49},{49,1},{2,18}... | collective-permute-start | bytes 2064392 | tf_op jit(solution)/shard_map/ppermute | solution.py:29
  144.3 18.6 %copy-start.1 = (bf16[448,256]{1,0:T(8,128)(2,1)}, bf16[448,256]{1,0:T(8,128)(2,1)S(1)}, u32[]{:S(2)}) copy-start(bf16[448,256]{1,0:T(8,128)(2,1)S(1)} %reshape.209) | copy-start | bytes 688132
  162.9 18.0 %collective-permute-start.5 = (bf16[1344,256]{1,0:T(8,128)(2,1)}, bf16[1344,256]{1,0:T(8,128)(2,1)S(1)}, u32[]{:S(2)}, u32[]{:S(2)}) collective-permute-start(bf16[1344,256]{1,0:T(8,128)(2,1)} %get-tuple-element.33), channel_id=1, source_target_pairs={{0,48},{16,0},{32,16},{48,32},{1,49},{17,1},{33,17},{49,33},{2,50}... | collective-permute-start | bytes 2064392 | tf_op jit(solution)/shard_map/ppermute | solution.py:30
  164.8 20.4 %collective-permute-start.4 = (bf16[1344,256]{1,0:T(8,128)(2,1)}, bf16[1344,256]{1,0:T(8,128)(2,1)}, u32[]{:S(2)}, u32[]{:S(2)}) collective-permute-start(bf16[1344,256]{1,0:T(8,128)(2,1)} %get-tuple-element.32), channel_id=1, source_target_pairs={{0,16},{16,32},{32,48},{48,0},{1,17},{17,33},{33,49},{49,1},{2,18}... | collective-permute-start | bytes 2064392 | tf_op jit(solution)/shard_map/ppermute | solution.py:34
  181.9 17.2 %collective-permute-start.6 = (bf16[1344,256]{1,0:T(8,128)(2,1)}, bf16[1344,256]{1,0:T(8,128)(2,1)}, u32[]{:S(2)}, u32[]{:S(2)}) collective-permute-start(bf16[1344,256]{1,0:T(8,128)(2,1)} %broadcast_select_fusion), channel_id=1, source_target_pairs={{0,48},{16,0},{32,16},{48,32},{1,49},{17,1},{33,17},{49,33},{2,50}... | collective-permute-start | bytes 2064392 | tf_op jit(solution)/shard_map/ppermute | solution.py:35
  201.5 30.1 %copy-start.7 = (f32[128,8]{0,1:T(8,128)S(1)}, f32[128,8]{0,1:T(8,128)}, u32[]{:S(2)}) copy-start(f32[128,8]{0,1:T(8,128)} %param.8) | copy-start | bytes 12292
  201.5 34.8 %copy-start.3 = (bf16[1,1024,224]{1,2,0:T(8,128)(2,1)S(1)}, bf16[1,1024,224]{1,2,0:T(8,128)(2,1)}, u32[]{:S(2)}) copy-start(bf16[1,1024,224]{1,2,0:T(8,128)(2,1)} %param.10) | copy-start | bytes 1376260
  222.8 13.9 %collective-permute-start.7 = (bf16[8,768,128]{2,1,0:T(8,128)(2,1)}, bf16[8,768,128]{2,1,0:T(8,128)(2,1)}, u32[]{:S(2)}, u32[]{:S(2)}) collective-permute-start(bf16[8,768,128]{2,1,0:T(8,128)(2,1)} %bitcast.60), channel_id=1, source_target_pairs={{0,1},{1,0},{2,3},{3,2},{4,5},{5,4},{6,7},{7,6},{8,9},{9,8},{10,11... | collective-permute-start | bytes 4718600 | tf_op jit(solution)/shard_map/ppermute | solution.py:106
  231.6 16.2 %collective-permute-start.8 = (f32[128,8]{0,1:T(8,128)S(1)}, f32[128,8]{0,1:T(8,128)S(1)}, u32[]{:S(2)}, u32[]{:S(2)}) collective-permute-start(f32[128,8]{0,1:T(8,128)S(1)} %copy-done.7), channel_id=1, source_target_pairs={{0,78},{2,76},{4,74},{6,72},{8,70},{10,68},{12,66},{14,64},{64,14}... | collective-permute-start | bytes 12296 | tf_op jit(solution)/shard_map/ppermute | solution.py:83
  236.7 2.2 copy-start.8
  240.9 19.1 %all-to-all-start.2 = ((bf16[16,2,48,224]{3,2,1,0:T(8,128)(2,1)}), bf16[16,2,48,224]{3,2,1,0:T(8,128)(2,1)S(1)}, u32[]{:S(2)}, u32[]{:S(2)}) async-start(bf16[16,2,48,224]{3,2,1,0:T(8,128)(2,1)} %copy.62), calls=%async_computation.2 | async-start | bytes 1572864 | tf_op jit(solution)/shard_map/all_to_all | solution.py:119
  264.5 16.4 %collective-permute-start.9 = (f32[128,224]{1,0:T(8,128)S(1)}, f32[128,224]{1,0:T(8,128)S(1)}, u32[]{:S(2)}, u32[]{:S(2)}) collective-permute-start(f32[128,224]{1,0:T(8,128)S(1)} %fusion.18), channel_id=1, source_target_pairs={{0,64},{64,0},{1,65},{65,1},{2,66},{66,2},{3,67},{67,3},{4,68},{68... | collective-permute-start | bytes 344072 | tf_op jit(solution)/shard_map/ppermute | solution.py:124
Sparse Core Ops, SparseCore 0:
  164.9 57.7 all-gather.2

commit v8 on v6

--- a/solution.py
+++ b/solution.py
@@ -82,9 +82,9 @@
 
     def dispatch(rows, source):
         near = lax.dynamic_index_in_dim(source.reshape(rows_y, 2, rows_x, capacity), zhi, 1, keepdims=False)
-        padded = jnp.concatenate([rows, jnp.zeros((1, half_width), rows.dtype)], axis=0)
-        sent = padded[near.reshape(-1)].reshape(lines, capacity, half_width)
-        return lax.all_to_all(sent, ("y", "x"), 0, 0, tiled=True)
+        pick = (near.reshape(-1, 1) == jnp.arange(token_rows, dtype=jnp.int32)[None, :]).astype(rows.dtype)
+        sent = jnp.dot(pick, rows, preferred_element_type=jnp.float32).astype(rows.dtype)
+        return lax.all_to_all(sent.reshape(lines, capacity, half_width), ("y", "x"), 0, 0, tiled=True)
 
     arrived = jnp.stack([dispatch(own_half, own_source), dispatch(far_half, far_source)], axis=0)
     total_rows = lines * 2 * capacity

time: 271 us -> 264 us (0.974)
  local copies, waits for them, and re-layouts: 32.2 us -> 24 us
  waiting for transfers between devices: 125 us -> 120 us
  matrix products: 4.47 us -> 9.46 us
    gather x2 -> x0, local copies, waits for them, and re-layouts: 8.13 us -> none  [dispatch(): sent = padded[near.reshape(-1)].reshape(lines, capacity, half_width)]
    ppermute x3, waiting for transfers between devices: 41.4 us -> 36.3 us  [run_layer(): lax.ppermute((own_half, expert_ids, route_weights), ('zhi', 'zlo'), mirror)]
    dot_general x0 -> x2, matrix products: none -> 4.99 us  [dispatch(): jnp.dot(pick, rows, preferred_element_type=jnp.float32).astype(rows.dtype)]
  transfers between devices with their start and end apart: 18 -> 18, of which waited for: 12 -> 12; matrix products, arithmetic and copies ran while one was open for 11% -> 10% of each run, Pallas kernels for 0% -> 0%
where the time goes in v8:
time: 264 us; the launch traced here: 263 us
  waiting for transfers between devices  120 us (45%)
  starting transfers between devices  77.7 us (29%)
  local copies, waits for them, and re-layouts  24 us (9%)
  other arithmetic  16.2 us (6%)
  between operations  15.3 us (6%)
  matrix products  9.46 us (4%)
    ppermute x3, waiting for transfers between devices, run_layer(): lax.ppermute((own_half, expert_ids, route_weights), ('zhi', 'zlo'), mirror)  36.3 us
    all_to_all x2, waiting for transfers between devices, dispatch(): lax.all_to_all(sent.reshape(lines, capacity, half_width), ('y', 'x'), 0,...  35.2 us
    ppermute x3, starting transfers between devices, run_layer(): lax.ppermute((own_half, expert_ids, route_weights), ('zhi', 'zlo'), mirror)  17.8 us
    all_to_all x2, starting transfers between devices, dispatch(): lax.all_to_all(sent.reshape(lines, capacity, half_width), ('y', 'x'), 0,...  14.1 us
    ppermute x2, waiting for transfers between devices, swap_panels(): from_behind = lax.ppermute(first, 'x', ahead)  12.2 us
    all_to_all x1, waiting for transfers between devices, run_layer(): returned = lax.all_to_all(by_line, ('y', 'x'), 0, 0, tiled=True)  12.1 us
    ppermute x1, starting transfers between devices, run_layer(): partner_part = lax.ppermute(gathered, 'core', FLIP)  8.75 us
    scatter x2, local copies, waits for them, and re-layouts, routing(): jnp.full((expert_count * capacity,), token_rows, jnp.int32).at[place]  8.63 us
  transfers between devices with their start and end apart: 18, of which 12 were waited for; matrix products, arithmetic and copies ran while one was open for 10% of the time, Pallas kernels for 0%

profile of v8, /device:TPU:1, one launch (start us, length us, event | category | flops | bytes accessed | tf_op | source)
XLA Modules:
  0.0 262.8 jit_solution(17096300405303846358)
XLA Ops:
  10.1 4.3 %scatter_custom_fusion = s32[1536]{0:T(1024)S(1)} fusion(s32[1024]{0:T(1024)S(1)} %bitcast.53, s32[1024]{0:T(1024)S(1)} %reshape.229, s32[]{:T(128)} %constant.108.clone.1), kind=kCustom, calls=%fused_computation.102 | custom fusion | bytes 6148 | tf_op jit(solution)/shard_map/scatter | solution.py:52
  17.1 7.8 %all-to-all-start = ((bf16[16,48,1792]{2,1,0:T(8,128)(2,1)}), bf16[16,48,1792]{2,1,0:T(8,128)(2,1)}, u32[]{:S(2)}, u32[]{:S(2)}) async-start(bf16[16,48,1792]{2,1,0:T(8,128)(2,1)} %bitcast.41), calls=%async_computation | async-start | bytes 5505024 | tf_op jit(solution)/shard_map/all_to_all | solution.py:87
  24.9 11.1 %collective-permute-start = (s32[128,8]{0,1:T(8,128)S(1)}, s32[128,8]{0,1:T(8,128)S(1)}, u32[]{:S(2)}, u32[]{:S(2)}) collective-permute-start(s32[128,8]{0,1:T(8,128)S(1)} %copy-done.5), channel_id=1, source_target_pairs={{0,78},{2,76},{4,74},{6,72},{8,70},{10,68},{12,66},{14,64},{64,14}... | collective-permute-start | bytes 12296 | tf_op jit(solution)/shard_map/ppermute | solution.py:79
  38.6 4.3 %scatter_custom_fusion.1 = s32[1536]{0:T(1024)S(1)} fusion(s32[1024]{0:T(1024)S(1)} %bitcast.52, s32[1024]{0:T(1024)S(1)} %reshape.229, s32[]{:T(128)} %constant.108.clone.1), kind=kCustom, calls=%fused_computation.100 | custom fusion | bytes 6148 | tf_op jit(solution)/shard_map/scatter | solution.py:52
  43.1 36.3 %collective-permute-done.1 = bf16[128,1792]{1,0:T(8,128)(2,1)S(1)} collective-permute-done((bf16[128,1792]{1,0:T(8,128)(2,1)S(1)}, bf16[128,1792]{1,0:T(8,128)(2,1)S(1)}, u32[]{:S(2)}, u32[]{:S(2)}) %collective-permute-start.1) | collective-permute-done | bytes 458784 | tf_op jit(solution)/shard_map/ppermute | solution.py:79
  82.0 6.4 %all-to-all-start.1 = ((bf16[16,48,1792]{2,1,0:T(8,128)(2,1)}), bf16[16,48,1792]{2,1,0:T(8,128)(2,1)}, u32[]{:S(2)}, u32[]{:S(2)}) async-start(bf16[16,48,1792]{2,1,0:T(8,128)(2,1)} %bitcast.42), calls=%async_computation.1 | async-start | bytes 5505024 | tf_op jit(solution)/shard_map/all_to_all | solution.py:87
  88.4 35.2 %all-to-all-done.1 = bf16[16,48,1792]{2,1,0:T(8,128)(2,1)} async-done(((bf16[16,48,1792]{2,1,0:T(8,128)(2,1)}), bf16[16,48,1792]{2,1,0:T(8,128)(2,1)}, u32[]{:S(2)}, u32[]{:S(2)}) %all-to-all-start.1) | async-done | bytes 2752544 | tf_op jit(solution)/shard_map/all_to_all | solution.py:87
  123.6 3.2 %pad_maximum_fusion = bf16[2,16,48,1792]{3,2,1,0:T(8,128)(2,1)S(1)} fusion(bf16[1,16,48,1792]{3,2,1,0:T(8,128)(2,1)} %bitcast.5, bf16[1,16,48,1792]{3,2,1,0:T(8,128)(2,1)} %bitcast.2), kind=kLoop, calls=%fused_computation.4 | loop fusion | flops 2752512 | bytes 11010048 | tf_op jit(solution)/shard_map/stack | solution.py:89
  130.5 6.3 %collective-permute-start.2 = (f32[768,256]{1,0:T(8,128)}, f32[768,256]{1,0:T(8,128)S(1)}, u32[]{:S(2)}, u32[]{:S(2)}) collective-permute-start(f32[768,256]{1,0:T(8,128)} %constant_dynamic-slice_fusion), channel_id=1, source_target_pairs={{0,1},{1,0},{2,3},{3,2},{4,5},{5,4},{6,7},{7,6},{8,9},{9,8},{10,11... | collective-permute-start | bytes 2359304 | tf_op jit(solution)/shard_map/ppermute | solution.py:95
  146.9 4.9 %collective-permute-done.7 = bf16[1,512,224]{1,2,0:T(8,128)(2,1)S(1)} collective-permute-done((bf16[1,512,224]{1,2,0:T(8,128)(2,1)}, bf16[1,512,224]{1,2,0:T(8,128)(2,1)S(1)}, u32[]{:S(2)}, u32[]{:S(2)}) %collective-permute-start.7) | collective-permute-done | bytes 229408 | tf_op jit(solution)/shard_map/ppermute | solution.py:23
  154.5 7.3 %collective-permute-done.3 = bf16[1,1,896,256]{3,2,1,0:T(8,128)(2,1)S(1)} collective-permute-done((bf16[1,1,896,256]{3,2,1,0:T(8,128)(2,1)S(1)}, bf16[1,1,896,256]{3,2,1,0:T(8,128)(2,1)S(1)}, u32[]{:S(2)}, u32[]{:S(2)}) %collective-permute-start.3) | collective-permute-done | bytes 458784 | tf_op jit(solution)/shard_map/ppermute | solution.py:23
  164.5 3.4 %collective-permute-start.8 = (bf16[1,512,224]{1,2,0:T(8,128)(2,1)}, bf16[1,512,224]{1,2,0:T(8,128)(2,1)}, u32[]{:S(2)}, u32[]{:S(2)}) collective-permute-start(bf16[1,512,224]{1,2,0:T(8,128)(2,1)} %get-tuple-element.31), channel_id=1, source_target_pairs={{0,16},{16,32},{32,48},{48,0},{1,17},{17,33},{33,49},{49,1},{2,18}... | collective-permute-start | bytes 688136 | tf_op jit(solution)/shard_map/ppermute | solution.py:32
  168.7 3.1 %collective-permute-start.10 = (bf16[1,512,224]{1,2,0:T(8,128)(2,1)}, bf16[1,512,224]{1,2,0:T(8,128)(2,1)}, u32[]{:S(2)}, u32[]{:S(2)}) collective-permute-start(bf16[1,512,224]{1,2,0:T(8,128)(2,1)} %broadcast_select_fusion.2), channel_id=1, source_target_pairs={{0,48},{16,0},{32,16},{48,32},{1,49},{17,1},{33,17},{49,33},{2,50}... | collective-permute-start | bytes 688136 | tf_op jit(solution)/shard_map/ppermute | solution.py:33
  176.4 3.4 %collective-permute-start.6 = (bf16[1,1,896,256]{3,2,1,0:T(8,128)(2,1)}, bf16[1,1,896,256]{3,2,1,0:T(8,128)(2,1)}, u32[]{:S(2)}, u32[]{:S(2)}) collective-permute-start(bf16[1,1,896,256]{3,2,1,0:T(8,128)(2,1)} %broadcast_select_fusion), channel_id=1, source_target_pairs={{0,48},{16,0},{32,16},{48,32},{1,49},{17,1},{33,17},{49,33},{2,50}... | collective-permute-start | bytes 1376264 | tf_op jit(solution)/shard_map/ppermute | solution.py:33
  185.6 3.1 %collective-permute-done.6 = bf16[1,1,896,256]{3,2,1,0:T(8,128)(2,1)} collective-permute-done((bf16[1,1,896,256]{3,2,1,0:T(8,128)(2,1)}, bf16[1,1,896,256]{3,2,1,0:T(8,128)(2,1)}, u32[]{:S(2)}, u32[]{:S(2)}) %collective-permute-start.6) | collective-permute-done | bytes 458784 | tf_op jit(solution)/shard_map/ppermute | solution.py:33
  191.0 5.3 %all-gather.3.cloned.1.call-done = bf16[6144,128]{1,0:T(8,128)(2,1)} async-done(((bf16[768,128]{1,0:T(8,128)(2,1)}), bf16[6144,128]{1,0:T(8,128)(2,1)}) %all-gather.3.cloned.1.call-update) | async-done | bytes 1572880 | tf_op jit(solution)/shard_map/all_gather | solution.py:100
  196.3 8.7 %collective-permute-start.11 = (bf16[8,768,128]{2,1,0:T(8,128)(2,1)}, bf16[8,768,128]{2,1,0:T(8,128)(2,1)}, u32[]{:S(2)}, u32[]{:S(2)}) collective-permute-start(bf16[8,768,128]{2,1,0:T(8,128)(2,1)} %bitcast.54), channel_id=1, source_target_pairs={{0,1},{1,0},{2,3},{3,2},{4,5},{5,4},{6,7},{7,6},{8,9},{9,8},{10,11... | collective-permute-start | bytes 4718600 | tf_op jit(solution)/shard_map/ppermute | solution.py:102
  205.1 4.8 %collective-permute-start.12 = (f32[128,8]{0,1:T(8,128)S(1)}, f32[128,8]{0,1:T(8,128)S(1)}, u32[]{:S(2)}, u32[]{:S(2)}) collective-permute-start(f32[128,8]{0,1:T(8,128)S(1)} %copy-done.6), channel_id=1, source_target_pairs={{0,78},{2,76},{4,74},{6,72},{8,70},{10,68},{12,66},{14,64},{64,14}... | collective-permute-start | bytes 12296 | tf_op jit(solution)/shard_map/ppermute | solution.py:79
  214.4 6.5 %all-to-all-start.2 = ((bf16[16,2,48,224]{3,2,1,0:T(8,128)(2,1)}), bf16[16,2,48,224]{3,2,1,0:T(8,128)(2,1)S(1)}, u32[]{:S(2)}, u32[]{:S(2)}) async-start(bf16[16,2,48,224]{3,2,1,0:T(8,128)(2,1)} %copy.52), calls=%async_computation.2 | async-start | bytes 1572864 | tf_op jit(solution)/shard_map/all_to_all | solution.py:115
  221.4 12.1 %all-to-all-done.2 = bf16[16,2,48,224]{3,2,1,0:T(8,128)(2,1)S(1)} async-done(((bf16[16,2,48,224]{3,2,1,0:T(8,128)(2,1)}), bf16[16,2,48,224]{3,2,1,0:T(8,128)(2,1)S(1)}, u32[]{:S(2)}, u32[]{:S(2)}) %all-to-all-start.2) | async-done | bytes 688160 | tf_op jit(solution)/shard_map/all_to_all | solution.py:115
  233.6 3.9 %gather_fusion.1 = bf16[1024,224]{1,0:T(8,128)(2,1)S(1)} fusion(bf16[769,224]{1,0:T(8,128)(2,1)S(1)} %concatenate.19, s32[1024]{0:T(1024)S(1)} %broadcast_clamp_fusion), kind=kCustom, calls=%fused_computation.1 | custom fusion | bytes 921600 | tf_op jit(solution)/shard_map/gather | solution.py:62
  237.9 4.4 %collective-permute-start.13 = (f32[128,224]{1,0:T(8,128)S(1)}, f32[128,224]{1,0:T(8,128)S(1)}, u32[]{:S(2)}, u32[]{:S(2)}) collective-permute-start(f32[128,224]{1,0:T(8,128)S(1)} %fusion.18), channel_id=1, source_target_pairs={{0,64},{64,0},{1,65},{65,1},{2,66},{66,2},{3,67},{67,3},{4,68},{68... | collective-permute-start | bytes 344072 | tf_op jit(solution)/shard_map/ppermute | solution.py:120
  242.4 3.9 %gather_fusion = bf16[1024,224]{1,0:T(8,128)(2,1)S(1)} fusion(bf16[769,224]{1,0:T(8,128)(2,1)S(1)} %concatenate.18, s32[1024]{0:T(1024)S(1)} %broadcast_clamp_fusion.1), kind=kCustom, calls=%fused_computation | custom fusion | bytes 921600 | tf_op jit(solution)/shard_map/gather | solution.py:62
  246.7 8.5 %collective-permute-done.13 = f32[128,224]{1,0:T(8,128)S(1)} collective-permute-done((f32[128,224]{1,0:T(8,128)S(1)}, f32[128,224]{1,0:T(8,128)S(1)}, u32[]{:S(2)}, u32[]{:S(2)}) %collective-permute-start.13) | collective-permute-done | bytes 114720 | tf_op jit(solution)/shard_map/ppermute | solution.py:120
  (105 shorter events, 49.1 us)
Async XLA Ops:
  7.2 7.4 %copy-start = (bf16[128,3584]{1,0:T(8,128)(2,1)S(1)}, bf16[128,3584]{1,0:T(8,128)(2,1)}, u32[]{:S(2)}) copy-start(bf16[128,3584]{1,0:T(8,128)(2,1)} %param.6) | copy-start | bytes 2752516
  17.1 7.8 %copy-start.5 = (s32[128,8]{0,1:T(8,128)S(1)}, s32[128,8]{0,1:T(8,128)}, u32[]{:S(2)}) copy-start(s32[128,8]{0,1:T(8,128)} %param.7) | copy-start | bytes 12292
  17.1 64.8 %all-to-all-start = ((bf16[16,48,1792]{2,1,0:T(8,128)(2,1)}), bf16[16,48,1792]{2,1,0:T(8,128)(2,1)}, u32[]{:S(2)}, u32[]{:S(2)}) async-start(bf16[16,48,1792]{2,1,0:T(8,128)(2,1)} %bitcast.41), calls=%async_computation | async-start | bytes 5505024 | tf_op jit(solution)/shard_map/all_to_all | solution.py:87
  24.9 13.1 %collective-permute-start = (s32[128,8]{0,1:T(8,128)S(1)}, s32[128,8]{0,1:T(8,128)S(1)}, u32[]{:S(2)}, u32[]{:S(2)}) collective-permute-start(s32[128,8]{0,1:T(8,128)S(1)} %copy-done.5), channel_id=1, source_target_pairs={{0,78},{2,76},{4,74},{6,72},{8,70},{10,68},{12,66},{14,64},{64,14}... | collective-permute-start | bytes 12296 | tf_op jit(solution)/shard_map/ppermute | solution.py:79
  36.0 43.4 %collective-permute-start.1 = (bf16[128,1792]{1,0:T(8,128)(2,1)S(1)}, bf16[128,1792]{1,0:T(8,128)(2,1)S(1)}, u32[]{:S(2)}, u32[]{:S(2)}) collective-permute-start(bf16[128,1792]{1,0:T(8,128)(2,1)S(1)} %constant_dynamic-slice_fusion.2), channel_id=1, source_target_pairs={{0,78},{2,76},{4,74},{6,72},{8,70},{10,68},{12,66},{14,64},{64,14}... | collective-permute-start | bytes 1376264 | tf_op jit(solution)/shard_map/ppermute | solution.py:79
  82.0 41.6 %all-to-all-start.1 = ((bf16[16,48,1792]{2,1,0:T(8,128)(2,1)}), bf16[16,48,1792]{2,1,0:T(8,128)(2,1)}, u32[]{:S(2)}, u32[]{:S(2)}) async-start(bf16[16,48,1792]{2,1,0:T(8,128)(2,1)} %bitcast.42), calls=%async_computation.1 | async-start | bytes 5505024 | tf_op jit(solution)/shard_map/all_to_all | solution.py:87
  88.3 108.0 %all-gather.3.cloned.1.call-start = ((), (), s32[]{:S(2)}) async-start(), calls=%async_computation.3 | async-start | bytes 1769472 | tf_op jit(solution)/shard_map/all_gather | solution.py:100
  130.5 8.4 %collective-permute-start.2 = (f32[768,256]{1,0:T(8,128)}, f32[768,256]{1,0:T(8,128)S(1)}, u32[]{:S(2)}, u32[]{:S(2)}) collective-permute-start(f32[768,256]{1,0:T(8,128)} %constant_dynamic-slice_fusion), channel_id=1, source_target_pairs={{0,1},{1,0},{2,3},{3,2},{4,5},{5,4},{6,7},{7,6},{8,9},{9,8},{10,11... | collective-permute-start | bytes 2359304 | tf_op jit(solution)/shard_map/ppermute | solution.py:95
  136.9 4.2 %copy-start.2 = (bf16[1,1024,224]{1,2,0:T(8,128)(2,1)S(1)}, bf16[1,1024,224]{1,2,0:T(8,128)(2,1)}, u32[]{:S(2)}) copy-start(bf16[1,1024,224]{1,2,0:T(8,128)(2,1)} %param.10) | copy-start | bytes 1376260
  140.2 5.4 %copy-start.8 = (s32[32]{0:T(128)S(1)}, s32[32]{0:T(128)}, u32[]{:S(2)}) copy-start(s32[32]{0:T(128)} %param.11) | copy-start | bytes 388
  141.7 10.1 %collective-permute-start.7 = (bf16[1,512,224]{1,2,0:T(8,128)(2,1)}, bf16[1,512,224]{1,2,0:T(8,128)(2,1)S(1)}, u32[]{:S(2)}, u32[]{:S(2)}) collective-permute-start(bf16[1,512,224]{1,2,0:T(8,128)(2,1)} %slice.28), channel_id=1, source_target_pairs={{0,16},{16,32},{32,48},{48,0},{1,17},{17,33},{33,49},{49,1},{2,18}... | collective-permute-start | bytes 688136 | tf_op jit(solution)/shard_map/ppermute | solution.py:23
  143.7 18.1 %collective-permute-start.3 = (bf16[1,1,896,256]{3,2,1,0:T(8,128)(2,1)S(1)}, bf16[1,1,896,256]{3,2,1,0:T(8,128)(2,1)S(1)}, u32[]{:S(2)}, u32[]{:S(2)}) collective-permute-start(bf16[1,1,896,256]{3,2,1,0:T(8,128)(2,1)S(1)} %slice.26), channel_id=1, source_target_pairs={{0,16},{16,32},{32,48},{48,0},{1,17},{17,33},{33,49},{49,1},{2,18}... | collective-permute-start | bytes 1376264 | tf_op jit(solution)/shard_map/ppermute | solution.py:23
  152.5 15.3 %collective-permute-start.9 = (bf16[1,512,224]{1,2,0:T(8,128)(2,1)S(1)}, bf16[1,512,224]{1,2,0:T(8,128)(2,1)S(1)}, u32[]{:S(2)}, u32[]{:S(2)}) collective-permute-start(bf16[1,512,224]{1,2,0:T(8,128)(2,1)S(1)} %get-tuple-element.32), channel_id=1, source_target_pairs={{0,48},{16,0},{32,16},{48,32},{1,49},{17,1},{33,17},{49,33},{2,50}... | collective-permute-start | bytes 688136 | tf_op jit(solution)/shard_map/ppermute | solution.py:24
  162.6 12.9 %collective-permute-start.5 = (bf16[1,1,896,256]{3,2,1,0:T(8,128)(2,1)S(1)}, bf16[1,1,896,256]{3,2,1,0:T(8,128)(2,1)S(1)}, u32[]{:S(2)}, u32[]{:S(2)}) collective-permute-start(bf16[1,1,896,256]{3,2,1,0:T(8,128)(2,1)S(1)} %get-tuple-element.28), channel_id=1, source_target_pairs={{0,48},{16,0},{32,16},{48,32},{1,49},{17,1},{33,17},{49,33},{2,50}... | collective-permute-start | bytes 1376264 | tf_op jit(solution)/shard_map/ppermute | solution.py:24
  164.5 15.3 %collective-permute-start.8 = (bf16[1,512,224]{1,2,0:T(8,128)(2,1)}, bf16[1,512,224]{1,2,0:T(8,128)(2,1)}, u32[]{:S(2)}, u32[]{:S(2)}) collective-permute-start(bf16[1,512,224]{1,2,0:T(8,128)(2,1)} %get-tuple-element.31), channel_id=1, source_target_pairs={{0,16},{16,32},{32,48},{48,0},{1,17},{17,33},{33,49},{49,1},{2,18}... | collective-permute-start | bytes 688136 | tf_op jit(solution)/shard_map/ppermute | solution.py:32
  167.9 7.6 %copy-start.4 = (bf16[1,512,224]{1,2,0:T(8,128)(2,1)}, bf16[1,512,224]{1,2,0:T(8,128)(2,1)S(1)}, u32[]{:S(2)}) copy-start(bf16[1,512,224]{1,2,0:T(8,128)(2,1)S(1)} %collective-permute-done.9) | copy-start | bytes 688132
  168.7 11.8 %collective-permute-start.10 = (bf16[1,512,224]{1,2,0:T(8,128)(2,1)}, bf16[1,512,224]{1,2,0:T(8,128)(2,1)}, u32[]{:S(2)}, u32[]{:S(2)}) collective-permute-start(bf16[1,512,224]{1,2,0:T(8,128)(2,1)} %broadcast_select_fusion.2), channel_id=1, source_target_pairs={{0,48},{16,0},{32,16},{48,32},{1,49},{17,1},{33,17},{49,33},{2,50}... | collective-permute-start | bytes 688136 | tf_op jit(solution)/shard_map/ppermute | solution.py:33
  171.8 13.8 %collective-permute-start.4 = (bf16[1,1,896,256]{3,2,1,0:T(8,128)(2,1)}, bf16[1,1,896,256]{3,2,1,0:T(8,128)(2,1)}, u32[]{:S(2)}, u32[]{:S(2)}) collective-permute-start(bf16[1,1,896,256]{3,2,1,0:T(8,128)(2,1)} %get-tuple-element.27), channel_id=1, source_target_pairs={{0,16},{16,32},{32,48},{48,0},{1,17},{17,33},{33,49},{49,1},{2,18}... | collective-permute-start | bytes 1376264 | tf_op jit(solution)/shard_map/ppermute | solution.py:32
  176.4 12.3 %collective-permute-start.6 = (bf16[1,1,896,256]{3,2,1,0:T(8,128)(2,1)}, bf16[1,1,896,256]{3,2,1,0:T(8,128)(2,1)}, u32[]{:S(2)}, u32[]{:S(2)}) collective-permute-start(bf16[1,1,896,256]{3,2,1,0:T(8,128)(2,1)} %broadcast_select_fusion), channel_id=1, source_target_pairs={{0,48},{16,0},{32,16},{48,32},{1,49},{17,1},{33,17},{49,33},{2,50}... | collective-permute-start | bytes 1376264 | tf_op jit(solution)/shard_map/ppermute | solution.py:33
  190.0 15.1 %copy-start.6 = (f32[128,8]{0,1:T(8,128)S(1)}, f32[128,8]{0,1:T(8,128)}, u32[]{:S(2)}) copy-start(f32[128,8]{0,1:T(8,128)} %param.8) | copy-start | bytes 12292
  196.3 13.9 %collective-permute-start.11 = (bf16[8,768,128]{2,1,0:T(8,128)(2,1)}, bf16[8,768,128]{2,1,0:T(8,128)(2,1)}, u32[]{:S(2)}, u32[]{:S(2)}) collective-permute-start(bf16[8,768,128]{2,1,0:T(8,128)(2,1)} %bitcast.54), channel_id=1, source_target_pairs={{0,1},{1,0},{2,3},{3,2},{4,5},{5,4},{6,7},{7,6},{8,9},{9,8},{10,11... | collective-permute-start | bytes 4718600 | tf_op jit(solution)/shard_map/ppermute | solution.py:102
  205.1 16.2 %collective-permute-start.12 = (f32[128,8]{0,1:T(8,128)S(1)}, f32[128,8]{0,1:T(8,128)S(1)}, u32[]{:S(2)}, u32[]{:S(2)}) collective-permute-start(f32[128,8]{0,1:T(8,128)S(1)} %copy-done.6), channel_id=1, source_target_pairs={{0,78},{2,76},{4,74},{6,72},{8,70},{10,68},{12,66},{14,64},{64,14}... | collective-permute-start | bytes 12296 | tf_op jit(solution)/shard_map/ppermute | solution.py:79
  214.4 19.0 %all-to-all-start.2 = ((bf16[16,2,48,224]{3,2,1,0:T(8,128)(2,1)}), bf16[16,2,48,224]{3,2,1,0:T(8,128)(2,1)S(1)}, u32[]{:S(2)}, u32[]{:S(2)}) async-start(bf16[16,2,48,224]{3,2,1,0:T(8,128)(2,1)} %copy.52), calls=%async_computation.2 | async-start | bytes 1572864 | tf_op jit(solution)/shard_map/all_to_all | solution.py:115
  237.9 17.3 %collective-permute-start.13 = (f32[128,224]{1,0:T(8,128)S(1)}, f32[128,224]{1,0:T(8,128)S(1)}, u32[]{:S(2)}, u32[]{:S(2)}) collective-permute-start(f32[128,224]{1,0:T(8,128)S(1)} %fusion.18), channel_id=1, source_target_pairs={{0,64},{64,0},{1,65},{65,1},{2,66},{66,2},{3,67},{67,3},{4,68},{68... | collective-permute-start | bytes 344072 | tf_op jit(solution)/shard_map/ppermute | solution.py:120
  (3 other events, 6.6 us)
Sparse Core Ops, SparseCore 0:
  141.1 55.1 all-gather.2

commit v9 on v8

--- a/solution.py
+++ b/solution.py
@@ -9,10 +9,7 @@
 FLIP = [(0, 1), (1, 0)]
 
 
-def swap_panels(gate_up, down, partner):
-    here = lax.axis_index(EXPERT)
-    kind = jnp.bitwise_xor(partner[here], here)
-    even = (lax.axis_index("x") & 1) == 0
+def swap_start(gate_up, down):
     gate_rows = gate_up.shape[2] // 2
     down_rows = down.shape[1] // 2
     first = (gate_up[:, :, :gate_rows], down[:, :down_rows])
@@ -22,6 +19,17 @@
     behind = [(i, (i + ring - 1) % ring) for i in range(ring)]
     from_behind = lax.ppermute(first, "x", ahead)
     from_ahead = lax.ppermute(second, "x", behind)
+    return (first, second, from_behind, from_ahead)
+
+
+def swap_finish(state, partner):
+    first, second, from_behind, from_ahead = state
+    here = lax.axis_index(EXPERT)
+    kind = jnp.bitwise_xor(partner[here], here)
+    even = (lax.axis_index("x") & 1) == 0
+    ring = lax.axis_size("x")
+    ahead = [(i, (i + 1) % ring) for i in range(ring)]
+    behind = [(i, (i + ring - 1) % ring) for i in range(ring)]
     is_two = kind == 2
 
     def pick(flag, left, right):
@@ -76,7 +84,9 @@
     zhi = lax.axis_index("zhi")
     own_half = lax.dynamic_slice_in_dim(tokens, side * half_width, half_width, 1)
     mirror = [(high * chunks + low, (1 - high) * chunks + chunks - 1 - low) for high in range(2) for low in range(chunks)]
+    swap_state = swap_start(swap_in[0], swap_in[1])
     far_half, far_ids, far_weights = lax.ppermute((own_half, expert_ids, route_weights), ("zhi", "zlo"), mirror)
+    far_half, swap_state = lax.optimization_barrier((far_half, swap_state))
     own_slots, own_source = routing(expert_ids, expert_count, capacity)
     far_slots, far_source = routing(far_ids, expert_count, capacity)
 
@@ -95,8 +105,8 @@
     summed = mine + lax.ppermute(other, "core", FLIP)
     block_units = gate_up.shape[1] // 2
     hidden = (jax.nn.silu(summed[:, :block_units]) * summed[:, block_units:]).astype(jnp.bfloat16)
-    hidden, swap_in = lax.optimization_barrier((hidden, swap_in))
-    swapped = swap_panels(*swap_in)
+    hidden, swap_state = lax.optimization_barrier((hidden, swap_state))
+    swapped = swap_finish(swap_state, swap_in[2])
     gathered = lax.all_gather(hidden, "zlo", axis=0, tiled=False)
     gathered, swapped = lax.optimization_barrier((gathered, swapped))
     partner_part = lax.ppermute(gathered, "core", FLIP)

time: 264 us -> 275 us (1.042)
  waiting for transfers between devices: 120 us -> 127 us
    all_gather x1, waiting for transfers between devices: 5.34 us -> 24.9 us  [run_layer(): gathered = lax.all_gather(hidden, 'zlo', axis=0, tiled=False)]
    ppermute x8, waiting for transfers between devices: 20.7 us -> 10.3 us  [the longest x2 6.01 us: swap_finish(): got_behind = lax.ppermute(send_ahead, 'x', ahead)]
    ppermute x3, waiting for transfers between devices: 36.3 us -> 28.7 us  [run_layer(): lax.ppermute((own_half, expert_ids, route_weights), ('zhi', 'zlo'), mirror)]
    all_to_all x2, waiting for transfers between devices: 35.2 us -> 39.2 us  [dispatch(): lax.all_to_all(sent.reshape(lines, capacity, half_width), ('y', 'x'), 0,...]
    ppermute x8, starting transfers between devices: 19.7 us -> 23.5 us  [the longest x2 7.7 us: swap_start(): from_ahead = lax.ppermute(second, 'x', behind)]
  transfers between devices with their start and end apart: 18 -> 18, of which waited for: 12 -> 9; matrix products, arithmetic and copies ran while one was open for 10% -> 11% of each run, Pallas kernels for 0% -> 0%
where the time goes in v9:
time: 275 us; the launch traced here: 274 us
  waiting for transfers between devices  127 us (46%)
  starting transfers between devices  77.1 us (28%)
  local copies, waits for them, and re-layouts  26.6 us (10%)
  other arithmetic  17.9 us (7%)
  between operations  15.3 us (6%)
  matrix products  10.5 us (4%)
    all_to_all x2, waiting for transfers between devices, dispatch(): lax.all_to_all(sent.reshape(lines, capacity, half_width), ('y', 'x'), 0,...  39.2 us
    ppermute x3, waiting for transfers between devices, run_layer(): lax.ppermute((own_half, expert_ids, route_weights), ('zhi', 'zlo'), mirror)  28.7 us
    all_gather x1, waiting for transfers between devices, run_layer(): gathered = lax.all_gather(hidden, 'zlo', axis=0, tiled=False)  24.9 us
    ppermute x3, starting transfers between devices, run_layer(): lax.ppermute((own_half, expert_ids, route_weights), ('zhi', 'zlo'), mirror)  18.4 us
    all_to_all x1, waiting for transfers between devices, run_layer(): returned = lax.all_to_all(by_line, ('y', 'x'), 0, 0, tiled=True)  13.2 us
    all_to_all x2, starting transfers between devices, dispatch(): lax.all_to_all(sent.reshape(lines, capacity, half_width), ('y', 'x'), 0,...  12.2 us
    scatter x2, local copies, waits for them, and re-layouts, routing(): jnp.full((expert_count * capacity,), token_rows, jnp.int32).at[place]  8.63 us
    ppermute x1, waiting for transfers between devices, run_layer(): mixed = own_sum + lax.ppermute(far_sum, 'zhi', FLIP)  8.37 us
  transfers between devices with their start and end apart: 18, of which 9 were waited for; matrix products, arithmetic and copies ran while one was open for 11% of the time, Pallas kernels for 0%

profile of v9, /device:TPU:1, one launch (start us, length us, event | category | flops | bytes accessed | tf_op | source)
XLA Modules:
  0.0 274.2 jit_solution(14162481113744663773)
XLA Ops:
  10.1 4.3 %scatter_custom_fusion = s32[1536]{0:T(1024)S(1)} fusion(s32[1024]{0:T(1024)S(1)} %bitcast.53, s32[1024]{0:T(1024)S(1)} %reshape.229, s32[]{:T(128)} %constant.108.clone.1), kind=kCustom, calls=%fused_computation.102 | custom fusion | bytes 6148 | tf_op jit(solution)/shard_map/scatter | solution.py:60
  17.1 7.8 %all-to-all-start = ((bf16[16,48,1792]{2,1,0:T(8,128)(2,1)}), bf16[16,48,1792]{2,1,0:T(8,128)(2,1)}, u32[]{:S(2)}, u32[]{:S(2)}) async-start(bf16[16,48,1792]{2,1,0:T(8,128)(2,1)} %bitcast.41), calls=%async_computation | async-start | bytes 5505024 | tf_op jit(solution)/shard_map/all_to_all | solution.py:97
  24.9 11.3 %collective-permute-start.1 = (bf16[128,1792]{1,0:T(8,128)(2,1)S(1)}, bf16[128,1792]{1,0:T(8,128)(2,1)}, u32[]{:S(2)}, u32[]{:S(2)}) collective-permute-start(bf16[128,1792]{1,0:T(8,128)(2,1)S(1)} %constant_dynamic-slice_fusion.2), channel_id=1, source_target_pairs={{0,78},{2,76},{4,74},{6,72},{8,70},{10,68},{12,66},{14,64},{64,14}... | collective-permute-start | bytes 1376264 | tf_op jit(solution)/shard_map/ppermute | solution.py:88
  39.3 3.2 %collective-permute-start.2 = (bf16[1,1,896,256]{3,2,1,0:T(8,128)(2,1)S(1)}, bf16[1,1,896,256]{3,2,1,0:T(8,128)(2,1)}, u32[]{:S(2)}, u32[]{:S(2)}) collective-permute-start(bf16[1,1,896,256]{3,2,1,0:T(8,128)(2,1)S(1)} %get-tuple-element.37), channel_id=1, source_target_pairs={{0,16},{16,32},{32,48},{48,0},{1,17},{17,33},{33,49},{49,1},{2,18}... | collective-permute-start | bytes 1376264 | tf_op jit(solution)/shard_map/ppermute | solution.py:20
  42.6 3.3 %collective-permute-start.4 = (bf16[1,1,896,256]{3,2,1,0:T(8,128)(2,1)S(1)}, bf16[1,1,896,256]{3,2,1,0:T(8,128)(2,1)}, u32[]{:S(2)}, u32[]{:S(2)}) collective-permute-start(bf16[1,1,896,256]{3,2,1,0:T(8,128)(2,1)S(1)} %get-tuple-element.35), channel_id=1, source_target_pairs={{0,48},{16,0},{32,16},{48,32},{1,49},{17,1},{33,17},{49,33},{2,50}... | collective-permute-start | bytes 1376264 | tf_op jit(solution)/shard_map/ppermute | solution.py:21
  47.9 28.7 %collective-permute-done = s32[128,8]{0,1:T(8,128)S(1)} collective-permute-done((s32[128,8]{0,1:T(8,128)S(1)}, s32[128,8]{0,1:T(8,128)S(1)}, u32[]{:S(2)}, u32[]{:S(2)}) %collective-permute-start) | collective-permute-done | bytes 4128 | tf_op jit(solution)/shard_map/ppermute | solution.py:88
  76.6 4.4 %collective-permute-start.5 = (bf16[1,512,224]{1,2,0:T(8,128)(2,1)S(1)}, bf16[1,512,224]{1,2,0:T(8,128)(2,1)}, u32[]{:S(2)}, u32[]{:S(2)}) collective-permute-start(bf16[1,512,224]{1,2,0:T(8,128)(2,1)S(1)} %get-tuple-element.39), channel_id=1, source_target_pairs={{0,48},{16,0},{32,16},{48,32},{1,49},{17,1},{33,17},{49,33},{2,50}... | collective-permute-start | bytes 688136 | tf_op jit(solution)/shard_map/ppermute | solution.py:21
  84.6 4.3 %scatter_custom_fusion.1 = s32[1536]{0:T(1024)S(1)} fusion(s32[1024]{0:T(1024)S(1)} %bitcast.52, s32[1024]{0:T(1024)S(1)} %reshape.229, s32[]{:T(128)} %constant.108.clone.1), kind=kCustom, calls=%fused_computation.100 | custom fusion | bytes 6148 | tf_op jit(solution)/shard_map/scatter | solution.py:60
  89.2 3.5 %convolution_convert_fusion = bf16[768,1792]{1,0:T(8,128)(2,1)} fusion(bf16[128,1792]{1,0:T(8,128)(2,1)} %collective-permute-done.1, s32[768]{0:T(1024)S(1)} %eq.95), kind=kOutput, calls=%fused_computation.5 | convolution fusion | flops 353796096 | bytes 3214336 | tf_op jit(solution)/shard_map/dot_general | solution.py:96
  92.7 4.5 %all-to-all-start.1 = ((bf16[16,48,1792]{2,1,0:T(8,128)(2,1)}), bf16[16,48,1792]{2,1,0:T(8,128)(2,1)}, u32[]{:S(2)}, u32[]{:S(2)}) async-start(bf16[16,48,1792]{2,1,0:T(8,128)(2,1)} %bitcast.42), calls=%async_computation.1 | async-start | bytes 5505024 | tf_op jit(solution)/shard_map/all_to_all | solution.py:97
  97.2 39.2 %all-to-all-done.1 = bf16[16,48,1792]{2,1,0:T(8,128)(2,1)} async-done(((bf16[16,48,1792]{2,1,0:T(8,128)(2,1)}), bf16[16,48,1792]{2,1,0:T(8,128)(2,1)}, u32[]{:S(2)}, u32[]{:S(2)}) %all-to-all-start.1) | async-done | bytes 2752544 | tf_op jit(solution)/shard_map/all_to_all | solution.py:97
  143.3 4.4 %collective-permute-start.6 = (f32[768,256]{1,0:T(8,128)}, f32[768,256]{1,0:T(8,128)}, u32[]{:S(2)}, u32[]{:S(2)}) collective-permute-start(f32[768,256]{1,0:T(8,128)} %constant_dynamic-slice_fusion), channel_id=1, source_target_pairs={{0,1},{1,0},{2,3},{3,2},{4,5},{5,4},{6,7},{7,6},{8,9},{9,8},{10,11... | collective-permute-start | bytes 2359304 | tf_op jit(solution)/shard_map/ppermute | solution.py:105
  156.9 3.4 %collective-permute-start.9 = (bf16[1,512,224]{1,2,0:T(8,128)(2,1)}, bf16[1,512,224]{1,2,0:T(8,128)(2,1)}, u32[]{:S(2)}, u32[]{:S(2)}) collective-permute-start(bf16[1,512,224]{1,2,0:T(8,128)(2,1)} %broadcast_select_fusion.3), channel_id=1, source_target_pairs={{0,16},{16,32},{32,48},{48,0},{1,17},{17,33},{33,49},{49,1},{2,18}... | collective-permute-start | bytes 688136 | tf_op jit(solution)/shard_map/ppermute | solution.py:40
  169.2 4.3 %collective-permute-done.8 = bf16[1,1,896,256]{3,2,1,0:T(8,128)(2,1)} collective-permute-done((bf16[1,1,896,256]{3,2,1,0:T(8,128)(2,1)S(1)}, bf16[1,1,896,256]{3,2,1,0:T(8,128)(2,1)}, u32[]{:S(2)}, u32[]{:S(2)}) %collective-permute-start.8) | collective-permute-done | bytes 458784 | tf_op jit(solution)/shard_map/ppermute | solution.py:41
  173.5 5.4 %collective-permute-done.7 = bf16[1,1,896,256]{3,2,1,0:T(8,128)(2,1)} collective-permute-done((bf16[1,1,896,256]{3,2,1,0:T(8,128)(2,1)}, bf16[1,1,896,256]{3,2,1,0:T(8,128)(2,1)}, u32[]{:S(2)}, u32[]{:S(2)}) %collective-permute-start.7) | collective-permute-done | bytes 458784 | tf_op jit(solution)/shard_map/ppermute | solution.py:40
  181.3 24.9 %all-gather.3.cloned.1.call-done = bf16[6144,128]{1,0:T(8,128)(2,1)} async-done(((bf16[768,128]{1,0:T(8,128)(2,1)}), bf16[6144,128]{1,0:T(8,128)(2,1)}) %all-gather.3.cloned.1.call-update) | async-done | bytes 1572880 | tf_op jit(solution)/shard_map/all_gather | solution.py:110
  206.2 8.3 %collective-permute-start.11 = (bf16[8,768,128]{2,1,0:T(8,128)(2,1)}, bf16[8,768,128]{2,1,0:T(8,128)(2,1)S(1)}, u32[]{:S(2)}, u32[]{:S(2)}) collective-permute-start(bf16[8,768,128]{2,1,0:T(8,128)(2,1)} %bitcast.54), channel_id=1, source_target_pairs={{0,1},{1,0},{2,3},{3,2},{4,5},{5,4},{6,7},{7,6},{8,9},{9,8},{10,11... | collective-permute-start | bytes 4718600 | tf_op jit(solution)/shard_map/ppermute | solution.py:112
  214.5 5.2 %collective-permute-start.12 = (f32[128,8]{0,1:T(8,128)S(1)}, f32[128,8]{0,1:T(8,128)S(1)}, u32[]{:S(2)}, u32[]{:S(2)}) collective-permute-start(f32[128,8]{0,1:T(8,128)S(1)} %copy-done.5), channel_id=1, source_target_pairs={{0,78},{2,76},{4,74},{6,72},{8,70},{10,68},{12,66},{14,64},{64,14}... | collective-permute-start | bytes 12296 | tf_op jit(solution)/shard_map/ppermute | solution.py:88
  225.4 6.6 %all-to-all-start.2 = ((bf16[16,2,48,224]{3,2,1,0:T(8,128)(2,1)}), bf16[16,2,48,224]{3,2,1,0:T(8,128)(2,1)S(1)}, u32[]{:S(2)}, u32[]{:S(2)}) async-start(bf16[16,2,48,224]{3,2,1,0:T(8,128)(2,1)} %copy.52), calls=%async_computation.2 | async-start | bytes 1572864 | tf_op jit(solution)/shard_map/all_to_all | solution.py:125
  232.5 13.2 %all-to-all-done.2 = bf16[16,2,48,224]{3,2,1,0:T(8,128)(2,1)S(1)} async-done(((bf16[16,2,48,224]{3,2,1,0:T(8,128)(2,1)}), bf16[16,2,48,224]{3,2,1,0:T(8,128)(2,1)S(1)}, u32[]{:S(2)}, u32[]{:S(2)}) %all-to-all-start.2) | async-done | bytes 688160 | tf_op jit(solution)/shard_map/all_to_all | solution.py:125
  245.8 3.9 %gather_fusion.1 = bf16[1024,224]{1,0:T(8,128)(2,1)S(1)} fusion(bf16[769,224]{1,0:T(8,128)(2,1)S(1)} %concatenate.19, s32[1024]{0:T(1024)S(1)} %broadcast_clamp_fusion), kind=kCustom, calls=%fused_computation.1 | custom fusion | bytes 921600 | tf_op jit(solution)/shard_map/gather | solution.py:70
  250.1 3.7 %collective-permute-start.13 = (f32[128,224]{1,0:T(8,128)S(1)}, f32[128,224]{1,0:T(8,128)S(1)}, u32[]{:S(2)}, u32[]{:S(2)}) collective-permute-start(f32[128,224]{1,0:T(8,128)S(1)} %fusion.18), channel_id=1, source_target_pairs={{0,64},{64,0},{1,65},{65,1},{2,66},{66,2},{3,67},{67,3},{4,68},{68... | collective-permute-start | bytes 344072 | tf_op jit(solution)/shard_map/ppermute | solution.py:130
  253.9 3.9 %gather_fusion = bf16[1024,224]{1,0:T(8,128)(2,1)S(1)} fusion(bf16[769,224]{1,0:T(8,128)(2,1)S(1)} %concatenate.18, s32[1024]{0:T(1024)S(1)} %broadcast_clamp_fusion.1), kind=kCustom, calls=%fused_computation | custom fusion | bytes 921600 | tf_op jit(solution)/shard_map/gather | solution.py:70
  258.2 8.4 %collective-permute-done.13 = f32[128,224]{1,0:T(8,128)S(1)} collective-permute-done((f32[128,224]{1,0:T(8,128)S(1)}, f32[128,224]{1,0:T(8,128)S(1)}, u32[]{:S(2)}, u32[]{:S(2)}) %collective-permute-start.13) | collective-permute-done | bytes 114720 | tf_op jit(solution)/shard_map/ppermute | solution.py:130
  (107 shorter events, 49.0 us)
Async XLA Ops:
  7.2 7.4 %copy-start = (bf16[128,3584]{1,0:T(8,128)(2,1)S(1)}, bf16[128,3584]{1,0:T(8,128)(2,1)}, u32[]{:S(2)}) copy-start(bf16[128,3584]{1,0:T(8,128)(2,1)} %param.6) | copy-start | bytes 2752516
  17.1 19.0 %copy-start.4 = (s32[128,8]{0,1:T(8,128)S(1)}, s32[128,8]{0,1:T(8,128)}, u32[]{:S(2)}) copy-start(s32[128,8]{0,1:T(8,128)} %param.7) | copy-start | bytes 12292
  17.1 75.5 %all-to-all-start = ((bf16[16,48,1792]{2,1,0:T(8,128)(2,1)}), bf16[16,48,1792]{2,1,0:T(8,128)(2,1)}, u32[]{:S(2)}, u32[]{:S(2)}) async-start(bf16[16,48,1792]{2,1,0:T(8,128)(2,1)} %bitcast.41), calls=%async_computation | async-start | bytes 5505024 | tf_op jit(solution)/shard_map/all_to_all | solution.py:97
  24.9 20.9 %copy-start.1 = (bf16[1,1024,224]{1,2,0:T(8,128)(2,1)S(1)}, bf16[1,1024,224]{1,2,0:T(8,128)(2,1)}, u32[]{:S(2)}) copy-start(bf16[1,1024,224]{1,2,0:T(8,128)(2,1)} %param.10) | copy-start | bytes 1376260
  24.9 64.3 %collective-permute-start.1 = (bf16[128,1792]{1,0:T(8,128)(2,1)S(1)}, bf16[128,1792]{1,0:T(8,128)(2,1)}, u32[]{:S(2)}, u32[]{:S(2)}) collective-permute-start(bf16[128,1792]{1,0:T(8,128)(2,1)S(1)} %constant_dynamic-slice_fusion.2), channel_id=1, source_target_pairs={{0,78},{2,76},{4,74},{6,72},{8,70},{10,68},{12,66},{14,64},{64,14}... | collective-permute-start | bytes 1376264 | tf_op jit(solution)/shard_map/ppermute | solution.py:88
  36.2 40.5 %collective-permute-start = (s32[128,8]{0,1:T(8,128)S(1)}, s32[128,8]{0,1:T(8,128)S(1)}, u32[]{:S(2)}, u32[]{:S(2)}) collective-permute-start(s32[128,8]{0,1:T(8,128)S(1)} %copy-done.4), channel_id=1, source_target_pairs={{0,78},{2,76},{4,74},{6,72},{8,70},{10,68},{12,66},{14,64},{64,14}... | collective-permute-start | bytes 12296 | tf_op jit(solution)/shard_map/ppermute | solution.py:88
  39.3 49.8 %collective-permute-start.2 = (bf16[1,1,896,256]{3,2,1,0:T(8,128)(2,1)S(1)}, bf16[1,1,896,256]{3,2,1,0:T(8,128)(2,1)}, u32[]{:S(2)}, u32[]{:S(2)}) collective-permute-start(bf16[1,1,896,256]{3,2,1,0:T(8,128)(2,1)S(1)} %get-tuple-element.37), channel_id=1, source_target_pairs={{0,16},{16,32},{32,48},{48,0},{1,17},{17,33},{33,49},{49,1},{2,18}... | collective-permute-start | bytes 1376264 | tf_op jit(solution)/shard_map/ppermute | solution.py:20
  42.6 46.6 %collective-permute-start.4 = (bf16[1,1,896,256]{3,2,1,0:T(8,128)(2,1)S(1)}, bf16[1,1,896,256]{3,2,1,0:T(8,128)(2,1)}, u32[]{:S(2)}, u32[]{:S(2)}) collective-permute-start(bf16[1,1,896,256]{3,2,1,0:T(8,128)(2,1)S(1)} %get-tuple-element.35), channel_id=1, source_target_pairs={{0,48},{16,0},{32,16},{48,32},{1,49},{17,1},{33,17},{49,33},{2,50}... | collective-permute-start | bytes 1376264 | tf_op jit(solution)/shard_map/ppermute | solution.py:21
  45.9 43.2 %collective-permute-start.3 = (bf16[1,512,224]{1,2,0:T(8,128)(2,1)S(1)}, bf16[1,512,224]{1,2,0:T(8,128)(2,1)S(1)}, u32[]{:S(2)}, u32[]{:S(2)}) collective-permute-start(bf16[1,512,224]{1,2,0:T(8,128)(2,1)S(1)} %get-tuple-element.41), channel_id=1, source_target_pairs={{0,16},{16,32},{32,48},{48,0},{1,17},{17,33},{33,49},{49,1},{2,18}... | collective-permute-start | bytes 688136 | tf_op jit(solution)/shard_map/ppermute | solution.py:20
  76.6 12.5 %collective-permute-start.5 = (bf16[1,512,224]{1,2,0:T(8,128)(2,1)S(1)}, bf16[1,512,224]{1,2,0:T(8,128)(2,1)}, u32[]{:S(2)}, u32[]{:S(2)}) collective-permute-start(bf16[1,512,224]{1,2,0:T(8,128)(2,1)S(1)} %get-tuple-element.39), channel_id=1, source_target_pairs={{0,48},{16,0},{32,16},{48,32},{1,49},{17,1},{33,17},{49,33},{2,50}... | collective-permute-start | bytes 688136 | tf_op jit(solution)/shard_map/ppermute | solution.py:21
  92.7 43.7 %all-to-all-start.1 = ((bf16[16,48,1792]{2,1,0:T(8,128)(2,1)}), bf16[16,48,1792]{2,1,0:T(8,128)(2,1)}, u32[]{:S(2)}, u32[]{:S(2)}) async-start(bf16[16,48,1792]{2,1,0:T(8,128)(2,1)} %bitcast.42), calls=%async_computation.1 | async-start | bytes 5505024 | tf_op jit(solution)/shard_map/all_to_all | solution.py:97
  97.2 109.0 %all-gather.3.cloned.1.call-start = ((), (), s32[]{:S(2)}) async-start(), calls=%async_computation.3 | async-start | bytes 1769472 | tf_op jit(solution)/shard_map/all_gather | solution.py:110
  136.4 3.2 %copy-start.3 = (bf16[1,1,1792,256]{3,2,1,0:T(8,128)(2,1)S(1)}, bf16[1,1,1792,256]{3,2,1,0:T(8,128)(2,1)}, u32[]{:S(2)}) copy-start(bf16[1,1,1792,256]{3,2,1,0:T(8,128)(2,1)} %param.9) | copy-start | bytes 2752516
  143.3 6.7 %collective-permute-start.6 = (f32[768,256]{1,0:T(8,128)}, f32[768,256]{1,0:T(8,128)}, u32[]{:S(2)}, u32[]{:S(2)}) collective-permute-start(f32[768,256]{1,0:T(8,128)} %constant_dynamic-slice_fusion), channel_id=1, source_target_pairs={{0,1},{1,0},{2,3},{3,2},{4,5},{5,4},{6,7},{7,6},{8,9},{9,8},{10,11... | collective-permute-start | bytes 2359304 | tf_op jit(solution)/shard_map/ppermute | solution.py:105
  147.8 4.5 %copy-start.9 = (s32[32]{0:T(128)S(1)}, s32[32]{0:T(128)}, u32[]{:S(2)}) copy-start(s32[32]{0:T(128)} %param.11) | copy-start | bytes 388
  154.3 12.2 %collective-permute-start.10 = (bf16[1,512,224]{1,2,0:T(8,128)(2,1)}, bf16[1,512,224]{1,2,0:T(8,128)(2,1)}, u32[]{:S(2)}, u32[]{:S(2)}) collective-permute-start(bf16[1,512,224]{1,2,0:T(8,128)(2,1)} %broadcast_select_fusion.2), channel_id=1, source_target_pairs={{0,48},{16,0},{32,16},{48,32},{1,49},{17,1},{33,17},{49,33},{2,50}... | collective-permute-start | bytes 688136 | tf_op jit(solution)/shard_map/ppermute | solution.py:41
  156.9 10.2 %collective-permute-start.9 = (bf16[1,512,224]{1,2,0:T(8,128)(2,1)}, bf16[1,512,224]{1,2,0:T(8,128)(2,1)}, u32[]{:S(2)}, u32[]{:S(2)}) collective-permute-start(bf16[1,512,224]{1,2,0:T(8,128)(2,1)} %broadcast_select_fusion.3), channel_id=1, source_target_pairs={{0,16},{16,32},{32,48},{48,0},{1,17},{17,33},{33,49},{49,1},{2,18}... | collective-permute-start | bytes 688136 | tf_op jit(solution)/shard_map/ppermute | solution.py:40
  160.3 13.1 %collective-permute-start.8 = (bf16[1,1,896,256]{3,2,1,0:T(8,128)(2,1)S(1)}, bf16[1,1,896,256]{3,2,1,0:T(8,128)(2,1)}, u32[]{:S(2)}, u32[]{:S(2)}) collective-permute-start(bf16[1,1,896,256]{3,2,1,0:T(8,128)(2,1)S(1)} %broadcast_select_fusion), channel_id=1, source_target_pairs={{0,48},{16,0},{32,16},{48,32},{1,49},{17,1},{33,17},{49,33},{2,50}... | collective-permute-start | bytes 1376264 | tf_op jit(solution)/shard_map/ppermute | solution.py:41
  164.3 14.6 %collective-permute-start.7 = (bf16[1,1,896,256]{3,2,1,0:T(8,128)(2,1)}, bf16[1,1,896,256]{3,2,1,0:T(8,128)(2,1)}, u32[]{:S(2)}, u32[]{:S(2)}) collective-permute-start(bf16[1,1,896,256]{3,2,1,0:T(8,128)(2,1)} %broadcast_select_fusion.1), channel_id=1, source_target_pairs={{0,16},{16,32},{32,48},{48,0},{1,17},{17,33},{33,49},{49,1},{2,18}... | collective-permute-start | bytes 1376264 | tf_op jit(solution)/shard_map/ppermute | solution.py:40
  180.3 34.2 %copy-start.5 = (f32[128,8]{0,1:T(8,128)S(1)}, f32[128,8]{0,1:T(8,128)}, u32[]{:S(2)}) copy-start(f32[128,8]{0,1:T(8,128)} %param.8) | copy-start | bytes 12292
  206.2 13.8 %collective-permute-start.11 = (bf16[8,768,128]{2,1,0:T(8,128)(2,1)}, bf16[8,768,128]{2,1,0:T(8,128)(2,1)S(1)}, u32[]{:S(2)}, u32[]{:S(2)}) collective-permute-start(bf16[8,768,128]{2,1,0:T(8,128)(2,1)} %bitcast.54), channel_id=1, source_target_pairs={{0,1},{1,0},{2,3},{3,2},{4,5},{5,4},{6,7},{7,6},{8,9},{9,8},{10,11... | collective-permute-start | bytes 4718600 | tf_op jit(solution)/shard_map/ppermute | solution.py:112
  214.5 17.9 %collective-permute-start.12 = (f32[128,8]{0,1:T(8,128)S(1)}, f32[128,8]{0,1:T(8,128)S(1)}, u32[]{:S(2)}, u32[]{:S(2)}) collective-permute-start(f32[128,8]{0,1:T(8,128)S(1)} %copy-done.5), channel_id=1, source_target_pairs={{0,78},{2,76},{4,74},{6,72},{8,70},{10,68},{12,66},{14,64},{64,14}... | collective-permute-start | bytes 12296 | tf_op jit(solution)/shard_map/ppermute | solution.py:88
  225.4 20.2 %all-to-all-start.2 = ((bf16[16,2,48,224]{3,2,1,0:T(8,128)(2,1)}), bf16[16,2,48,224]{3,2,1,0:T(8,128)(2,1)S(1)}, u32[]{:S(2)}, u32[]{:S(2)}) async-start(bf16[16,2,48,224]{3,2,1,0:T(8,128)(2,1)} %copy.52), calls=%async_computation.2 | async-start | bytes 1572864 | tf_op jit(solution)/shard_map/all_to_all | solution.py:125
  250.1 16.5 %collective-permute-start.13 = (f32[128,224]{1,0:T(8,128)S(1)}, f32[128,224]{1,0:T(8,128)S(1)}, u32[]{:S(2)}, u32[]{:S(2)}) collective-permute-start(f32[128,224]{1,0:T(8,128)S(1)} %fusion.18), channel_id=1, source_target_pairs={{0,64},{64,0},{1,65},{65,1},{2,66},{66,2},{3,67},{67,3},{4,68},{68... | collective-permute-start | bytes 344072 | tf_op jit(solution)/shard_map/ppermute | solution.py:130
  (4 other events, 6.9 us)
Sparse Core Ops, SparseCore 0:
  152.4 53.7 all-gather.2

commit v10 on v8

--- a/solution.py
+++ b/solution.py
@@ -86,12 +86,16 @@
         sent = jnp.dot(pick, rows, preferred_element_type=jnp.float32).astype(rows.dtype)
         return lax.all_to_all(sent.reshape(lines, capacity, half_width), ("y", "x"), 0, 0, tiled=True)
 
-    arrived = jnp.stack([dispatch(own_half, own_source), dispatch(far_half, far_source)], axis=0)
-    total_rows = lines * 2 * capacity
-    half_rows = total_rows // 2
-    partial_value = jnp.dot(arrived.reshape(total_rows, half_width), gate_up, preferred_element_type=jnp.float32)
-    mine = lax.dynamic_slice_in_dim(partial_value, side * half_rows, half_rows, 0)
-    other = lax.dynamic_slice_in_dim(partial_value, (1 - side) * half_rows, half_rows, 0)
+    part_rows = lines * capacity
+
+    def partial(arrived):
+        return jnp.dot(arrived.reshape(part_rows, half_width), gate_up, preferred_element_type=jnp.float32)
+
+    own_value = partial(dispatch(own_half, own_source))
+    far_value = partial(dispatch(far_half, far_source))
+    keep_own = side == 0
+    mine = jnp.where(keep_own, own_value, far_value)
+    other = jnp.where(keep_own, far_value, own_value)
     summed = mine + lax.ppermute(other, "core", FLIP)
     block_units = gate_up.shape[1] // 2
     hidden = (jax.nn.silu(summed[:, :block_units]) * summed[:, block_units:]).astype(jnp.bfloat16)

time: 264 us -> 262 us (level)
  matrix products: 9.46 us -> 14.6 us
  other arithmetic: 16.2 us -> 12 us
    dot_general x1 -> x2, matrix products: 1.62 us -> 5.35 us  [partial(): jnp.dot(arrived.reshape(part_rows, half_width), gate_up, preferred_elemen...]
    another operation x1 -> x0, other arithmetic: 3.19 us -> none  [run_layer(): jnp.stack([dispatch(own_half, own_source), dispatch(far_half, far_source)...]
    all_to_all x2, waiting for transfers between devices: 35.2 us -> 32.5 us  [dispatch(): lax.all_to_all(sent.reshape(lines, capacity, half_width), ('y', 'x'), 0,...]
  transfers between devices with their start and end apart: 18 -> 18, of which waited for: 12 -> 12; matrix products, arithmetic and copies ran while one was open for 10% -> 11% of each run, Pallas kernels for 0% -> 0%
where the time goes in v10:
time: 262 us
  waiting for transfers between devices  118 us (45%)
  starting transfers between devices  79.4 us (30%)
  local copies, waits for them, and re-layouts  21.9 us (8%)
  between operations  15.2 us (6%)
  matrix products  14.6 us (6%)
  other arithmetic  12 us (5%)
    ppermute x3, waiting for transfers between devices, run_layer(): lax.ppermute((own_half, expert_ids, route_weights), ('zhi', 'zlo'), mirror)  36.3 us
    all_to_all x2, waiting for transfers between devices, dispatch(): lax.all_to_all(sent.reshape(lines, capacity, half_width), ('y', 'x'), 0,...  32.5 us
    ppermute x3, starting transfers between devices, run_layer(): lax.ppermute((own_half, expert_ids, route_weights), ('zhi', 'zlo'), mirror)  18 us
    all_to_all x1, waiting for transfers between devices, run_layer(): returned = lax.all_to_all(by_line, ('y', 'x'), 0, 0, tiled=True)  14.3 us
    all_to_all x2, starting transfers between devices, dispatch(): lax.all_to_all(sent.reshape(lines, capacity, half_width), ('y', 'x'), 0,...  14.3 us
    ppermute x2, waiting for transfers between devices, swap_panels(): from_behind = lax.ppermute(first, 'x', ahead)  12.2 us
    scatter x2, local copies, waits for them, and re-layouts, routing(): jnp.full((expert_count * capacity,), token_rows, jnp.int32).at[place]  8.63 us
    ppermute x1, starting transfers between devices, run_layer(): partner_part = lax.ppermute(gathered, 'core', FLIP)  8.57 us
  transfers between devices with their start and end apart: 18, of which 12 were waited for; matrix products, arithmetic and copies ran while one was open for 11% of the time, Pallas kernels for 0%

profile of v10, /device:TPU:1, one launch (start us, length us, event | category | flops | bytes accessed | tf_op | source)
XLA Modules:
  0.0 261.5 jit_solution(4289178630104294274)
XLA Ops:
  10.1 4.3 %scatter_custom_fusion = s32[1536]{0:T(1024)S(1)} fusion(s32[1024]{0:T(1024)S(1)} %bitcast.55, s32[1024]{0:T(1024)S(1)} %reshape.233, s32[]{:T(128)} %constant.107.clone.1), kind=kCustom, calls=%fused_computation.104 | custom fusion | bytes 6148 | tf_op jit(solution)/shard_map/scatter | solution.py:52
  17.1 7.7 %all-to-all-start = ((bf16[16,48,1792]{2,1,0:T(8,128)(2,1)}), bf16[16,48,1792]{2,1,0:T(8,128)(2,1)}, u32[]{:S(2)}, u32[]{:S(2)}) async-start(bf16[16,48,1792]{2,1,0:T(8,128)(2,1)} %bitcast.45), calls=%async_computation | async-start | bytes 5505024 | tf_op jit(solution)/shard_map/all_to_all | solution.py:87
  24.9 11.1 %collective-permute-start = (s32[128,8]{0,1:T(8,128)S(1)}, s32[128,8]{0,1:T(8,128)S(1)}, u32[]{:S(2)}, u32[]{:S(2)}) collective-permute-start(s32[128,8]{0,1:T(8,128)S(1)} %copy-done.4), channel_id=1, source_target_pairs={{0,78},{2,76},{4,74},{6,72},{8,70},{10,68},{12,66},{14,64},{64,14}... | collective-permute-start | bytes 12296 | tf_op jit(solution)/shard_map/ppermute | solution.py:79
  38.6 4.3 %scatter_custom_fusion.1 = s32[1536]{0:T(1024)S(1)} fusion(s32[1024]{0:T(1024)S(1)} %bitcast.56, s32[1024]{0:T(1024)S(1)} %reshape.233, s32[]{:T(128)} %constant.107.clone.1), kind=kCustom, calls=%fused_computation.102 | custom fusion | bytes 6148 | tf_op jit(solution)/shard_map/scatter | solution.py:52
  43.1 36.3 %collective-permute-done.1 = bf16[128,1792]{1,0:T(8,128)(2,1)S(1)} collective-permute-done((bf16[128,1792]{1,0:T(8,128)(2,1)S(1)}, bf16[128,1792]{1,0:T(8,128)(2,1)S(1)}, u32[]{:S(2)}, u32[]{:S(2)}) %collective-permute-start.1) | collective-permute-done | bytes 458784 | tf_op jit(solution)/shard_map/ppermute | solution.py:79
  82.0 6.5 %all-to-all-start.1 = ((bf16[16,48,1792]{2,1,0:T(8,128)(2,1)}), bf16[16,48,1792]{2,1,0:T(8,128)(2,1)}, u32[]{:S(2)}, u32[]{:S(2)}) async-start(bf16[16,48,1792]{2,1,0:T(8,128)(2,1)} %bitcast.46), calls=%async_computation.1 | async-start | bytes 5505024 | tf_op jit(solution)/shard_map/all_to_all | solution.py:87
  91.2 32.5 %all-to-all-done.1 = bf16[16,48,1792]{2,1,0:T(8,128)(2,1)} async-done(((bf16[16,48,1792]{2,1,0:T(8,128)(2,1)}), bf16[16,48,1792]{2,1,0:T(8,128)(2,1)}, u32[]{:S(2)}, u32[]{:S(2)}) %all-to-all-start.1) | async-done | bytes 2752544 | tf_op jit(solution)/shard_map/all_to_all | solution.py:87
  123.7 2.7 %broadcast_select_fusion.2 = (f32[768,256]{1,0:T(8,128)S(1)}, f32[768,256]{1,0:T(8,128)S(1)}) fusion(f32[768,256]{1,0:T(8,128)S(1)} %fusion.22, pred[]{:T(512)S(6)} %eq.85, bf16[768,1792]{1,0:T(8,128)(2,1)} %bitcast.6, bf16[1,1,1792,256]{3,2,1,0:T(8,128)(2,1)S(1)} %copy-done.1), kind=kOutput, calls=%fused_computation.38 | convolution fusion | flops 704839680 | bytes 6029313 | tf_op jit(solution)/shard_map/dot_general | solution.py:92
  126.4 6.4 %collective-permute-start.2 = (f32[768,256]{1,0:T(8,128)S(1)}, f32[768,256]{1,0:T(8,128)S(1)}, u32[]{:S(2)}, u32[]{:S(2)}) collective-permute-start(f32[768,256]{1,0:T(8,128)S(1)} %get-tuple-element.37), channel_id=1, source_target_pairs={{0,1},{1,0},{2,3},{3,2},{4,5},{5,4},{6,7},{7,6},{8,9},{9,8},{10,11... | collective-permute-start | bytes 2359304 | tf_op jit(solution)/shard_map/ppermute | solution.py:99
  141.6 4.9 %collective-permute-done.7 = bf16[1,512,224]{1,2,0:T(8,128)(2,1)S(1)} collective-permute-done((bf16[1,512,224]{1,2,0:T(8,128)(2,1)}, bf16[1,512,224]{1,2,0:T(8,128)(2,1)S(1)}, u32[]{:S(2)}, u32[]{:S(2)}) %collective-permute-start.7) | collective-permute-done | bytes 229408 | tf_op jit(solution)/shard_map/ppermute | solution.py:23
  149.1 7.3 %collective-permute-done.3 = bf16[1,1,896,256]{3,2,1,0:T(8,128)(2,1)S(1)} collective-permute-done((bf16[1,1,896,256]{3,2,1,0:T(8,128)(2,1)S(1)}, bf16[1,1,896,256]{3,2,1,0:T(8,128)(2,1)S(1)}, u32[]{:S(2)}, u32[]{:S(2)}) %collective-permute-start.3) | collective-permute-done | bytes 458784 | tf_op jit(solution)/shard_map/ppermute | solution.py:23
  159.2 3.4 %collective-permute-start.8 = (bf16[1,512,224]{1,2,0:T(8,128)(2,1)}, bf16[1,512,224]{1,2,0:T(8,128)(2,1)}, u32[]{:S(2)}, u32[]{:S(2)}) collective-permute-start(bf16[1,512,224]{1,2,0:T(8,128)(2,1)} %get-tuple-element.31), channel_id=1, source_target_pairs={{0,16},{16,32},{32,48},{48,0},{1,17},{17,33},{33,49},{49,1},{2,18}... | collective-permute-start | bytes 688136 | tf_op jit(solution)/shard_map/ppermute | solution.py:32
  165.3 4.6 %collective-permute-start.10 = (bf16[1,512,224]{1,2,0:T(8,128)(2,1)}, bf16[1,512,224]{1,2,0:T(8,128)(2,1)}, u32[]{:S(2)}, u32[]{:S(2)}) collective-permute-start(bf16[1,512,224]{1,2,0:T(8,128)(2,1)} %broadcast_select_fusion.3), channel_id=1, source_target_pairs={{0,48},{16,0},{32,16},{48,32},{1,49},{17,1},{33,17},{49,33},{2,50}... | collective-permute-start | bytes 688136 | tf_op jit(solution)/shard_map/ppermute | solution.py:33
  171.0 3.4 %collective-permute-start.6 = (bf16[1,1,896,256]{3,2,1,0:T(8,128)(2,1)}, bf16[1,1,896,256]{3,2,1,0:T(8,128)(2,1)}, u32[]{:S(2)}, u32[]{:S(2)}) collective-permute-start(bf16[1,1,896,256]{3,2,1,0:T(8,128)(2,1)} %broadcast_select_fusion), channel_id=1, source_target_pairs={{0,48},{16,0},{32,16},{48,32},{1,49},{17,1},{33,17},{49,33},{2,50}... | collective-permute-start | bytes 1376264 | tf_op jit(solution)/shard_map/ppermute | solution.py:33
  178.5 5.0 %collective-permute-done.6 = bf16[1,1,896,256]{3,2,1,0:T(8,128)(2,1)} collective-permute-done((bf16[1,1,896,256]{3,2,1,0:T(8,128)(2,1)}, bf16[1,1,896,256]{3,2,1,0:T(8,128)(2,1)}, u32[]{:S(2)}, u32[]{:S(2)}) %collective-permute-start.6) | collective-permute-done | bytes 458784 | tf_op jit(solution)/shard_map/ppermute | solution.py:33
  185.9 5.1 %all-gather.3.cloned.1.call-done = bf16[6144,128]{1,0:T(8,128)(2,1)} async-done(((bf16[768,128]{1,0:T(8,128)(2,1)}), bf16[6144,128]{1,0:T(8,128)(2,1)}) %all-gather.3.cloned.1.call-update) | async-done | bytes 1572880 | tf_op jit(solution)/shard_map/all_gather | solution.py:104
  191.0 8.6 %collective-permute-start.11 = (bf16[8,768,128]{2,1,0:T(8,128)(2,1)}, bf16[8,768,128]{2,1,0:T(8,128)(2,1)}, u32[]{:S(2)}, u32[]{:S(2)}) collective-permute-start(bf16[8,768,128]{2,1,0:T(8,128)(2,1)} %bitcast.57), channel_id=1, source_target_pairs={{0,1},{1,0},{2,3},{3,2},{4,5},{5,4},{6,7},{7,6},{8,9},{9,8},{10,11... | collective-permute-start | bytes 4718600 | tf_op jit(solution)/shard_map/ppermute | solution.py:106
  199.6 4.9 %collective-permute-start.12 = (f32[128,8]{0,1:T(8,128)S(1)}, f32[128,8]{0,1:T(8,128)S(1)}, u32[]{:S(2)}, u32[]{:S(2)}) collective-permute-start(f32[128,8]{0,1:T(8,128)S(1)} %copy-done.5), channel_id=1, source_target_pairs={{0,78},{2,76},{4,74},{6,72},{8,70},{10,68},{12,66},{14,64},{64,14}... | collective-permute-start | bytes 12296 | tf_op jit(solution)/shard_map/ppermute | solution.py:79
  210.4 6.5 %all-to-all-start.2 = ((bf16[16,2,48,224]{3,2,1,0:T(8,128)(2,1)}), bf16[16,2,48,224]{3,2,1,0:T(8,128)(2,1)S(1)}, u32[]{:S(2)}, u32[]{:S(2)}) async-start(bf16[16,2,48,224]{3,2,1,0:T(8,128)(2,1)} %copy.52), calls=%async_computation.2 | async-start | bytes 1572864 | tf_op jit(solution)/shard_map/all_to_all | solution.py:119
  217.4 14.3 %all-to-all-done.2 = bf16[16,2,48,224]{3,2,1,0:T(8,128)(2,1)S(1)} async-done(((bf16[16,2,48,224]{3,2,1,0:T(8,128)(2,1)}), bf16[16,2,48,224]{3,2,1,0:T(8,128)(2,1)S(1)}, u32[]{:S(2)}, u32[]{:S(2)}) %all-to-all-start.2) | async-done | bytes 688160 | tf_op jit(solution)/shard_map/all_to_all | solution.py:119
  232.0 3.9 %gather_fusion.1 = bf16[1024,224]{1,0:T(8,128)(2,1)S(1)} fusion(bf16[769,224]{1,0:T(8,128)(2,1)S(1)} %concatenate.19, s32[1024]{0:T(1024)S(1)} %broadcast_clamp_fusion), kind=kCustom, calls=%fused_computation.1 | custom fusion | bytes 921600 | tf_op jit(solution)/shard_map/gather | solution.py:62
  236.3 4.8 %collective-permute-start.13 = (f32[128,224]{1,0:T(8,128)S(1)}, f32[128,224]{1,0:T(8,128)S(1)}, u32[]{:S(2)}, u32[]{:S(2)}) collective-permute-start(f32[128,224]{1,0:T(8,128)S(1)} %fusion.18), channel_id=1, source_target_pairs={{0,64},{64,0},{1,65},{65,1},{2,66},{66,2},{3,67},{67,3},{4,68},{68... | collective-permute-start | bytes 344072 | tf_op jit(solution)/shard_map/ppermute | solution.py:124
  241.1 3.9 %gather_fusion = bf16[1024,224]{1,0:T(8,128)(2,1)S(1)} fusion(bf16[769,224]{1,0:T(8,128)(2,1)S(1)} %concatenate.18, s32[1024]{0:T(1024)S(1)} %broadcast_clamp_fusion.1), kind=kCustom, calls=%fused_computation | custom fusion | bytes 921600 | tf_op jit(solution)/shard_map/gather | solution.py:62
  245.4 8.5 %collective-permute-done.13 = f32[128,224]{1,0:T(8,128)S(1)} collective-permute-done((f32[128,224]{1,0:T(8,128)S(1)}, f32[128,224]{1,0:T(8,128)S(1)}, u32[]{:S(2)}, u32[]{:S(2)}) %collective-permute-start.13) | collective-permute-done | bytes 114720 | tf_op jit(solution)/shard_map/ppermute | solution.py:124
  (102 shorter events, 45.2 us)
Async XLA Ops:
  7.2 7.4 %copy-start = (bf16[128,3584]{1,0:T(8,128)(2,1)S(1)}, bf16[128,3584]{1,0:T(8,128)(2,1)}, u32[]{:S(2)}) copy-start(bf16[128,3584]{1,0:T(8,128)(2,1)} %param.6) | copy-start | bytes 2752516
  17.1 7.8 %copy-start.4 = (s32[128,8]{0,1:T(8,128)S(1)}, s32[128,8]{0,1:T(8,128)}, u32[]{:S(2)}) copy-start(s32[128,8]{0,1:T(8,128)} %param.7) | copy-start | bytes 12292
  17.1 64.9 %all-to-all-start = ((bf16[16,48,1792]{2,1,0:T(8,128)(2,1)}), bf16[16,48,1792]{2,1,0:T(8,128)(2,1)}, u32[]{:S(2)}, u32[]{:S(2)}) async-start(bf16[16,48,1792]{2,1,0:T(8,128)(2,1)} %bitcast.45), calls=%async_computation | async-start | bytes 5505024 | tf_op jit(solution)/shard_map/all_to_all | solution.py:87
  24.9 13.1 %collective-permute-start = (s32[128,8]{0,1:T(8,128)S(1)}, s32[128,8]{0,1:T(8,128)S(1)}, u32[]{:S(2)}, u32[]{:S(2)}) collective-permute-start(s32[128,8]{0,1:T(8,128)S(1)} %copy-done.4), channel_id=1, source_target_pairs={{0,78},{2,76},{4,74},{6,72},{8,70},{10,68},{12,66},{14,64},{64,14}... | collective-permute-start | bytes 12296 | tf_op jit(solution)/shard_map/ppermute | solution.py:79
  36.0 43.4 %collective-permute-start.1 = (bf16[128,1792]{1,0:T(8,128)(2,1)S(1)}, bf16[128,1792]{1,0:T(8,128)(2,1)S(1)}, u32[]{:S(2)}, u32[]{:S(2)}) collective-permute-start(bf16[128,1792]{1,0:T(8,128)(2,1)S(1)} %constant_dynamic-slice_fusion.1), channel_id=1, source_target_pairs={{0,78},{2,76},{4,74},{6,72},{8,70},{10,68},{12,66},{14,64},{64,14}... | collective-permute-start | bytes 1376264 | tf_op jit(solution)/shard_map/ppermute | solution.py:79
  82.0 6.6 %copy-start.1 = (bf16[1,1,1792,256]{3,2,1,0:T(8,128)(2,1)S(1)}, bf16[1,1,1792,256]{3,2,1,0:T(8,128)(2,1)}, u32[]{:S(2)}) copy-start(bf16[1,1,1792,256]{3,2,1,0:T(8,128)(2,1)} %param.9) | copy-start | bytes 2752516
  82.0 41.7 %all-to-all-start.1 = ((bf16[16,48,1792]{2,1,0:T(8,128)(2,1)}), bf16[16,48,1792]{2,1,0:T(8,128)(2,1)}, u32[]{:S(2)}, u32[]{:S(2)}) async-start(bf16[16,48,1792]{2,1,0:T(8,128)(2,1)} %bitcast.46), calls=%async_computation.1 | async-start | bytes 5505024 | tf_op jit(solution)/shard_map/all_to_all | solution.py:87
  88.5 102.5 %all-gather.3.cloned.1.call-start = ((), (), s32[]{:S(2)}) async-start(), calls=%async_computation.3 | async-start | bytes 1769472 | tf_op jit(solution)/shard_map/all_gather | solution.py:104
  126.4 8.3 %collective-permute-start.2 = (f32[768,256]{1,0:T(8,128)S(1)}, f32[768,256]{1,0:T(8,128)S(1)}, u32[]{:S(2)}, u32[]{:S(2)}) collective-permute-start(f32[768,256]{1,0:T(8,128)S(1)} %get-tuple-element.37), channel_id=1, source_target_pairs={{0,1},{1,0},{2,3},{3,2},{4,5},{5,4},{6,7},{7,6},{8,9},{9,8},{10,11... | collective-permute-start | bytes 2359304 | tf_op jit(solution)/shard_map/ppermute | solution.py:99
  134.9 5.5 %copy-start.7 = (s32[32]{0:T(128)S(1)}, s32[32]{0:T(128)}, u32[]{:S(2)}) copy-start(s32[32]{0:T(128)} %param.11) | copy-start | bytes 388
  136.4 10.1 %collective-permute-start.7 = (bf16[1,512,224]{1,2,0:T(8,128)(2,1)}, bf16[1,512,224]{1,2,0:T(8,128)(2,1)S(1)}, u32[]{:S(2)}, u32[]{:S(2)}) collective-permute-start(bf16[1,512,224]{1,2,0:T(8,128)(2,1)} %slice.28), channel_id=1, source_target_pairs={{0,16},{16,32},{32,48},{48,0},{1,17},{17,33},{33,49},{49,1},{2,18}... | collective-permute-start | bytes 688136 | tf_op jit(solution)/shard_map/ppermute | solution.py:23
  138.4 18.1 %collective-permute-start.3 = (bf16[1,1,896,256]{3,2,1,0:T(8,128)(2,1)S(1)}, bf16[1,1,896,256]{3,2,1,0:T(8,128)(2,1)S(1)}, u32[]{:S(2)}, u32[]{:S(2)}) collective-permute-start(bf16[1,1,896,256]{3,2,1,0:T(8,128)(2,1)S(1)} %slice.26), channel_id=1, source_target_pairs={{0,16},{16,32},{32,48},{48,0},{1,17},{17,33},{33,49},{49,1},{2,18}... | collective-permute-start | bytes 1376264 | tf_op jit(solution)/shard_map/ppermute | solution.py:23
  147.2 17.3 %collective-permute-start.9 = (bf16[1,512,224]{1,2,0:T(8,128)(2,1)S(1)}, bf16[1,512,224]{1,2,0:T(8,128)(2,1)S(1)}, u32[]{:S(2)}, u32[]{:S(2)}) collective-permute-start(bf16[1,512,224]{1,2,0:T(8,128)(2,1)S(1)} %get-tuple-element.32), channel_id=1, source_target_pairs={{0,48},{16,0},{32,16},{48,32},{1,49},{17,1},{33,17},{49,33},{2,50}... | collective-permute-start | bytes 688136 | tf_op jit(solution)/shard_map/ppermute | solution.py:24
  157.3 12.9 %collective-permute-start.5 = (bf16[1,1,896,256]{3,2,1,0:T(8,128)(2,1)S(1)}, bf16[1,1,896,256]{3,2,1,0:T(8,128)(2,1)S(1)}, u32[]{:S(2)}, u32[]{:S(2)}) collective-permute-start(bf16[1,1,896,256]{3,2,1,0:T(8,128)(2,1)S(1)} %get-tuple-element.28), channel_id=1, source_target_pairs={{0,48},{16,0},{32,16},{48,32},{1,49},{17,1},{33,17},{49,33},{2,50}... | collective-permute-start | bytes 1376264 | tf_op jit(solution)/shard_map/ppermute | solution.py:24
  159.2 15.3 %collective-permute-start.8 = (bf16[1,512,224]{1,2,0:T(8,128)(2,1)}, bf16[1,512,224]{1,2,0:T(8,128)(2,1)}, u32[]{:S(2)}, u32[]{:S(2)}) collective-permute-start(bf16[1,512,224]{1,2,0:T(8,128)(2,1)} %get-tuple-element.31), channel_id=1, source_target_pairs={{0,16},{16,32},{32,48},{48,0},{1,17},{17,33},{33,49},{49,1},{2,18}... | collective-permute-start | bytes 688136 | tf_op jit(solution)/shard_map/ppermute | solution.py:32
  162.6 16.0 %collective-permute-start.4 = (bf16[1,1,896,256]{3,2,1,0:T(8,128)(2,1)}, bf16[1,1,896,256]{3,2,1,0:T(8,128)(2,1)}, u32[]{:S(2)}, u32[]{:S(2)}) collective-permute-start(bf16[1,1,896,256]{3,2,1,0:T(8,128)(2,1)} %get-tuple-element.27), channel_id=1, source_target_pairs={{0,16},{16,32},{32,48},{48,0},{1,17},{17,33},{33,49},{49,1},{2,18}... | collective-permute-start | bytes 1376264 | tf_op jit(solution)/shard_map/ppermute | solution.py:32
  164.5 5.7 %copy-start.3 = (bf16[1,512,224]{1,2,0:T(8,128)(2,1)}, bf16[1,512,224]{1,2,0:T(8,128)(2,1)S(1)}, u32[]{:S(2)}) copy-start(bf16[1,512,224]{1,2,0:T(8,128)(2,1)S(1)} %collective-permute-done.9) | copy-start | bytes 688132
  165.3 9.9 %collective-permute-start.10 = (bf16[1,512,224]{1,2,0:T(8,128)(2,1)}, bf16[1,512,224]{1,2,0:T(8,128)(2,1)}, u32[]{:S(2)}, u32[]{:S(2)}) collective-permute-start(bf16[1,512,224]{1,2,0:T(8,128)(2,1)} %broadcast_select_fusion.3), channel_id=1, source_target_pairs={{0,48},{16,0},{32,16},{48,32},{1,49},{17,1},{33,17},{49,33},{2,50}... | collective-permute-start | bytes 688136 | tf_op jit(solution)/shard_map/ppermute | solution.py:33
  171.0 12.5 %collective-permute-start.6 = (bf16[1,1,896,256]{3,2,1,0:T(8,128)(2,1)}, bf16[1,1,896,256]{3,2,1,0:T(8,128)(2,1)}, u32[]{:S(2)}, u32[]{:S(2)}) collective-permute-start(bf16[1,1,896,256]{3,2,1,0:T(8,128)(2,1)} %broadcast_select_fusion), channel_id=1, source_target_pairs={{0,48},{16,0},{32,16},{48,32},{1,49},{17,1},{33,17},{49,33},{2,50}... | collective-permute-start | bytes 1376264 | tf_op jit(solution)/shard_map/ppermute | solution.py:33
  184.9 14.6 %copy-start.5 = (f32[128,8]{0,1:T(8,128)S(1)}, f32[128,8]{0,1:T(8,128)}, u32[]{:S(2)}) copy-start(f32[128,8]{0,1:T(8,128)} %param.8) | copy-start | bytes 12292
  191.0 13.8 %collective-permute-start.11 = (bf16[8,768,128]{2,1,0:T(8,128)(2,1)}, bf16[8,768,128]{2,1,0:T(8,128)(2,1)}, u32[]{:S(2)}, u32[]{:S(2)}) collective-permute-start(bf16[8,768,128]{2,1,0:T(8,128)(2,1)} %bitcast.57), channel_id=1, source_target_pairs={{0,1},{1,0},{2,3},{3,2},{4,5},{5,4},{6,7},{7,6},{8,9},{9,8},{10,11... | collective-permute-start | bytes 4718600 | tf_op jit(solution)/shard_map/ppermute | solution.py:106
  199.6 17.7 %collective-permute-start.12 = (f32[128,8]{0,1:T(8,128)S(1)}, f32[128,8]{0,1:T(8,128)S(1)}, u32[]{:S(2)}, u32[]{:S(2)}) collective-permute-start(f32[128,8]{0,1:T(8,128)S(1)} %copy-done.5), channel_id=1, source_target_pairs={{0,78},{2,76},{4,74},{6,72},{8,70},{10,68},{12,66},{14,64},{64,14}... | collective-permute-start | bytes 12296 | tf_op jit(solution)/shard_map/ppermute | solution.py:79
  210.4 21.3 %all-to-all-start.2 = ((bf16[16,2,48,224]{3,2,1,0:T(8,128)(2,1)}), bf16[16,2,48,224]{3,2,1,0:T(8,128)(2,1)S(1)}, u32[]{:S(2)}, u32[]{:S(2)}) async-start(bf16[16,2,48,224]{3,2,1,0:T(8,128)(2,1)} %copy.52), calls=%async_computation.2 | async-start | bytes 1572864 | tf_op jit(solution)/shard_map/all_to_all | solution.py:119
  236.3 17.6 %collective-permute-start.13 = (f32[128,224]{1,0:T(8,128)S(1)}, f32[128,224]{1,0:T(8,128)S(1)}, u32[]{:S(2)}, u32[]{:S(2)}) collective-permute-start(f32[128,224]{1,0:T(8,128)S(1)} %fusion.18), channel_id=1, source_target_pairs={{0,64},{64,0},{1,65},{65,1},{2,66},{66,2},{3,67},{67,3},{4,68},{68... | collective-permute-start | bytes 344072 | tf_op jit(solution)/shard_map/ppermute | solution.py:124
  (2 other events, 3.2 us)
Sparse Core Ops, SparseCore 0:
  135.8 55.1 all-gather.2

commit v11 on v10

--- a/solution.py
+++ b/solution.py
@@ -114,8 +114,9 @@
         value = jnp.einsum("qrk,qkc->rc", hidden_part, down_blocks, preferred_element_type=jnp.float32)
         return value.astype(jnp.bfloat16)
 
-    expert_out = jnp.concatenate([project(first_hidden), project(second_hidden)], axis=0)
-    by_line = jnp.transpose(expert_out.reshape(2, lines, capacity, out_columns), (1, 0, 2, 3))
+    by_line = jnp.stack(
+        [project(part).reshape(lines, capacity, out_columns) for part in (first_hidden, second_hidden)], axis=1
+    )
     returned = lax.all_to_all(by_line, ("y", "x"), 0, 0, tiled=True)
     own_table = returned[:, 0].reshape(lines * capacity, out_columns)
     far_table = returned[:, 1].reshape(lines * capacity, out_columns)

time: 262 us -> 261 us (level)
  no operation moved by 1% of the time
where the time goes in v11:
time: 261 us; the launch traced here: 260 us
  waiting for transfers between devices  117 us (45%)
  starting transfers between devices  79.1 us (30%)
  local copies, waits for them, and re-layouts  22 us (8%)
  between operations  15.2 us (6%)
  matrix products  14.5 us (6%)
  other arithmetic  12.3 us (5%)
    ppermute x3, waiting for transfers between devices, run_layer(): lax.ppermute((own_half, expert_ids, route_weights), ('zhi', 'zlo'), mirror)  36.3 us
    all_to_all x2, waiting for transfers between devices, dispatch(): lax.all_to_all(sent.reshape(lines, capacity, half_width), ('y', 'x'), 0,...  32.5 us
    ppermute x3, starting transfers between devices, run_layer(): lax.ppermute((own_half, expert_ids, route_weights), ('zhi', 'zlo'), mirror)  18 us
    all_to_all x2, starting transfers between devices, dispatch(): lax.all_to_all(sent.reshape(lines, capacity, half_width), ('y', 'x'), 0,...  14.3 us
    all_to_all x1, waiting for transfers between devices, run_layer(): returned = lax.all_to_all(by_line, ('y', 'x'), 0, 0, tiled=True)  13.2 us
    ppermute x2, waiting for transfers between devices, swap_panels(): from_behind = lax.ppermute(first, 'x', ahead)  12.2 us
    scatter x2, local copies, waits for them, and re-layouts, routing(): jnp.full((expert_count * capacity,), token_rows, jnp.int32).at[place]  8.63 us
    ppermute x1, starting transfers between devices, run_layer(): partner_part = lax.ppermute(gathered, 'core', FLIP)  8.58 us
  transfers between devices with their start and end apart: 18, of which 12 were waited for; matrix products, arithmetic and copies ran while one was open for 11% of the time, Pallas kernels for 0%

profile of v11, /device:TPU:1, one launch (start us, length us, event | category | flops | bytes accessed | tf_op | source)
XLA Modules:
  0.0 260.1 jit_solution(8237836598045630244)
XLA Ops:
  10.1 4.3 %scatter_custom_fusion = s32[1536]{0:T(1024)S(1)} fusion(s32[1024]{0:T(1024)S(1)} %bitcast.55, s32[1024]{0:T(1024)S(1)} %reshape.229, s32[]{:T(128)} %constant.107.clone.1), kind=kCustom, calls=%fused_computation.104 | custom fusion | bytes 6148 | tf_op jit(solution)/shard_map/scatter | solution.py:52
  17.1 7.7 %all-to-all-start = ((bf16[16,48,1792]{2,1,0:T(8,128)(2,1)}), bf16[16,48,1792]{2,1,0:T(8,128)(2,1)}, u32[]{:S(2)}, u32[]{:S(2)}) async-start(bf16[16,48,1792]{2,1,0:T(8,128)(2,1)} %bitcast.44), calls=%async_computation | async-start | bytes 5505024 | tf_op jit(solution)/shard_map/all_to_all | solution.py:87
  24.9 11.1 %collective-permute-start = (s32[128,8]{0,1:T(8,128)S(1)}, s32[128,8]{0,1:T(8,128)S(1)}, u32[]{:S(2)}, u32[]{:S(2)}) collective-permute-start(s32[128,8]{0,1:T(8,128)S(1)} %copy-done.4), channel_id=1, source_target_pairs={{0,78},{2,76},{4,74},{6,72},{8,70},{10,68},{12,66},{14,64},{64,14}... | collective-permute-start | bytes 12296 | tf_op jit(solution)/shard_map/ppermute | solution.py:79
  38.6 4.3 %scatter_custom_fusion.1 = s32[1536]{0:T(1024)S(1)} fusion(s32[1024]{0:T(1024)S(1)} %bitcast.56, s32[1024]{0:T(1024)S(1)} %reshape.229, s32[]{:T(128)} %constant.107.clone.1), kind=kCustom, calls=%fused_computation.102 | custom fusion | bytes 6148 | tf_op jit(solution)/shard_map/scatter | solution.py:52
  43.1 36.3 %collective-permute-done.1 = bf16[128,1792]{1,0:T(8,128)(2,1)S(1)} collective-permute-done((bf16[128,1792]{1,0:T(8,128)(2,1)S(1)}, bf16[128,1792]{1,0:T(8,128)(2,1)S(1)}, u32[]{:S(2)}, u32[]{:S(2)}) %collective-permute-start.1) | collective-permute-done | bytes 458784 | tf_op jit(solution)/shard_map/ppermute | solution.py:79
  82.0 6.5 %all-to-all-start.1 = ((bf16[16,48,1792]{2,1,0:T(8,128)(2,1)}), bf16[16,48,1792]{2,1,0:T(8,128)(2,1)}, u32[]{:S(2)}, u32[]{:S(2)}) async-start(bf16[16,48,1792]{2,1,0:T(8,128)(2,1)} %bitcast.45), calls=%async_computation.1 | async-start | bytes 5505024 | tf_op jit(solution)/shard_map/all_to_all | solution.py:87
  91.2 32.5 %all-to-all-done.1 = bf16[16,48,1792]{2,1,0:T(8,128)(2,1)} async-done(((bf16[16,48,1792]{2,1,0:T(8,128)(2,1)}), bf16[16,48,1792]{2,1,0:T(8,128)(2,1)}, u32[]{:S(2)}, u32[]{:S(2)}) %all-to-all-start.1) | async-done | bytes 2752544 | tf_op jit(solution)/shard_map/all_to_all | solution.py:87
  123.7 2.7 %broadcast_select_fusion.2 = (f32[768,256]{1,0:T(8,128)S(1)}, f32[768,256]{1,0:T(8,128)S(1)}) fusion(f32[768,256]{1,0:T(8,128)S(1)} %fusion.22, pred[]{:T(512)S(6)} %eq.85, bf16[768,1792]{1,0:T(8,128)(2,1)} %bitcast.6, bf16[1,1,1792,256]{3,2,1,0:T(8,128)(2,1)S(1)} %copy-done.1), kind=kOutput, calls=%fused_computation.38 | convolution fusion | flops 704839680 | bytes 6029313 | tf_op jit(solution)/shard_map/dot_general | solution.py:92
  126.4 6.4 %collective-permute-start.2 = (f32[768,256]{1,0:T(8,128)S(1)}, f32[768,256]{1,0:T(8,128)S(1)}, u32[]{:S(2)}, u32[]{:S(2)}) collective-permute-start(f32[768,256]{1,0:T(8,128)S(1)} %get-tuple-element.37), channel_id=1, source_target_pairs={{0,1},{1,0},{2,3},{3,2},{4,5},{5,4},{6,7},{7,6},{8,9},{9,8},{10,11... | collective-permute-start | bytes 2359304 | tf_op jit(solution)/shard_map/ppermute | solution.py:99
  141.6 4.9 %collective-permute-done.7 = bf16[1,512,224]{1,2,0:T(8,128)(2,1)S(1)} collective-permute-done((bf16[1,512,224]{1,2,0:T(8,128)(2,1)}, bf16[1,512,224]{1,2,0:T(8,128)(2,1)S(1)}, u32[]{:S(2)}, u32[]{:S(2)}) %collective-permute-start.7) | collective-permute-done | bytes 229408 | tf_op jit(solution)/shard_map/ppermute | solution.py:23
  149.2 7.3 %collective-permute-done.3 = bf16[1,1,896,256]{3,2,1,0:T(8,128)(2,1)S(1)} collective-permute-done((bf16[1,1,896,256]{3,2,1,0:T(8,128)(2,1)S(1)}, bf16[1,1,896,256]{3,2,1,0:T(8,128)(2,1)S(1)}, u32[]{:S(2)}, u32[]{:S(2)}) %collective-permute-start.3) | collective-permute-done | bytes 458784 | tf_op jit(solution)/shard_map/ppermute | solution.py:23
  159.2 3.4 %collective-permute-start.8 = (bf16[1,512,224]{1,2,0:T(8,128)(2,1)}, bf16[1,512,224]{1,2,0:T(8,128)(2,1)}, u32[]{:S(2)}, u32[]{:S(2)}) collective-permute-start(bf16[1,512,224]{1,2,0:T(8,128)(2,1)} %get-tuple-element.31), channel_id=1, source_target_pairs={{0,16},{16,32},{32,48},{48,0},{1,17},{17,33},{33,49},{49,1},{2,18}... | collective-permute-start | bytes 688136 | tf_op jit(solution)/shard_map/ppermute | solution.py:32
  165.3 4.6 %collective-permute-start.10 = (bf16[1,512,224]{1,2,0:T(8,128)(2,1)}, bf16[1,512,224]{1,2,0:T(8,128)(2,1)}, u32[]{:S(2)}, u32[]{:S(2)}) collective-permute-start(bf16[1,512,224]{1,2,0:T(8,128)(2,1)} %broadcast_select_fusion.3), channel_id=1, source_target_pairs={{0,48},{16,0},{32,16},{48,32},{1,49},{17,1},{33,17},{49,33},{2,50}... | collective-permute-start | bytes 688136 | tf_op jit(solution)/shard_map/ppermute | solution.py:33
  171.1 3.4 %collective-permute-start.6 = (bf16[1,1,896,256]{3,2,1,0:T(8,128)(2,1)}, bf16[1,1,896,256]{3,2,1,0:T(8,128)(2,1)}, u32[]{:S(2)}, u32[]{:S(2)}) collective-permute-start(bf16[1,1,896,256]{3,2,1,0:T(8,128)(2,1)} %broadcast_select_fusion), channel_id=1, source_target_pairs={{0,48},{16,0},{32,16},{48,32},{1,49},{17,1},{33,17},{49,33},{2,50}... | collective-permute-start | bytes 1376264 | tf_op jit(solution)/shard_map/ppermute | solution.py:33
  178.5 5.0 %collective-permute-done.6 = bf16[1,1,896,256]{3,2,1,0:T(8,128)(2,1)} collective-permute-done((bf16[1,1,896,256]{3,2,1,0:T(8,128)(2,1)}, bf16[1,1,896,256]{3,2,1,0:T(8,128)(2,1)}, u32[]{:S(2)}, u32[]{:S(2)}) %collective-permute-start.6) | collective-permute-done | bytes 458784 | tf_op jit(solution)/shard_map/ppermute | solution.py:33
  186.0 5.0 %all-gather.3.cloned.1.call-done = bf16[6144,128]{1,0:T(8,128)(2,1)} async-done(((bf16[768,128]{1,0:T(8,128)(2,1)}), bf16[6144,128]{1,0:T(8,128)(2,1)}) %all-gather.3.cloned.1.call-update) | async-done | bytes 1572880 | tf_op jit(solution)/shard_map/all_gather | solution.py:104
  191.0 8.6 %collective-permute-start.11 = (bf16[8,768,128]{2,1,0:T(8,128)(2,1)}, bf16[8,768,128]{2,1,0:T(8,128)(2,1)}, u32[]{:S(2)}, u32[]{:S(2)}) collective-permute-start(bf16[8,768,128]{2,1,0:T(8,128)(2,1)} %bitcast.57), channel_id=1, source_target_pairs={{0,1},{1,0},{2,3},{3,2},{4,5},{5,4},{6,7},{7,6},{8,9},{9,8},{10,11... | collective-permute-start | bytes 4718600 | tf_op jit(solution)/shard_map/ppermute | solution.py:106
  199.6 5.0 %collective-permute-start.12 = (f32[128,8]{0,1:T(8,128)S(1)}, f32[128,8]{0,1:T(8,128)S(1)}, u32[]{:S(2)}, u32[]{:S(2)}) collective-permute-start(f32[128,8]{0,1:T(8,128)S(1)} %copy-done.5), channel_id=1, source_target_pairs={{0,78},{2,76},{4,74},{6,72},{8,70},{10,68},{12,66},{14,64},{64,14}... | collective-permute-start | bytes 12296 | tf_op jit(solution)/shard_map/ppermute | solution.py:79
  210.5 6.4 %all-to-all-start.2 = ((bf16[16,2,48,224]{3,2,1,0:T(8,128)(2,1)}), bf16[16,2,48,224]{3,2,1,0:T(8,128)(2,1)S(1)}, u32[]{:S(2)}, u32[]{:S(2)}) async-start(bf16[16,2,48,224]{3,2,1,0:T(8,128)(2,1)} %copy.55), calls=%async_computation.2 | async-start | bytes 1572864 | tf_op jit(solution)/shard_map/all_to_all | solution.py:120
  217.4 13.2 %all-to-all-done.2 = bf16[16,2,48,224]{3,2,1,0:T(8,128)(2,1)S(1)} async-done(((bf16[16,2,48,224]{3,2,1,0:T(8,128)(2,1)}), bf16[16,2,48,224]{3,2,1,0:T(8,128)(2,1)S(1)}, u32[]{:S(2)}, u32[]{:S(2)}) %all-to-all-start.2) | async-done | bytes 688160 | tf_op jit(solution)/shard_map/all_to_all | solution.py:120
  230.8 3.9 %gather_fusion.1 = bf16[1024,224]{1,0:T(8,128)(2,1)S(1)} fusion(bf16[769,224]{1,0:T(8,128)(2,1)S(1)} %concatenate.15, s32[1024]{0:T(1024)S(1)} %broadcast_clamp_fusion), kind=kCustom, calls=%fused_computation.1 | custom fusion | bytes 921600 | tf_op jit(solution)/shard_map/gather | solution.py:62
  235.1 4.5 %collective-permute-start.13 = (f32[128,224]{1,0:T(8,128)S(1)}, f32[128,224]{1,0:T(8,128)S(1)}, u32[]{:S(2)}, u32[]{:S(2)}) collective-permute-start(f32[128,224]{1,0:T(8,128)S(1)} %fusion.18), channel_id=1, source_target_pairs={{0,64},{64,0},{1,65},{65,1},{2,66},{66,2},{3,67},{67,3},{4,68},{68... | collective-permute-start | bytes 344072 | tf_op jit(solution)/shard_map/ppermute | solution.py:125
  239.7 3.9 %gather_fusion = bf16[1024,224]{1,0:T(8,128)(2,1)S(1)} fusion(bf16[769,224]{1,0:T(8,128)(2,1)S(1)} %concatenate.14, s32[1024]{0:T(1024)S(1)} %broadcast_clamp_fusion.1), kind=kCustom, calls=%fused_computation | custom fusion | bytes 921600 | tf_op jit(solution)/shard_map/gather | solution.py:62
  244.0 8.5 %collective-permute-done.13 = f32[128,224]{1,0:T(8,128)S(1)} collective-permute-done((f32[128,224]{1,0:T(8,128)S(1)}, f32[128,224]{1,0:T(8,128)S(1)}, u32[]{:S(2)}, u32[]{:S(2)}) %collective-permute-start.13) | collective-permute-done | bytes 114720 | tf_op jit(solution)/shard_map/ppermute | solution.py:125
  (101 shorter events, 45.3 us)
Async XLA Ops:
  7.2 7.4 %copy-start = (bf16[128,3584]{1,0:T(8,128)(2,1)S(1)}, bf16[128,3584]{1,0:T(8,128)(2,1)}, u32[]{:S(2)}) copy-start(bf16[128,3584]{1,0:T(8,128)(2,1)} %param.6) | copy-start | bytes 2752516
  17.1 7.8 %copy-start.4 = (s32[128,8]{0,1:T(8,128)S(1)}, s32[128,8]{0,1:T(8,128)}, u32[]{:S(2)}) copy-start(s32[128,8]{0,1:T(8,128)} %param.7) | copy-start | bytes 12292
  17.1 64.9 %all-to-all-start = ((bf16[16,48,1792]{2,1,0:T(8,128)(2,1)}), bf16[16,48,1792]{2,1,0:T(8,128)(2,1)}, u32[]{:S(2)}, u32[]{:S(2)}) async-start(bf16[16,48,1792]{2,1,0:T(8,128)(2,1)} %bitcast.44), calls=%async_computation | async-start | bytes 5505024 | tf_op jit(solution)/shard_map/all_to_all | solution.py:87
  24.9 13.1 %collective-permute-start = (s32[128,8]{0,1:T(8,128)S(1)}, s32[128,8]{0,1:T(8,128)S(1)}, u32[]{:S(2)}, u32[]{:S(2)}) collective-permute-start(s32[128,8]{0,1:T(8,128)S(1)} %copy-done.4), channel_id=1, source_target_pairs={{0,78},{2,76},{4,74},{6,72},{8,70},{10,68},{12,66},{14,64},{64,14}... | collective-permute-start | bytes 12296 | tf_op jit(solution)/shard_map/ppermute | solution.py:79
  36.0 43.4 %collective-permute-start.1 = (bf16[128,1792]{1,0:T(8,128)(2,1)S(1)}, bf16[128,1792]{1,0:T(8,128)(2,1)S(1)}, u32[]{:S(2)}, u32[]{:S(2)}) collective-permute-start(bf16[128,1792]{1,0:T(8,128)(2,1)S(1)} %constant_dynamic-slice_fusion.1), channel_id=1, source_target_pairs={{0,78},{2,76},{4,74},{6,72},{8,70},{10,68},{12,66},{14,64},{64,14}... | collective-permute-start | bytes 1376264 | tf_op jit(solution)/shard_map/ppermute | solution.py:79
  82.0 6.6 %copy-start.1 = (bf16[1,1,1792,256]{3,2,1,0:T(8,128)(2,1)S(1)}, bf16[1,1,1792,256]{3,2,1,0:T(8,128)(2,1)}, u32[]{:S(2)}) copy-start(bf16[1,1,1792,256]{3,2,1,0:T(8,128)(2,1)} %param.9) | copy-start | bytes 2752516
  82.0 41.7 %all-to-all-start.1 = ((bf16[16,48,1792]{2,1,0:T(8,128)(2,1)}), bf16[16,48,1792]{2,1,0:T(8,128)(2,1)}, u32[]{:S(2)}, u32[]{:S(2)}) async-start(bf16[16,48,1792]{2,1,0:T(8,128)(2,1)} %bitcast.45), calls=%async_computation.1 | async-start | bytes 5505024 | tf_op jit(solution)/shard_map/all_to_all | solution.py:87
  88.5 102.5 %all-gather.3.cloned.1.call-start = ((), (), s32[]{:S(2)}) async-start(), calls=%async_computation.3 | async-start | bytes 1769472 | tf_op jit(solution)/shard_map/all_gather | solution.py:104
  126.4 8.3 %collective-permute-start.2 = (f32[768,256]{1,0:T(8,128)S(1)}, f32[768,256]{1,0:T(8,128)S(1)}, u32[]{:S(2)}, u32[]{:S(2)}) collective-permute-start(f32[768,256]{1,0:T(8,128)S(1)} %get-tuple-element.37), channel_id=1, source_target_pairs={{0,1},{1,0},{2,3},{3,2},{4,5},{5,4},{6,7},{7,6},{8,9},{9,8},{10,11... | collective-permute-start | bytes 2359304 | tf_op jit(solution)/shard_map/ppermute | solution.py:99
  134.9 5.5 %copy-start.6 = (s32[32]{0:T(128)S(1)}, s32[32]{0:T(128)}, u32[]{:S(2)}) copy-start(s32[32]{0:T(128)} %param.11) | copy-start | bytes 388
  136.4 10.1 %collective-permute-start.7 = (bf16[1,512,224]{1,2,0:T(8,128)(2,1)}, bf16[1,512,224]{1,2,0:T(8,128)(2,1)S(1)}, u32[]{:S(2)}, u32[]{:S(2)}) collective-permute-start(bf16[1,512,224]{1,2,0:T(8,128)(2,1)} %slice.28), channel_id=1, source_target_pairs={{0,16},{16,32},{32,48},{48,0},{1,17},{17,33},{33,49},{49,1},{2,18}... | collective-permute-start | bytes 688136 | tf_op jit(solution)/shard_map/ppermute | solution.py:23
  138.4 18.1 %collective-permute-start.3 = (bf16[1,1,896,256]{3,2,1,0:T(8,128)(2,1)S(1)}, bf16[1,1,896,256]{3,2,1,0:T(8,128)(2,1)S(1)}, u32[]{:S(2)}, u32[]{:S(2)}) collective-permute-start(bf16[1,1,896,256]{3,2,1,0:T(8,128)(2,1)S(1)} %slice.26), channel_id=1, source_target_pairs={{0,16},{16,32},{32,48},{48,0},{1,17},{17,33},{33,49},{49,1},{2,18}... | collective-permute-start | bytes 1376264 | tf_op jit(solution)/shard_map/ppermute | solution.py:23
  147.2 17.3 %collective-permute-start.9 = (bf16[1,512,224]{1,2,0:T(8,128)(2,1)S(1)}, bf16[1,512,224]{1,2,0:T(8,128)(2,1)S(1)}, u32[]{:S(2)}, u32[]{:S(2)}) collective-permute-start(bf16[1,512,224]{1,2,0:T(8,128)(2,1)S(1)} %get-tuple-element.32), channel_id=1, source_target_pairs={{0,48},{16,0},{32,16},{48,32},{1,49},{17,1},{33,17},{49,33},{2,50}... | collective-permute-start | bytes 688136 | tf_op jit(solution)/shard_map/ppermute | solution.py:24
  157.3 12.9 %collective-permute-start.5 = (bf16[1,1,896,256]{3,2,1,0:T(8,128)(2,1)S(1)}, bf16[1,1,896,256]{3,2,1,0:T(8,128)(2,1)S(1)}, u32[]{:S(2)}, u32[]{:S(2)}) collective-permute-start(bf16[1,1,896,256]{3,2,1,0:T(8,128)(2,1)S(1)} %get-tuple-element.28), channel_id=1, source_target_pairs={{0,48},{16,0},{32,16},{48,32},{1,49},{17,1},{33,17},{49,33},{2,50}... | collective-permute-start | bytes 1376264 | tf_op jit(solution)/shard_map/ppermute | solution.py:24
  159.2 15.3 %collective-permute-start.8 = (bf16[1,512,224]{1,2,0:T(8,128)(2,1)}, bf16[1,512,224]{1,2,0:T(8,128)(2,1)}, u32[]{:S(2)}, u32[]{:S(2)}) collective-permute-start(bf16[1,512,224]{1,2,0:T(8,128)(2,1)} %get-tuple-element.31), channel_id=1, source_target_pairs={{0,16},{16,32},{32,48},{48,0},{1,17},{17,33},{33,49},{49,1},{2,18}... | collective-permute-start | bytes 688136 | tf_op jit(solution)/shard_map/ppermute | solution.py:32
  162.6 16.0 %collective-permute-start.4 = (bf16[1,1,896,256]{3,2,1,0:T(8,128)(2,1)}, bf16[1,1,896,256]{3,2,1,0:T(8,128)(2,1)}, u32[]{:S(2)}, u32[]{:S(2)}) collective-permute-start(bf16[1,1,896,256]{3,2,1,0:T(8,128)(2,1)} %get-tuple-element.27), channel_id=1, source_target_pairs={{0,16},{16,32},{32,48},{48,0},{1,17},{17,33},{33,49},{49,1},{2,18}... | collective-permute-start | bytes 1376264 | tf_op jit(solution)/shard_map/ppermute | solution.py:32
  164.5 5.7 %copy-start.3 = (bf16[1,512,224]{1,2,0:T(8,128)(2,1)}, bf16[1,512,224]{1,2,0:T(8,128)(2,1)S(1)}, u32[]{:S(2)}) copy-start(bf16[1,512,224]{1,2,0:T(8,128)(2,1)S(1)} %collective-permute-done.9) | copy-start | bytes 688132
  165.3 9.9 %collective-permute-start.10 = (bf16[1,512,224]{1,2,0:T(8,128)(2,1)}, bf16[1,512,224]{1,2,0:T(8,128)(2,1)}, u32[]{:S(2)}, u32[]{:S(2)}) collective-permute-start(bf16[1,512,224]{1,2,0:T(8,128)(2,1)} %broadcast_select_fusion.3), channel_id=1, source_target_pairs={{0,48},{16,0},{32,16},{48,32},{1,49},{17,1},{33,17},{49,33},{2,50}... | collective-permute-start | bytes 688136 | tf_op jit(solution)/shard_map/ppermute | solution.py:33
  171.1 12.5 %collective-permute-start.6 = (bf16[1,1,896,256]{3,2,1,0:T(8,128)(2,1)}, bf16[1,1,896,256]{3,2,1,0:T(8,128)(2,1)}, u32[]{:S(2)}, u32[]{:S(2)}) collective-permute-start(bf16[1,1,896,256]{3,2,1,0:T(8,128)(2,1)} %broadcast_select_fusion), channel_id=1, source_target_pairs={{0,48},{16,0},{32,16},{48,32},{1,49},{17,1},{33,17},{49,33},{2,50}... | collective-permute-start | bytes 1376264 | tf_op jit(solution)/shard_map/ppermute | solution.py:33
  185.0 14.6 %copy-start.5 = (f32[128,8]{0,1:T(8,128)S(1)}, f32[128,8]{0,1:T(8,128)}, u32[]{:S(2)}) copy-start(f32[128,8]{0,1:T(8,128)} %param.8) | copy-start | bytes 12292
  191.0 13.9 %collective-permute-start.11 = (bf16[8,768,128]{2,1,0:T(8,128)(2,1)}, bf16[8,768,128]{2,1,0:T(8,128)(2,1)}, u32[]{:S(2)}, u32[]{:S(2)}) collective-permute-start(bf16[8,768,128]{2,1,0:T(8,128)(2,1)} %bitcast.57), channel_id=1, source_target_pairs={{0,1},{1,0},{2,3},{3,2},{4,5},{5,4},{6,7},{7,6},{8,9},{9,8},{10,11... | collective-permute-start | bytes 4718600 | tf_op jit(solution)/shard_map/ppermute | solution.py:106
  199.6 17.7 %collective-permute-start.12 = (f32[128,8]{0,1:T(8,128)S(1)}, f32[128,8]{0,1:T(8,128)S(1)}, u32[]{:S(2)}, u32[]{:S(2)}) collective-permute-start(f32[128,8]{0,1:T(8,128)S(1)} %copy-done.5), channel_id=1, source_target_pairs={{0,78},{2,76},{4,74},{6,72},{8,70},{10,68},{12,66},{14,64},{64,14}... | collective-permute-start | bytes 12296 | tf_op jit(solution)/shard_map/ppermute | solution.py:79
  210.5 20.1 %all-to-all-start.2 = ((bf16[16,2,48,224]{3,2,1,0:T(8,128)(2,1)}), bf16[16,2,48,224]{3,2,1,0:T(8,128)(2,1)S(1)}, u32[]{:S(2)}, u32[]{:S(2)}) async-start(bf16[16,2,48,224]{3,2,1,0:T(8,128)(2,1)} %copy.55), calls=%async_computation.2 | async-start | bytes 1572864 | tf_op jit(solution)/shard_map/all_to_all | solution.py:120
  235.1 17.4 %collective-permute-start.13 = (f32[128,224]{1,0:T(8,128)S(1)}, f32[128,224]{1,0:T(8,128)S(1)}, u32[]{:S(2)}, u32[]{:S(2)}) collective-permute-start(f32[128,224]{1,0:T(8,128)S(1)} %fusion.18), channel_id=1, source_target_pairs={{0,64},{64,0},{1,65},{65,1},{2,66},{66,2},{3,67},{67,3},{4,68},{68... | collective-permute-start | bytes 344072 | tf_op jit(solution)/shard_map/ppermute | solution.py:125
  (1 other events, 1.0 us)
Sparse Core Ops, SparseCore 0:
  135.8 55.1 all-gather.2
